TPU v7x, 768 devices: a whole 4x8x12 slice. The times are simulated.
768 devices in a mesh: slab: 8 (over y), kmom: 16 (over z_lo, x), energy: 6 (over z_hi, core).
Axes of the slice: x: 4, y: 8, z: 12 (z_hi: 3, z_lo: 4; z = z_hi * 4 + z_lo), core: 2. Of those that a mesh axis runs over, the one named last changes fastest.
Arguments:
- free_green: float32 [8, 6, 16, 2, 256, 256], P('slab', 'energy', 'kmom'), as said below
- coupling: float32 [8, 256, 256], P('slab'), may hold values from -0.375 to 0.375
- coupling_tiles: int32 [8, 8, 3], P('slab'), may hold values from 0 to 7, as said below
- occupation: float32 [6], P('energy'), may hold values from 0.05 to 1
- phonon_weight: float32 [2, 16, 16], replicated, may hold values from 0.2 to 1
- phonon_mode: int32 [2], replicated, may hold values from 0 to 1, each once
Outputs:
- green: float32 [8, 6, 16, 2, 256, 256], P('slab', 'energy', 'kmom')
- self_energy: bfloat16 [8, 6, 16, 2, 256, 256], P('slab', 'energy', 'kmom')
Inputs may be any that keep to these rules, and one draw needn't show every extreme that they name: `coupling_tiles`: the 3 column tiles of one row tile are distinct. `phonon_mode`: each value once. `free_green`: the imaginary part of every diagonal entry is negative.
All inputs are finite; a program needn't handle non-finite values.
Results may differ from a plain program's by a relative error of at most 0.0034.
Values may be sent and summed in bfloat16 or wider, within the bound.
No kernel may reach another device: no remote copies, remote signals or barrier semaphores. Data moves between devices by JAX's collectives and lax.ppermute only.
A program may use at most 32 MiB of HBM per device.

v0:
```python
import jax
import jax.numpy as jnp
from jax import lax
from jax.sharding import PartitionSpec as P


def passed_along(shard, axis, by):
    length = lax.axis_size(axis)
    pairs = [(i, i + by) for i in range(length) if 0 <= i + by < length]
    return lax.ppermute(shard, axis, pairs)


def extended_2(block, sides, width):
    for axis, dim in sides:
        count = lax.axis_size(axis)
        forward = [(i, i + 1) for i in range(count - 1)]
        backward = [(target, source) for source, target in forward]
        low = lax.ppermute(
            lax.slice_in_dim(block, block.shape[dim] - width, None, axis=dim), axis, forward
        )
        high = lax.ppermute(lax.slice_in_dim(block, 0, width, axis=dim), axis, backward)
        block = jnp.concatenate([low, block, high], axis=dim)
    return block


def complex_product(left_factor, right_factor):
    left_real = left_factor[..., 0, :, :]
    left_imag = left_factor[..., 1, :, :]
    right_real = right_factor[..., 0, :, :]
    right_imag = right_factor[..., 1, :, :]
    highest = lax.Precision.HIGHEST
    real_part = jnp.matmul(left_real, right_real, precision=highest) - jnp.matmul(
        left_imag, right_imag, precision=highest
    )
    imag_part = jnp.matmul(left_real, right_imag, precision=highest) + jnp.matmul(
        left_imag, right_real, precision=highest
    )
    return jnp.stack([real_part, imag_part], axis=-3)


def sandwich(pair_map, inner):
    return complex_product(complex_product(pair_map, inner), jnp.swapaxes(pair_map, -1, -2))


def on_device(free_green, coupling, coupling_tiles, occupation, phonon_weight, phonon_mode):
    slab_count = free_green.shape[0]
    block_width = coupling.shape[-1]
    tile_count = coupling_tiles.shape[1]
    tile_size = block_width // tile_count
    column_tile = jnp.arange(block_width, dtype=jnp.int32) // tile_size
    tile_hit = jnp.any(coupling_tiles[..., None] == column_tile, axis=-2).astype(jnp.float32)
    tile_mask = jnp.broadcast_to(
        tile_hit[:, :, None, :], (slab_count, tile_count, tile_size, block_width)
    ).reshape(slab_count, block_width, block_width)
    coupled = coupling * tile_mask
    pair_maps = [
        jnp.einsum("ekcij,jl->ekcil", free_green[0], coupled[0], precision=lax.Precision.HIGHEST)
    ]

    def sweep(beyond):
        current = beyond
        current = free_green[0] + sandwich(pair_maps[0], current)
        results = [current]
        return results[::-1]

    zero_block = jnp.zeros(free_green.shape[1:], jnp.float32)

    def advance(turn_index, beyond):
        first_green = sweep(beyond)[0]
        return passed_along(first_green, "slab", -1)

    beyond = lax.fori_loop(0, lax.axis_size("slab") - 1, advance, zero_block)
    green = jnp.stack(sweep(beyond))
    filling = occupation[None, :, None, None, None]
    real_part = -filling * (green[:, :, :, 0] - jnp.swapaxes(green[:, :, :, 0], -1, -2))
    imag_part = -filling * (green[:, :, :, 1] + jnp.swapaxes(green[:, :, :, 1], -1, -2))
    lesser = jnp.stack([real_part, imag_part], axis=3).astype(jnp.bfloat16)
    e_local = occupation.shape[0]
    k_local = green.shape[2]
    k_first = lax.axis_index("kmom") * k_local
    weights_mine = lax.dynamic_slice_in_dim(phonon_weight, k_first, k_local, 1)
    branch_count = phonon_weight.shape[0]
    gathered = lax.all_gather(lesser, "kmom", axis=2, tiled=True)
    mixed = jnp.einsum(
        "bkq,seqcij->bsekcij",
        weights_mine,
        gathered.astype(jnp.float32),
        precision=lax.Precision.HIGHEST,
    )
    extended = extended_2(mixed, (("energy", 2),), 1)
    self_energy = jnp.zeros(green.shape, jnp.float32)
    for branch in range(branch_count):
        self_energy = (
            self_energy
            + lax.dynamic_slice_in_dim(extended[branch], 1 + phonon_mode[branch], e_local, 1)
            + lax.dynamic_slice_in_dim(extended[branch], 1 - phonon_mode[branch], e_local, 1)
        )
    return (green, self_energy.astype(jnp.bfloat16))


def solution(mesh):
    in_specs = (
        P("slab", "energy", "kmom", None, None, None),
        P("slab", None, None),
        P("slab", None, None),
        P("energy"),
        P(),
        P(),
    )
    out_specs = (
        P("slab", "energy", "kmom", None, None, None),
        P("slab", "energy", "kmom", None, None, None),
    )
    return jax.shard_map(
        on_device, mesh=mesh, in_specs=in_specs, out_specs=out_specs, check_vma=False
    )
```

profile of v0, /device:TPU:1, one launch (start us, length us, event | category | flops | bytes accessed | tf_op | source)
XLA Modules:
  0.0 316.1 jit_solution(3802214802709687340)
XLA Ops:
  9.1 2.1 fusion.30
  11.4 114.9 %while.10 = (s32[]{:T(128)}, f32[1,1,2,256,256]{4,3,2,1,0:T(8,128)S(1)}, f32[1,1,1,2,256,256]{5,4,3,2,1,0:T(8,128)S(1)}, f32[1,1,2,256,256]{4,3,2,1,0:T(8,128)S(1)}, s32[]{:T(128)}) while((s32[]{:T(128)}, f32[1,1,2,256,256]{4,3,2,1,0:T(8,128)S(1)}, f32[1,1,1,2,256,256]{5,4,3,2,1,0:T(8,128)S(1)}, f32[1,1,2,256,256]{4,3,2,1,0:T(8,128)S(1)}, ...), condition=%wide.region_2.3_spmd, body=%wide.region_1.2_spmd.sunk | while | flops 1611137024 | bytes 11010149 | solution.py:72
  14.7 1.3 collective-permute-start
  16.1 9.3 %collective-permute-done = f32[1,1,2,256,256]{4,3,2,1,0:T(8,128)S(1)} collective-permute-done((f32[1,1,2,256,256]{4,3,2,1,0:T(8,128)S(1)}, f32[1,1,2,256,256]{4,3,2,1,0:T(8,128)S(1)}, u32[]{:S(2)}, u32[]{:S(2)}) %collective-permute-start) | collective-permute-done | bytes 524320 | tf_op jit(solution)/shard_map/while/body/eval_jaxpr/ppermute | solution.py:10
  28.6 1.3 collective-permute-start
  29.9 13.4 %collective-permute-done = f32[1,1,2,256,256]{4,3,2,1,0:T(8,128)S(1)} collective-permute-done((f32[1,1,2,256,256]{4,3,2,1,0:T(8,128)S(1)}, f32[1,1,2,256,256]{4,3,2,1,0:T(8,128)S(1)}, u32[]{:S(2)}, u32[]{:S(2)}) %collective-permute-start) | collective-permute-done | bytes 524320 | tf_op jit(solution)/shard_map/while/body/eval_jaxpr/ppermute | solution.py:10
  46.6 1.3 collective-permute-start
  47.9 10.1 %collective-permute-done = f32[1,1,2,256,256]{4,3,2,1,0:T(8,128)S(1)} collective-permute-done((f32[1,1,2,256,256]{4,3,2,1,0:T(8,128)S(1)}, f32[1,1,2,256,256]{4,3,2,1,0:T(8,128)S(1)}, u32[]{:S(2)}, u32[]{:S(2)}) %collective-permute-start) | collective-permute-done | bytes 524320 | tf_op jit(solution)/shard_map/while/body/eval_jaxpr/ppermute | solution.py:10
  61.3 1.3 collective-permute-start
  62.6 18.9 %collective-permute-done = f32[1,1,2,256,256]{4,3,2,1,0:T(8,128)S(1)} collective-permute-done((f32[1,1,2,256,256]{4,3,2,1,0:T(8,128)S(1)}, f32[1,1,2,256,256]{4,3,2,1,0:T(8,128)S(1)}, u32[]{:S(2)}, u32[]{:S(2)}) %collective-permute-start) | collective-permute-done | bytes 524320 | tf_op jit(solution)/shard_map/while/body/eval_jaxpr/ppermute | solution.py:10
  84.8 1.3 collective-permute-start
  86.1 11.2 %collective-permute-done = f32[1,1,2,256,256]{4,3,2,1,0:T(8,128)S(1)} collective-permute-done((f32[1,1,2,256,256]{4,3,2,1,0:T(8,128)S(1)}, f32[1,1,2,256,256]{4,3,2,1,0:T(8,128)S(1)}, u32[]{:S(2)}, u32[]{:S(2)}) %collective-permute-start) | collective-permute-done | bytes 524320 | tf_op jit(solution)/shard_map/while/body/eval_jaxpr/ppermute | solution.py:10
  100.6 1.3 collective-permute-start
  101.9 10.3 %collective-permute-done = f32[1,1,2,256,256]{4,3,2,1,0:T(8,128)S(1)} collective-permute-done((f32[1,1,2,256,256]{4,3,2,1,0:T(8,128)S(1)}, f32[1,1,2,256,256]{4,3,2,1,0:T(8,128)S(1)}, u32[]{:S(2)}, u32[]{:S(2)}) %collective-permute-start) | collective-permute-done | bytes 524320 | tf_op jit(solution)/shard_map/while/body/eval_jaxpr/ppermute | solution.py:10
  115.5 1.3 collective-permute-start
  116.9 9.5 %collective-permute-done = f32[1,1,2,256,256]{4,3,2,1,0:T(8,128)S(1)} collective-permute-done((f32[1,1,2,256,256]{4,3,2,1,0:T(8,128)S(1)}, f32[1,1,2,256,256]{4,3,2,1,0:T(8,128)S(1)}, u32[]{:S(2)}, u32[]{:S(2)}) %collective-permute-start) | collective-permute-done | bytes 524320 | tf_op jit(solution)/shard_map/while/body/eval_jaxpr/ppermute | solution.py:10
  132.4 97.7 %all-gather.2.cloned.1.call-done = bf16[1,1,16,2,256,256]{5,4,3,1,0,2:T(8,128)(2,1)} async-done(((bf16[1,1,1,2,256,256]{5,4,3,1,0,2:T(8,128)(2,1)}), bf16[1,1,16,2,256,256]{5,4,3,1,0,2:T(8,128)(2,1)}) %all-gather.2.cloned.1.call-update) | async-done | bytes 4194320 | tf_op jit(solution)/shard_map/all_gather | solution.py:83
  230.1 5.8 %fusion.25 = f32[2,1,1,1,2,256,256]{6,0,5,4,3,2,1:T(2,128)S(1)} fusion(f32[2,16,1,1]{1,0,3,2:T(2,128)S(1)} %bitcast.204, bf16[1,1,16,2,256,256]{5,4,3,1,0,2:T(8,128)(2,1)} %all-gather.2.cloned.1.call-done), kind=kOutput, calls=%fused_computation.33 | convolution fusion | flops 50331648 | bytes 5243008 | tf_op jit(solution)/shard_map/bkq,seqcij->bsekcij/dot_general | solution.py:84
  235.8 16.7 %collective-permute-start.1 = (f32[2,1,1,1,2,256,256]{6,0,5,4,3,2,1:T(2,128)S(1)}, f32[2,1,1,1,2,256,256]{6,0,5,4,3,2,1:T(2,128)S(1)}, u32[]{:S(2)}, u32[]{:S(2)}) collective-permute-start(f32[2,1,1,1,2,256,256]{6,0,5,4,3,2,1:T(2,128)S(1)} %fusion.25), channel_id=1, source_target_pairs={{0,1},{1,2},{2,3},{3,4},{4,5},{6,7},{7,8},{8,9},{9,10},{10,11},{12... | collective-permute-start | bytes 3145736 | tf_op jit(solution)/shard_map/ppermute | solution.py:18
  252.5 1.9 collective-permute-start.2
  259.9 4.4 %collective-permute-done.1 = f32[2,1,1,1,2,256,256]{6,0,5,4,3,2,1:T(2,128)S(1)} collective-permute-done((f32[2,1,1,1,2,256,256]{6,0,5,4,3,2,1:T(2,128)S(1)}, f32[2,1,1,1,2,256,256]{6,0,5,4,3,2,1:T(2,128)S(1)}, u32[]{:S(2)}, u32[]{:S(2)}) %collective-permute-start.1) | collective-permute-done | bytes 1048608 | tf_op jit(solution)/shard_map/ppermute | solution.py:18
  264.3 37.5 %collective-permute-done.2 = f32[2,1,1,1,2,256,256]{6,0,5,4,3,2,1:T(2,128)} collective-permute-done((f32[2,1,1,1,2,256,256]{6,0,5,4,3,2,1:T(2,128)S(1)}, f32[2,1,1,1,2,256,256]{6,0,5,4,3,2,1:T(2,128)}, u32[]{:S(2)}, u32[]{:S(2)}) %collective-permute-start.2) | collective-permute-done | bytes 1048608 | tf_op jit(solution)/shard_map/ppermute | solution.py:21
  301.9 3.0 pad_maximum_fusion
  304.9 2.7 fusion.51
  (100 shorter events, 32.2 us)
Async XLA Ops:
  7.2 125.2 %copy-start = (f32[2,16,16]{2,1,0:T(8,128)S(1)}, f32[2,16,16]{2,1,0:T(8,128)}, u32[]{:S(2)}) copy-start(f32[2,16,16]{2,1,0:T(8,128)} %param.12) | copy-start | bytes 6148
  7.2 4.2 %copy-start.1 = (f32[1,1,1,2,256,256]{5,4,3,2,1,0:T(8,128)S(1)}, f32[1,1,1,2,256,256]{5,4,3,2,1,0:T(8,128)}, u32[]{:S(2)}) copy-start(f32[1,1,1,2,256,256]{5,4,3,2,1,0:T(8,128)} %param.8) | copy-start | bytes 1572868
  7.2 222.9 %all-gather.2.cloned.1.call-start = ((), (), s32[]{:S(2)}) async-start(), calls=%async_computation | async-start | bytes 4456448 | tf_op jit(solution)/shard_map/all_gather | solution.py:83
  14.7 10.6 %collective-permute-start = (f32[1,1,2,256,256]{4,3,2,1,0:T(8,128)S(1)}, f32[1,1,2,256,256]{4,3,2,1,0:T(8,128)S(1)}, u32[]{:S(2)}, u32[]{:S(2)}) collective-permute-start(f32[1,1,2,256,256]{4,3,2,1,0:T(8,128)S(1)} %maximum_add_fusion.3), channel_id=1, source_target_pairs={{96,0},{192,96},{288,192},{384,288},{480,384},{576,480},{672,576},... | collective-permute-start | bytes 1572872 | tf_op jit(solution)/shard_map/while/body/eval_jaxpr/ppermute | solution.py:10
  28.6 14.7 %collective-permute-start = (f32[1,1,2,256,256]{4,3,2,1,0:T(8,128)S(1)}, f32[1,1,2,256,256]{4,3,2,1,0:T(8,128)S(1)}, u32[]{:S(2)}, u32[]{:S(2)}) collective-permute-start(f32[1,1,2,256,256]{4,3,2,1,0:T(8,128)S(1)} %maximum_add_fusion.3), channel_id=1, source_target_pairs={{96,0},{192,96},{288,192},{384,288},{480,384},{576,480},{672,576},... | collective-permute-start | bytes 1572872 | tf_op jit(solution)/shard_map/while/body/eval_jaxpr/ppermute | solution.py:10
  46.6 11.4 %collective-permute-start = (f32[1,1,2,256,256]{4,3,2,1,0:T(8,128)S(1)}, f32[1,1,2,256,256]{4,3,2,1,0:T(8,128)S(1)}, u32[]{:S(2)}, u32[]{:S(2)}) collective-permute-start(f32[1,1,2,256,256]{4,3,2,1,0:T(8,128)S(1)} %maximum_add_fusion.3), channel_id=1, source_target_pairs={{96,0},{192,96},{288,192},{384,288},{480,384},{576,480},{672,576},... | collective-permute-start | bytes 1572872 | tf_op jit(solution)/shard_map/while/body/eval_jaxpr/ppermute | solution.py:10
  61.3 20.2 %collective-permute-start = (f32[1,1,2,256,256]{4,3,2,1,0:T(8,128)S(1)}, f32[1,1,2,256,256]{4,3,2,1,0:T(8,128)S(1)}, u32[]{:S(2)}, u32[]{:S(2)}) collective-permute-start(f32[1,1,2,256,256]{4,3,2,1,0:T(8,128)S(1)} %maximum_add_fusion.3), channel_id=1, source_target_pairs={{96,0},{192,96},{288,192},{384,288},{480,384},{576,480},{672,576},... | collective-permute-start | bytes 1572872 | tf_op jit(solution)/shard_map/while/body/eval_jaxpr/ppermute | solution.py:10
  84.8 12.5 %collective-permute-start = (f32[1,1,2,256,256]{4,3,2,1,0:T(8,128)S(1)}, f32[1,1,2,256,256]{4,3,2,1,0:T(8,128)S(1)}, u32[]{:S(2)}, u32[]{:S(2)}) collective-permute-start(f32[1,1,2,256,256]{4,3,2,1,0:T(8,128)S(1)} %maximum_add_fusion.3), channel_id=1, source_target_pairs={{96,0},{192,96},{288,192},{384,288},{480,384},{576,480},{672,576},... | collective-permute-start | bytes 1572872 | tf_op jit(solution)/shard_map/while/body/eval_jaxpr/ppermute | solution.py:10
  100.6 11.6 %collective-permute-start = (f32[1,1,2,256,256]{4,3,2,1,0:T(8,128)S(1)}, f32[1,1,2,256,256]{4,3,2,1,0:T(8,128)S(1)}, u32[]{:S(2)}, u32[]{:S(2)}) collective-permute-start(f32[1,1,2,256,256]{4,3,2,1,0:T(8,128)S(1)} %maximum_add_fusion.3), channel_id=1, source_target_pairs={{96,0},{192,96},{288,192},{384,288},{480,384},{576,480},{672,576},... | collective-permute-start | bytes 1572872 | tf_op jit(solution)/shard_map/while/body/eval_jaxpr/ppermute | solution.py:10
  115.5 10.8 %collective-permute-start = (f32[1,1,2,256,256]{4,3,2,1,0:T(8,128)S(1)}, f32[1,1,2,256,256]{4,3,2,1,0:T(8,128)S(1)}, u32[]{:S(2)}, u32[]{:S(2)}) collective-permute-start(f32[1,1,2,256,256]{4,3,2,1,0:T(8,128)S(1)} %maximum_add_fusion.3), channel_id=1, source_target_pairs={{96,0},{192,96},{288,192},{384,288},{480,384},{576,480},{672,576},... | collective-permute-start | bytes 1572872 | tf_op jit(solution)/shard_map/while/body/eval_jaxpr/ppermute | solution.py:10
  130.4 105.4 %copy-start.2 = (f32[1,1,1,2,256,256]{5,4,3,2,1,0:T(8,128)}, f32[1,1,1,2,256,256]{5,4,3,2,1,0:T(8,128)S(1)}, u32[]{:S(2)}) copy-start(f32[1,1,1,2,256,256]{5,4,3,2,1,0:T(8,128)S(1)} %maximum_add_fusion.1) | copy-start | bytes 1572868
  131.6 122.8 %copy-start.3 = (s32[2]{0:T(128)S(1)}, s32[2]{0:T(128)}, u32[]{:S(2)}) copy-start(s32[2]{0:T(128)} %param.13) | copy-start | bytes 28
  235.8 28.5 %collective-permute-start.1 = (f32[2,1,1,1,2,256,256]{6,0,5,4,3,2,1:T(2,128)S(1)}, f32[2,1,1,1,2,256,256]{6,0,5,4,3,2,1:T(2,128)S(1)}, u32[]{:S(2)}, u32[]{:S(2)}) collective-permute-start(f32[2,1,1,1,2,256,256]{6,0,5,4,3,2,1:T(2,128)S(1)} %fusion.25), channel_id=1, source_target_pairs={{0,1},{1,2},{2,3},{3,4},{4,5},{6,7},{7,8},{8,9},{9,10},{10,11},{12... | collective-permute-start | bytes 3145736 | tf_op jit(solution)/shard_map/ppermute | solution.py:18
  252.5 49.4 %collective-permute-start.2 = (f32[2,1,1,1,2,256,256]{6,0,5,4,3,2,1:T(2,128)S(1)}, f32[2,1,1,1,2,256,256]{6,0,5,4,3,2,1:T(2,128)}, u32[]{:S(2)}, u32[]{:S(2)}) collective-permute-start(f32[2,1,1,1,2,256,256]{6,0,5,4,3,2,1:T(2,128)S(1)} %fusion.25), channel_id=1, source_target_pairs={{1,0},{2,1},{3,2},{4,3},{5,4},{7,6},{8,7},{9,8},{10,9},{11,10},{13... | collective-permute-start | bytes 3145736 | tf_op jit(solution)/shard_map/ppermute | solution.py:21
Sparse Core Ops, SparseCore 0:
  132.5 97.5 all-gather.1
where the time goes:
time: 317 us; the launch traced here: 316 us
  waiting for transfers between devices  222 us (70%)
  matrix products  33.9 us (11%)
  starting transfers between devices  27.7 us (9%)
  between operations  19.8 us (6%)
  other arithmetic  6.33 us (2%)
  local copies, waits for them, and re-layouts  5.45 us (2%)
    all_gather x1, waiting for transfers between devices, on_device(): gathered = lax.all_gather(lesser, 'kmom', axis=2, tiled=True)  97.7 us
    ppermute x7, waiting for transfers between devices, passed_along(): return lax.ppermute(shard, axis, pairs)  82.7 us
    ppermute x1, waiting for transfers between devices, extended_2(): lax.ppermute(lax.slice_in_dim(block, 0, width, axis=dim), axis, backward)  37.5 us
    ppermute x1, starting transfers between devices, extended_2(): lax.ppermute(lax.slice_in_dim(block, block.shape[dim] - width, None, axis...  16.7 us
    ppermute x7, starting transfers between devices, passed_along(): return lax.ppermute(shard, axis, pairs)  9.04 us
    dot_general x16, matrix products, complex_product(): jnp.matmul(left_imag, right_real, precision=highest)  6.52 us
    dot_general x16, matrix products, complex_product(): jnp.matmul(left_imag, right_imag, precision=highest)  6.52 us
    dot_general x16, matrix products, complex_product(): jnp.matmul(left_real, right_imag, precision=highest)  6.5 us
  transfers between devices with their start and end apart: 10, of which 10 were waited for; matrix products, arithmetic and copies ran while one was open for 0% of the time, Pallas kernels for 0%

commit v1 on v0

v1 whole, which is shorter than its diff:
```python
import jax
import jax.numpy as jnp
from jax import lax
from jax.sharding import PartitionSpec as P


def passed_along(shard, axis, by):
    length = lax.axis_size(axis)
    pairs = [(i, i + by) for i in range(length) if 0 <= i + by < length]
    return lax.ppermute(shard, axis, pairs)


def complex_product(left_factor, right_factor):
    left_real = left_factor[..., 0, :, :]
    left_imag = left_factor[..., 1, :, :]
    right_real = right_factor[..., 0, :, :]
    right_imag = right_factor[..., 1, :, :]
    highest = lax.Precision.HIGHEST
    real_part = jnp.matmul(left_real, right_real, precision=highest) - jnp.matmul(
        left_imag, right_imag, precision=highest
    )
    imag_part = jnp.matmul(left_real, right_imag, precision=highest) + jnp.matmul(
        left_imag, right_real, precision=highest
    )
    return jnp.stack([real_part, imag_part], axis=-3)


def sandwich(pair_map, inner):
    return complex_product(complex_product(pair_map, inner), jnp.swapaxes(pair_map, -1, -2))


def self_energy_of(green, occupation, phonon_weight, phonon_mode):
    filling = occupation[0]
    real_part = -filling * (green[0] - green[0].T)
    imag_part = -filling * (green[1] + green[1].T)
    lesser = jnp.stack([real_part, imag_part], axis=0).astype(jnp.bfloat16)
    width = lesser.shape[-1]
    moms = lax.axis_size("kmom")
    rows = width // moms
    chunks = lesser.reshape(2, moms, rows, width).transpose(1, 0, 2, 3)
    held = lax.all_to_all(chunks, "kmom", 0, 0)
    below = passed_along(held, "energy", 1)
    above = passed_along(held, "energy", -1)
    flat = held.reshape(moms, -1).astype(jnp.float32)
    near = below.reshape(moms, -1).astype(jnp.float32) + above.reshape(moms, -1).astype(jnp.float32)
    still = phonon_mode[0] == 0
    weight_still = jnp.where(still, phonon_weight[0], phonon_weight[1])
    weight_moved = jnp.where(still, phonon_weight[1], phonon_weight[0])
    summed = jnp.matmul(
        weight_still, flat + flat, precision=lax.Precision.HIGHEST
    ) + jnp.matmul(weight_moved, near, precision=lax.Precision.HIGHEST)
    out = summed.astype(jnp.bfloat16).reshape(moms, 2, rows, width)
    back = lax.all_to_all(out, "kmom", 0, 0)
    return back.transpose(1, 0, 2, 3).reshape(2, width, width)


def on_device(free_green, coupling, coupling_tiles, occupation, phonon_weight, phonon_mode):
    slab_count = free_green.shape[0]
    block_width = coupling.shape[-1]
    tile_count = coupling_tiles.shape[1]
    tile_size = block_width // tile_count
    column_tile = jnp.arange(block_width, dtype=jnp.int32) // tile_size
    tile_hit = jnp.any(coupling_tiles[..., None] == column_tile, axis=-2).astype(jnp.float32)
    tile_mask = jnp.broadcast_to(
        tile_hit[:, :, None, :], (slab_count, tile_count, tile_size, block_width)
    ).reshape(slab_count, block_width, block_width)
    coupled = coupling * tile_mask
    pair_map = jnp.einsum(
        "ekcij,jl->ekcil", free_green[0], coupled[0], precision=lax.Precision.HIGHEST
    )

    def sweep(beyond):
        return free_green[0] + sandwich(pair_map, beyond)

    zero_block = jnp.zeros(free_green.shape[1:], jnp.float32)

    def advance(turn_index, beyond):
        return passed_along(sweep(beyond), "slab", -1)

    beyond = lax.fori_loop(0, lax.axis_size("slab") - 1, advance, zero_block)
    green = sweep(beyond)
    self_energy = self_energy_of(green[0, 0], occupation, phonon_weight, phonon_mode)
    return green[None], self_energy.reshape(green.shape)[None]


def solution(mesh):
    in_specs = (
        P("slab", "energy", "kmom", None, None, None),
        P("slab", None, None),
        P("slab", None, None),
        P("energy"),
        P(),
        P(),
    )
    out_specs = (
        P("slab", "energy", "kmom", None, None, None),
        P("slab", "energy", "kmom", None, None, None),
    )
    return jax.shard_map(
        on_device, mesh=mesh, in_specs=in_specs, out_specs=out_specs, check_vma=False
    )
```

time: 317 us -> 198 us (0.62)
  the two profiles are of different devices: /device:TPU:1 before, /device:TPU:25 now
where the time goes in v1:
time: 198 us; the launch traced here: 197 us
  waiting for transfers between devices  112 us (57%)
  starting transfers between devices  47.2 us (24%)
  matrix products  28.2 us (14%)
  local copies, waits for them, and re-layouts  5.34 us (3%)
  other arithmetic  2.47 us (1%)
    ppermute x9, waiting for transfers between devices, passed_along(): return lax.ppermute(shard, axis, pairs)  96 us
    ppermute x9, starting transfers between devices, passed_along(): return lax.ppermute(shard, axis, pairs)  34.1 us
    all_to_all x1, starting transfers between devices, self_energy_of(): held = lax.all_to_all(chunks, 'kmom', 0, 0)  9.55 us
    all_to_all x1, waiting for transfers between devices, self_energy_of(): held = lax.all_to_all(chunks, 'kmom', 0, 0)  8.13 us
    all_to_all x1, waiting for transfers between devices, self_energy_of(): back = lax.all_to_all(out, 'kmom', 0, 0)  7.93 us
    dot_general x16, matrix products, complex_product(): jnp.matmul(left_imag, right_imag, precision=highest)  6.53 us
    dot_general x16, matrix products, complex_product(): jnp.matmul(left_imag, right_real, precision=highest)  6.52 us
    dot_general x16, matrix products, complex_product(): jnp.matmul(left_real, right_imag, precision=highest)  6.5 us
  transfers between devices with their start and end apart: 11, of which 11 were waited for; matrix products, arithmetic and copies ran while one was open for 1% of the time, Pallas kernels for 0%

profile of v1, /device:TPU:25, one launch (start us, length us, event | category | flops | bytes accessed | tf_op | source)
XLA Modules:
  0.0 197.5 jit_solution(6535309539673673068)
XLA Ops:
  2.5 1.1 fusion.23
  3.8 117.0 %while.10 = (s32[]{:T(128)}, f32[1,1,2,256,256]{4,3,2,1,0:T(8,128)S(1)}, f32[1,1,1,2,256,256]{5,4,3,2,1,0:T(8,128)S(1)}, f32[1,1,2,256,256]{4,3,2,1,0:T(8,128)S(1)}, s32[]{:T(128)}) while((s32[]{:T(128)}, f32[1,1,2,256,256]{4,3,2,1,0:T(8,128)S(1)}, f32[1,1,1,2,256,256]{5,4,3,2,1,0:T(8,128)S(1)}, f32[1,1,2,256,256]{4,3,2,1,0:T(8,128)S(1)}, ...), condition=%wide.region_2.3_spmd, body=%wide.region_1.2_spmd.sunk | while | flops 1611137024 | bytes 11010149 | solution.py:80
  7.1 2.1 %collective-permute-start = (f32[1,1,2,256,256]{4,3,2,1,0:T(8,128)S(1)}, f32[1,1,2,256,256]{4,3,2,1,0:T(8,128)S(1)}, u32[]{:S(2)}, u32[]{:S(2)}) collective-permute-start(f32[1,1,2,256,256]{4,3,2,1,0:T(8,128)S(1)} %maximum_add_fusion.4), channel_id=1, source_target_pairs={{96,0},{192,96},{288,192},{384,288},{480,384},{576,480},{672,576},... | collective-permute-start | bytes 1572872 | tf_op jit(solution)/shard_map/while/body/eval_jaxpr/ppermute | solution.py:10
  9.2 13.8 %collective-permute-done = f32[1,1,2,256,256]{4,3,2,1,0:T(8,128)S(1)} collective-permute-done((f32[1,1,2,256,256]{4,3,2,1,0:T(8,128)S(1)}, f32[1,1,2,256,256]{4,3,2,1,0:T(8,128)S(1)}, u32[]{:S(2)}, u32[]{:S(2)}) %collective-permute-start) | collective-permute-done | bytes 524320 | tf_op jit(solution)/shard_map/while/body/eval_jaxpr/ppermute | solution.py:10
  26.3 1.9 collective-permute-start
  28.2 13.1 %collective-permute-done = f32[1,1,2,256,256]{4,3,2,1,0:T(8,128)S(1)} collective-permute-done((f32[1,1,2,256,256]{4,3,2,1,0:T(8,128)S(1)}, f32[1,1,2,256,256]{4,3,2,1,0:T(8,128)S(1)}, u32[]{:S(2)}, u32[]{:S(2)}) %collective-permute-start) | collective-permute-done | bytes 524320 | tf_op jit(solution)/shard_map/while/body/eval_jaxpr/ppermute | solution.py:10
  44.7 1.9 collective-permute-start
  46.6 12.3 %collective-permute-done = f32[1,1,2,256,256]{4,3,2,1,0:T(8,128)S(1)} collective-permute-done((f32[1,1,2,256,256]{4,3,2,1,0:T(8,128)S(1)}, f32[1,1,2,256,256]{4,3,2,1,0:T(8,128)S(1)}, u32[]{:S(2)}, u32[]{:S(2)}) %collective-permute-start) | collective-permute-done | bytes 524320 | tf_op jit(solution)/shard_map/while/body/eval_jaxpr/ppermute | solution.py:10
  62.2 1.9 collective-permute-start
  64.1 11.4 %collective-permute-done = f32[1,1,2,256,256]{4,3,2,1,0:T(8,128)S(1)} collective-permute-done((f32[1,1,2,256,256]{4,3,2,1,0:T(8,128)S(1)}, f32[1,1,2,256,256]{4,3,2,1,0:T(8,128)S(1)}, u32[]{:S(2)}, u32[]{:S(2)}) %collective-permute-start) | collective-permute-done | bytes 524320 | tf_op jit(solution)/shard_map/while/body/eval_jaxpr/ppermute | solution.py:10
  78.9 1.9 collective-permute-start
  80.8 10.6 %collective-permute-done = f32[1,1,2,256,256]{4,3,2,1,0:T(8,128)S(1)} collective-permute-done((f32[1,1,2,256,256]{4,3,2,1,0:T(8,128)S(1)}, f32[1,1,2,256,256]{4,3,2,1,0:T(8,128)S(1)}, u32[]{:S(2)}, u32[]{:S(2)}) %collective-permute-start) | collective-permute-done | bytes 524320 | tf_op jit(solution)/shard_map/while/body/eval_jaxpr/ppermute | solution.py:10
  94.7 1.9 collective-permute-start
  96.6 9.7 %collective-permute-done = f32[1,1,2,256,256]{4,3,2,1,0:T(8,128)S(1)} collective-permute-done((f32[1,1,2,256,256]{4,3,2,1,0:T(8,128)S(1)}, f32[1,1,2,256,256]{4,3,2,1,0:T(8,128)S(1)}, u32[]{:S(2)}, u32[]{:S(2)}) %collective-permute-start) | collective-permute-done | bytes 524320 | tf_op jit(solution)/shard_map/while/body/eval_jaxpr/ppermute | solution.py:10
  109.6 1.9 collective-permute-start
  111.6 9.2 %collective-permute-done = f32[1,1,2,256,256]{4,3,2,1,0:T(8,128)S(1)} collective-permute-done((f32[1,1,2,256,256]{4,3,2,1,0:T(8,128)S(1)}, f32[1,1,2,256,256]{4,3,2,1,0:T(8,128)S(1)}, u32[]{:S(2)}, u32[]{:S(2)}) %collective-permute-start) | collective-permute-done | bytes 524320 | tf_op jit(solution)/shard_map/while/body/eval_jaxpr/ppermute | solution.py:10
  126.6 9.6 %all-to-all-start = ((bf16[16,2,16,256]{3,2,1,0:T(8,128)(2,1)}), bf16[16,2,16,256]{3,2,1,0:T(8,128)(2,1)S(1)}, u32[]{:S(2)}, u32[]{:S(2)}) async-start(bf16[16,2,16,256]{3,2,1,0:T(8,128)(2,1)} %maximum_bitcast_fusion), calls=%async_computation | async-start | bytes 524288 | tf_op jit(solution)/shard_map/all_to_all | solution.py:41
  136.9 8.1 %all-to-all-done = bf16[16,2,16,256]{3,2,1,0:T(8,128)(2,1)S(1)} async-done(((bf16[16,2,16,256]{3,2,1,0:T(8,128)(2,1)}), bf16[16,2,16,256]{3,2,1,0:T(8,128)(2,1)S(1)}, u32[]{:S(2)}, u32[]{:S(2)}) %all-to-all-start) | async-done | bytes 262176 | tf_op jit(solution)/shard_map/all_to_all | solution.py:41
  145.0 18.6 %collective-permute-start.1 = (bf16[16,2,16,256]{3,2,1,0:T(8,128)(2,1)S(1)}, bf16[16,2,16,256]{3,2,1,0:T(8,128)(2,1)S(1)}, u32[]{:S(2)}, u32[]{:S(2)}) collective-permute-start(bf16[16,2,16,256]{3,2,1,0:T(8,128)(2,1)S(1)} %all-to-all-done), channel_id=1, source_target_pairs={{0,1},{1,2},{2,3},{3,4},{4,5},{6,7},{7,8},{8,9},{9,10},{10,11},{12... | collective-permute-start | bytes 786440 | tf_op jit(solution)/shard_map/ppermute | solution.py:10
  163.6 1.9 collective-permute-start.2
  166.9 15.8 %collective-permute-done.2 = bf16[16,2,16,256]{3,2,1,0:T(8,128)(2,1)S(1)} collective-permute-done((bf16[16,2,16,256]{3,2,1,0:T(8,128)(2,1)S(1)}, bf16[16,2,16,256]{3,2,1,0:T(8,128)(2,1)S(1)}, u32[]{:S(2)}, u32[]{:S(2)}) %collective-permute-start.2) | collective-permute-done | bytes 262176 | tf_op jit(solution)/shard_map/ppermute | solution.py:10
  184.4 3.5 %all-to-all-start.1 = ((bf16[16,2,16,256]{3,2,1,0:T(8,128)(2,1)}), bf16[16,2,16,256]{3,2,1,0:T(8,128)(2,1)S(1)}, u32[]{:S(2)}, u32[]{:S(2)}) async-start(bf16[16,2,16,256]{3,2,1,0:T(8,128)(2,1)} %bitcast.59), calls=%async_computation.1 | async-start | bytes 524288 | tf_op jit(solution)/shard_map/all_to_all | solution.py:53
  188.0 0.9 maximum_add_fusion.1
  188.8 7.9 %all-to-all-done.1 = bf16[16,2,16,256]{3,2,1,0:T(8,128)(2,1)S(1)} async-done(((bf16[16,2,16,256]{3,2,1,0:T(8,128)(2,1)}), bf16[16,2,16,256]{3,2,1,0:T(8,128)(2,1)S(1)}, u32[]{:S(2)}, u32[]{:S(2)}) %all-to-all-start.1) | async-done | bytes 262176 | tf_op jit(solution)/shard_map/all_to_all | solution.py:53
  (104 shorter events, 34.2 us)
Async XLA Ops:
  0.6 0.7 copy-start.3
  0.6 1.0 copy-start.1
  1.4 1.1 copy-start
  7.1 15.9 %collective-permute-start = (f32[1,1,2,256,256]{4,3,2,1,0:T(8,128)S(1)}, f32[1,1,2,256,256]{4,3,2,1,0:T(8,128)S(1)}, u32[]{:S(2)}, u32[]{:S(2)}) collective-permute-start(f32[1,1,2,256,256]{4,3,2,1,0:T(8,128)S(1)} %maximum_add_fusion.4), channel_id=1, source_target_pairs={{96,0},{192,96},{288,192},{384,288},{480,384},{576,480},{672,576},... | collective-permute-start | bytes 1572872 | tf_op jit(solution)/shard_map/while/body/eval_jaxpr/ppermute | solution.py:10
  26.3 15.1 %collective-permute-start = (f32[1,1,2,256,256]{4,3,2,1,0:T(8,128)S(1)}, f32[1,1,2,256,256]{4,3,2,1,0:T(8,128)S(1)}, u32[]{:S(2)}, u32[]{:S(2)}) collective-permute-start(f32[1,1,2,256,256]{4,3,2,1,0:T(8,128)S(1)} %maximum_add_fusion.4), channel_id=1, source_target_pairs={{96,0},{192,96},{288,192},{384,288},{480,384},{576,480},{672,576},... | collective-permute-start | bytes 1572872 | tf_op jit(solution)/shard_map/while/body/eval_jaxpr/ppermute | solution.py:10
  44.7 14.2 %collective-permute-start = (f32[1,1,2,256,256]{4,3,2,1,0:T(8,128)S(1)}, f32[1,1,2,256,256]{4,3,2,1,0:T(8,128)S(1)}, u32[]{:S(2)}, u32[]{:S(2)}) collective-permute-start(f32[1,1,2,256,256]{4,3,2,1,0:T(8,128)S(1)} %maximum_add_fusion.4), channel_id=1, source_target_pairs={{96,0},{192,96},{288,192},{384,288},{480,384},{576,480},{672,576},... | collective-permute-start | bytes 1572872 | tf_op jit(solution)/shard_map/while/body/eval_jaxpr/ppermute | solution.py:10
  62.2 13.4 %collective-permute-start = (f32[1,1,2,256,256]{4,3,2,1,0:T(8,128)S(1)}, f32[1,1,2,256,256]{4,3,2,1,0:T(8,128)S(1)}, u32[]{:S(2)}, u32[]{:S(2)}) collective-permute-start(f32[1,1,2,256,256]{4,3,2,1,0:T(8,128)S(1)} %maximum_add_fusion.4), channel_id=1, source_target_pairs={{96,0},{192,96},{288,192},{384,288},{480,384},{576,480},{672,576},... | collective-permute-start | bytes 1572872 | tf_op jit(solution)/shard_map/while/body/eval_jaxpr/ppermute | solution.py:10
  78.9 12.5 %collective-permute-start = (f32[1,1,2,256,256]{4,3,2,1,0:T(8,128)S(1)}, f32[1,1,2,256,256]{4,3,2,1,0:T(8,128)S(1)}, u32[]{:S(2)}, u32[]{:S(2)}) collective-permute-start(f32[1,1,2,256,256]{4,3,2,1,0:T(8,128)S(1)} %maximum_add_fusion.4), channel_id=1, source_target_pairs={{96,0},{192,96},{288,192},{384,288},{480,384},{576,480},{672,576},... | collective-permute-start | bytes 1572872 | tf_op jit(solution)/shard_map/while/body/eval_jaxpr/ppermute | solution.py:10
  94.7 11.7 %collective-permute-start = (f32[1,1,2,256,256]{4,3,2,1,0:T(8,128)S(1)}, f32[1,1,2,256,256]{4,3,2,1,0:T(8,128)S(1)}, u32[]{:S(2)}, u32[]{:S(2)}) collective-permute-start(f32[1,1,2,256,256]{4,3,2,1,0:T(8,128)S(1)} %maximum_add_fusion.4), channel_id=1, source_target_pairs={{96,0},{192,96},{288,192},{384,288},{480,384},{576,480},{672,576},... | collective-permute-start | bytes 1572872 | tf_op jit(solution)/shard_map/while/body/eval_jaxpr/ppermute | solution.py:10
  109.6 11.1 %collective-permute-start = (f32[1,1,2,256,256]{4,3,2,1,0:T(8,128)S(1)}, f32[1,1,2,256,256]{4,3,2,1,0:T(8,128)S(1)}, u32[]{:S(2)}, u32[]{:S(2)}) collective-permute-start(f32[1,1,2,256,256]{4,3,2,1,0:T(8,128)S(1)} %maximum_add_fusion.4), channel_id=1, source_target_pairs={{96,0},{192,96},{288,192},{384,288},{480,384},{576,480},{672,576},... | collective-permute-start | bytes 1572872 | tf_op jit(solution)/shard_map/while/body/eval_jaxpr/ppermute | solution.py:10
  126.6 18.4 %all-to-all-start = ((bf16[16,2,16,256]{3,2,1,0:T(8,128)(2,1)}), bf16[16,2,16,256]{3,2,1,0:T(8,128)(2,1)S(1)}, u32[]{:S(2)}, u32[]{:S(2)}) async-start(bf16[16,2,16,256]{3,2,1,0:T(8,128)(2,1)} %maximum_bitcast_fusion), calls=%async_computation | async-start | bytes 524288 | tf_op jit(solution)/shard_map/all_to_all | solution.py:41
  136.2 0.7 copy-start.4
  145.0 21.9 %collective-permute-start.1 = (bf16[16,2,16,256]{3,2,1,0:T(8,128)(2,1)S(1)}, bf16[16,2,16,256]{3,2,1,0:T(8,128)(2,1)S(1)}, u32[]{:S(2)}, u32[]{:S(2)}) collective-permute-start(bf16[16,2,16,256]{3,2,1,0:T(8,128)(2,1)S(1)} %all-to-all-done), channel_id=1, source_target_pairs={{0,1},{1,2},{2,3},{3,4},{4,5},{6,7},{7,8},{8,9},{9,10},{10,11},{12... | collective-permute-start | bytes 786440 | tf_op jit(solution)/shard_map/ppermute | solution.py:10
  163.6 19.1 %collective-permute-start.2 = (bf16[16,2,16,256]{3,2,1,0:T(8,128)(2,1)S(1)}, bf16[16,2,16,256]{3,2,1,0:T(8,128)(2,1)S(1)}, u32[]{:S(2)}, u32[]{:S(2)}) collective-permute-start(bf16[16,2,16,256]{3,2,1,0:T(8,128)(2,1)S(1)} %all-to-all-done), channel_id=1, source_target_pairs={{1,0},{2,1},{3,2},{4,3},{5,4},{7,6},{8,7},{9,8},{10,9},{11,10},{13... | collective-permute-start | bytes 786440 | tf_op jit(solution)/shard_map/ppermute | solution.py:10
  165.6 0.7 copy-start.2
  184.4 12.3 %all-to-all-start.1 = ((bf16[16,2,16,256]{3,2,1,0:T(8,128)(2,1)}), bf16[16,2,16,256]{3,2,1,0:T(8,128)(2,1)S(1)}, u32[]{:S(2)}, u32[]{:S(2)}) async-start(bf16[16,2,16,256]{3,2,1,0:T(8,128)(2,1)} %bitcast.59), calls=%async_computation.1 | async-start | bytes 524288 | tf_op jit(solution)/shard_map/all_to_all | solution.py:53

commit v2 on v1

--- a/solution.py
+++ b/solution.py
@@ -15,12 +15,12 @@
     left_imag = left_factor[..., 1, :, :]
     right_real = right_factor[..., 0, :, :]
     right_imag = right_factor[..., 1, :, :]
-    highest = lax.Precision.HIGHEST
-    real_part = jnp.matmul(left_real, right_real, precision=highest) - jnp.matmul(
-        left_imag, right_imag, precision=highest
+    high = lax.Precision.HIGH
+    real_part = jnp.matmul(left_real, right_real, precision=high) - jnp.matmul(
+        left_imag, right_imag, precision=high
     )
-    imag_part = jnp.matmul(left_real, right_imag, precision=highest) + jnp.matmul(
-        left_imag, right_real, precision=highest
+    imag_part = jnp.matmul(left_real, right_imag, precision=high) + jnp.matmul(
+        left_imag, right_real, precision=high
     )
     return jnp.stack([real_part, imag_part], axis=-3)
 
@@ -72,12 +72,11 @@
     def sweep(beyond):
         return free_green[0] + sandwich(pair_map, beyond)
 
-    zero_block = jnp.zeros(free_green.shape[1:], jnp.float32)
-
     def advance(turn_index, beyond):
         return passed_along(sweep(beyond), "slab", -1)
 
-    beyond = lax.fori_loop(0, lax.axis_size("slab") - 1, advance, zero_block)
+    first = passed_along(free_green[0], "slab", -1)
+    beyond = lax.fori_loop(0, lax.axis_size("slab") - 2, advance, first)
     green = sweep(beyond)
     self_energy = self_energy_of(green[0, 0], occupation, phonon_weight, phonon_mode)
     return green[None], self_energy.reshape(green.shape)[None]

time: 198 us -> 186 us (0.939)
  matrix products: 28.2 us -> 19.5 us
  waiting for transfers between devices: 112 us -> 109 us
    dot_general x64 -> x56, matrix products: 26 us -> 17.3 us  [the longest x14 4.35 us: complex_product(): jnp.matmul(left_imag, right_imag, precision=high)]
    ppermute x9, waiting for transfers between devices: 96 us -> 93.1 us  [passed_along(): return lax.ppermute(shard, axis, pairs)]
  transfers between devices with their start and end apart: 11 -> 11, of which waited for: 11 -> 11; matrix products, arithmetic and copies ran while one was open for 1% -> 2% of each run, Pallas kernels for 0% -> 0%
where the time goes in v2:
time: 186 us; the launch traced here: 185 us
  waiting for transfers between devices  109 us (59%)
  starting transfers between devices  47.3 us (25%)
  matrix products  19.5 us (10%)
  local copies, waits for them, and re-layouts  4.62 us (2%)
  other arithmetic  2.4 us (1%)
    ppermute x9, waiting for transfers between devices, passed_along(): return lax.ppermute(shard, axis, pairs)  93.1 us
    ppermute x9, starting transfers between devices, passed_along(): return lax.ppermute(shard, axis, pairs)  34.3 us
    all_to_all x1, starting transfers between devices, self_energy_of(): held = lax.all_to_all(chunks, 'kmom', 0, 0)  9.54 us
    all_to_all x1, waiting for transfers between devices, self_energy_of(): held = lax.all_to_all(chunks, 'kmom', 0, 0)  8.13 us
    all_to_all x1, waiting for transfers between devices, self_energy_of(): back = lax.all_to_all(out, 'kmom', 0, 0)  7.93 us
    dot_general x14, matrix products, complex_product(): jnp.matmul(left_imag, right_imag, precision=high)  4.35 us
    dot_general x14, matrix products, complex_product(): jnp.matmul(left_imag, right_real, precision=high)  4.34 us
    dot_general x14, matrix products, complex_product(): jnp.matmul(left_real, right_imag, precision=high)  4.33 us
  transfers between devices with their start and end apart: 11, of which 11 were waited for; matrix products, arithmetic and copies ran while one was open for 2% of the time, Pallas kernels for 0%

profile of v2, /device:TPU:25, one launch (start us, length us, event | category | flops | bytes accessed | tf_op | source)
XLA Modules:
  0.0 185.1 jit_solution(5724609420233105989)
XLA Ops:
  0.6 2.2 %collective-permute-start.1 = (f32[1,1,2,256,256]{4,3,2,1,0:T(8,128)}, f32[1,1,2,256,256]{4,3,2,1,0:T(8,128)S(1)}, u32[]{:S(2)}, u32[]{:S(2)}) collective-permute-start(f32[1,1,2,256,256]{4,3,2,1,0:T(8,128)} %bitcast.188), channel_id=1, source_target_pairs={{96,0},{192,96},{288,192},{384,288},{480,384},{576,480},{672,576},... | collective-permute-start | bytes 1572872 | tf_op jit(solution)/shard_map/ppermute | solution.py:10
  3.1 1.0 copy-done
  4.0 1.1 fusion.23
  6.0 10.9 %collective-permute-done.1 = f32[1,1,2,256,256]{4,3,2,1,0:T(8,128)S(1)} collective-permute-done((f32[1,1,2,256,256]{4,3,2,1,0:T(8,128)}, f32[1,1,2,256,256]{4,3,2,1,0:T(8,128)S(1)}, u32[]{:S(2)}, u32[]{:S(2)}) %collective-permute-start.1) | collective-permute-done | bytes 524320 | tf_op jit(solution)/shard_map/ppermute | solution.py:10
  16.9 93.4 %while.10 = (s32[]{:T(128)}, f32[1,1,2,256,256]{4,3,2,1,0:T(8,128)S(1)}, f32[1,1,1,2,256,256]{5,4,3,2,1,0:T(8,128)S(1)}, f32[1,1,2,256,256]{4,3,2,1,0:T(8,128)S(1)}, s32[]{:T(128)}) while((s32[]{:T(128)}, f32[1,1,2,256,256]{4,3,2,1,0:T(8,128)S(1)}, f32[1,1,1,2,256,256]{5,4,3,2,1,0:T(8,128)S(1)}, f32[1,1,2,256,256]{4,3,2,1,0:T(8,128)S(1)}, ...), condition=%wide.region_2.3_spmd, body=%wide.region_1.2_spmd.sunk | while | flops 805830656 | bytes 11010149 | solution.py:79
  19.5 1.9 %collective-permute-start = (f32[1,1,2,256,256]{4,3,2,1,0:T(8,128)S(1)}, f32[1,1,2,256,256]{4,3,2,1,0:T(8,128)S(1)}, u32[]{:S(2)}, u32[]{:S(2)}) collective-permute-start(f32[1,1,2,256,256]{4,3,2,1,0:T(8,128)S(1)} %maximum_add_fusion.4), channel_id=1, source_target_pairs={{96,0},{192,96},{288,192},{384,288},{480,384},{576,480},{672,576},... | collective-permute-start | bytes 1572872 | tf_op jit(solution)/shard_map/while/body/eval_jaxpr/ppermute | solution.py:10
  21.4 13.1 %collective-permute-done = f32[1,1,2,256,256]{4,3,2,1,0:T(8,128)S(1)} collective-permute-done((f32[1,1,2,256,256]{4,3,2,1,0:T(8,128)S(1)}, f32[1,1,2,256,256]{4,3,2,1,0:T(8,128)S(1)}, u32[]{:S(2)}, u32[]{:S(2)}) %collective-permute-start) | collective-permute-done | bytes 524320 | tf_op jit(solution)/shard_map/while/body/eval_jaxpr/ppermute | solution.py:10
  37.1 1.9 %collective-permute-start = (f32[1,1,2,256,256]{4,3,2,1,0:T(8,128)S(1)}, f32[1,1,2,256,256]{4,3,2,1,0:T(8,128)S(1)}, u32[]{:S(2)}, u32[]{:S(2)}) collective-permute-start(f32[1,1,2,256,256]{4,3,2,1,0:T(8,128)S(1)} %maximum_add_fusion.4), channel_id=1, source_target_pairs={{96,0},{192,96},{288,192},{384,288},{480,384},{576,480},{672,576},... | collective-permute-start | bytes 1572872 | tf_op jit(solution)/shard_map/while/body/eval_jaxpr/ppermute | solution.py:10
  39.1 12.3 %collective-permute-done = f32[1,1,2,256,256]{4,3,2,1,0:T(8,128)S(1)} collective-permute-done((f32[1,1,2,256,256]{4,3,2,1,0:T(8,128)S(1)}, f32[1,1,2,256,256]{4,3,2,1,0:T(8,128)S(1)}, u32[]{:S(2)}, u32[]{:S(2)}) %collective-permute-start) | collective-permute-done | bytes 524320 | tf_op jit(solution)/shard_map/while/body/eval_jaxpr/ppermute | solution.py:10
  53.9 1.9 %collective-permute-start = (f32[1,1,2,256,256]{4,3,2,1,0:T(8,128)S(1)}, f32[1,1,2,256,256]{4,3,2,1,0:T(8,128)S(1)}, u32[]{:S(2)}, u32[]{:S(2)}) collective-permute-start(f32[1,1,2,256,256]{4,3,2,1,0:T(8,128)S(1)} %maximum_add_fusion.4), channel_id=1, source_target_pairs={{96,0},{192,96},{288,192},{384,288},{480,384},{576,480},{672,576},... | collective-permute-start | bytes 1572872 | tf_op jit(solution)/shard_map/while/body/eval_jaxpr/ppermute | solution.py:10
  55.9 11.4 %collective-permute-done = f32[1,1,2,256,256]{4,3,2,1,0:T(8,128)S(1)} collective-permute-done((f32[1,1,2,256,256]{4,3,2,1,0:T(8,128)S(1)}, f32[1,1,2,256,256]{4,3,2,1,0:T(8,128)S(1)}, u32[]{:S(2)}, u32[]{:S(2)}) %collective-permute-start) | collective-permute-done | bytes 524320 | tf_op jit(solution)/shard_map/while/body/eval_jaxpr/ppermute | solution.py:10
  69.9 1.9 %collective-permute-start = (f32[1,1,2,256,256]{4,3,2,1,0:T(8,128)S(1)}, f32[1,1,2,256,256]{4,3,2,1,0:T(8,128)S(1)}, u32[]{:S(2)}, u32[]{:S(2)}) collective-permute-start(f32[1,1,2,256,256]{4,3,2,1,0:T(8,128)S(1)} %maximum_add_fusion.4), channel_id=1, source_target_pairs={{96,0},{192,96},{288,192},{384,288},{480,384},{576,480},{672,576},... | collective-permute-start | bytes 1572872 | tf_op jit(solution)/shard_map/while/body/eval_jaxpr/ppermute | solution.py:10
  71.8 10.6 %collective-permute-done = f32[1,1,2,256,256]{4,3,2,1,0:T(8,128)S(1)} collective-permute-done((f32[1,1,2,256,256]{4,3,2,1,0:T(8,128)S(1)}, f32[1,1,2,256,256]{4,3,2,1,0:T(8,128)S(1)}, u32[]{:S(2)}, u32[]{:S(2)}) %collective-permute-start) | collective-permute-done | bytes 524320 | tf_op jit(solution)/shard_map/while/body/eval_jaxpr/ppermute | solution.py:10
  84.9 1.9 %collective-permute-start = (f32[1,1,2,256,256]{4,3,2,1,0:T(8,128)S(1)}, f32[1,1,2,256,256]{4,3,2,1,0:T(8,128)S(1)}, u32[]{:S(2)}, u32[]{:S(2)}) collective-permute-start(f32[1,1,2,256,256]{4,3,2,1,0:T(8,128)S(1)} %maximum_add_fusion.4), channel_id=1, source_target_pairs={{96,0},{192,96},{288,192},{384,288},{480,384},{576,480},{672,576},... | collective-permute-start | bytes 1572872 | tf_op jit(solution)/shard_map/while/body/eval_jaxpr/ppermute | solution.py:10
  86.9 9.7 %collective-permute-done = f32[1,1,2,256,256]{4,3,2,1,0:T(8,128)S(1)} collective-permute-done((f32[1,1,2,256,256]{4,3,2,1,0:T(8,128)S(1)}, f32[1,1,2,256,256]{4,3,2,1,0:T(8,128)S(1)}, u32[]{:S(2)}, u32[]{:S(2)}) %collective-permute-start) | collective-permute-done | bytes 524320 | tf_op jit(solution)/shard_map/while/body/eval_jaxpr/ppermute | solution.py:10
  99.2 1.9 %collective-permute-start = (f32[1,1,2,256,256]{4,3,2,1,0:T(8,128)S(1)}, f32[1,1,2,256,256]{4,3,2,1,0:T(8,128)S(1)}, u32[]{:S(2)}, u32[]{:S(2)}) collective-permute-start(f32[1,1,2,256,256]{4,3,2,1,0:T(8,128)S(1)} %maximum_add_fusion.4), channel_id=1, source_target_pairs={{96,0},{192,96},{288,192},{384,288},{480,384},{576,480},{672,576},... | collective-permute-start | bytes 1572872 | tf_op jit(solution)/shard_map/while/body/eval_jaxpr/ppermute | solution.py:10
  101.1 9.2 %collective-permute-done = f32[1,1,2,256,256]{4,3,2,1,0:T(8,128)S(1)} collective-permute-done((f32[1,1,2,256,256]{4,3,2,1,0:T(8,128)S(1)}, f32[1,1,2,256,256]{4,3,2,1,0:T(8,128)S(1)}, u32[]{:S(2)}, u32[]{:S(2)}) %collective-permute-start) | collective-permute-done | bytes 524320 | tf_op jit(solution)/shard_map/while/body/eval_jaxpr/ppermute | solution.py:10
  114.2 9.5 %all-to-all-start = ((bf16[16,2,16,256]{3,2,1,0:T(8,128)(2,1)}), bf16[16,2,16,256]{3,2,1,0:T(8,128)(2,1)S(1)}, u32[]{:S(2)}, u32[]{:S(2)}) async-start(bf16[16,2,16,256]{3,2,1,0:T(8,128)(2,1)} %maximum_bitcast_fusion), calls=%async_computation | async-start | bytes 524288 | tf_op jit(solution)/shard_map/all_to_all | solution.py:41
  124.4 8.1 %all-to-all-done = bf16[16,2,16,256]{3,2,1,0:T(8,128)(2,1)S(1)} async-done(((bf16[16,2,16,256]{3,2,1,0:T(8,128)(2,1)}), bf16[16,2,16,256]{3,2,1,0:T(8,128)(2,1)S(1)}, u32[]{:S(2)}, u32[]{:S(2)}) %all-to-all-start) | async-done | bytes 262176 | tf_op jit(solution)/shard_map/all_to_all | solution.py:41
  132.6 18.6 %collective-permute-start.2 = (bf16[16,2,16,256]{3,2,1,0:T(8,128)(2,1)S(1)}, bf16[16,2,16,256]{3,2,1,0:T(8,128)(2,1)S(1)}, u32[]{:S(2)}, u32[]{:S(2)}) collective-permute-start(bf16[16,2,16,256]{3,2,1,0:T(8,128)(2,1)S(1)} %all-to-all-done), channel_id=1, source_target_pairs={{0,1},{1,2},{2,3},{3,4},{4,5},{6,7},{7,8},{8,9},{9,10},{10,11},{12... | collective-permute-start | bytes 786440 | tf_op jit(solution)/shard_map/ppermute | solution.py:10
  151.2 1.9 %collective-permute-start.3 = (bf16[16,2,16,256]{3,2,1,0:T(8,128)(2,1)S(1)}, bf16[16,2,16,256]{3,2,1,0:T(8,128)(2,1)S(1)}, u32[]{:S(2)}, u32[]{:S(2)}) collective-permute-start(bf16[16,2,16,256]{3,2,1,0:T(8,128)(2,1)S(1)} %all-to-all-done), channel_id=1, source_target_pairs={{1,0},{2,1},{3,2},{4,3},{5,4},{7,6},{8,7},{9,8},{10,9},{11,10},{13... | collective-permute-start | bytes 786440 | tf_op jit(solution)/shard_map/ppermute | solution.py:10
  154.6 15.8 %collective-permute-done.3 = bf16[16,2,16,256]{3,2,1,0:T(8,128)(2,1)S(1)} collective-permute-done((bf16[16,2,16,256]{3,2,1,0:T(8,128)(2,1)S(1)}, bf16[16,2,16,256]{3,2,1,0:T(8,128)(2,1)S(1)}, u32[]{:S(2)}, u32[]{:S(2)}) %collective-permute-start.3) | collective-permute-done | bytes 262176 | tf_op jit(solution)/shard_map/ppermute | solution.py:10
  172.1 3.5 %all-to-all-start.1 = ((bf16[16,2,16,256]{3,2,1,0:T(8,128)(2,1)}), bf16[16,2,16,256]{3,2,1,0:T(8,128)(2,1)S(1)}, u32[]{:S(2)}, u32[]{:S(2)}) async-start(bf16[16,2,16,256]{3,2,1,0:T(8,128)(2,1)} %bitcast.59), calls=%async_computation.1 | async-start | bytes 524288 | tf_op jit(solution)/shard_map/all_to_all | solution.py:53
  176.5 7.9 %all-to-all-done.1 = bf16[16,2,16,256]{3,2,1,0:T(8,128)(2,1)S(1)} async-done(((bf16[16,2,16,256]{3,2,1,0:T(8,128)(2,1)}), bf16[16,2,16,256]{3,2,1,0:T(8,128)(2,1)S(1)}, u32[]{:S(2)}, u32[]{:S(2)}) %all-to-all-start.1) | async-done | bytes 262176 | tf_op jit(solution)/shard_map/all_to_all | solution.py:53
  (94 shorter events, 24.6 us)
Async XLA Ops:
  0.6 2.3 %copy-start.3 = (s32[1,8,3]{1,0,2:T(1,128)S(1)}, s32[1,8,3]{1,0,2:T(1,128)}, u32[]{:S(2)}) copy-start(s32[1,8,3]{1,0,2:T(1,128)} %param.10) | copy-start | bytes 292
  0.6 2.4 %copy-start.1 = (f32[1,256,256]{2,1,0:T(8,128)S(1)}, f32[1,256,256]{2,1,0:T(8,128)}, u32[]{:S(2)}) copy-start(f32[1,256,256]{2,1,0:T(8,128)} %param.9) | copy-start | bytes 786436
  0.6 16.3 %collective-permute-start.1 = (f32[1,1,2,256,256]{4,3,2,1,0:T(8,128)}, f32[1,1,2,256,256]{4,3,2,1,0:T(8,128)S(1)}, u32[]{:S(2)}, u32[]{:S(2)}) collective-permute-start(f32[1,1,2,256,256]{4,3,2,1,0:T(8,128)} %bitcast.188), channel_id=1, source_target_pairs={{96,0},{192,96},{288,192},{384,288},{480,384},{576,480},{672,576},... | collective-permute-start | bytes 1572872 | tf_op jit(solution)/shard_map/ppermute | solution.py:10
  3.0 1.0 copy-start
  19.5 15.1 %collective-permute-start = (f32[1,1,2,256,256]{4,3,2,1,0:T(8,128)S(1)}, f32[1,1,2,256,256]{4,3,2,1,0:T(8,128)S(1)}, u32[]{:S(2)}, u32[]{:S(2)}) collective-permute-start(f32[1,1,2,256,256]{4,3,2,1,0:T(8,128)S(1)} %maximum_add_fusion.4), channel_id=1, source_target_pairs={{96,0},{192,96},{288,192},{384,288},{480,384},{576,480},{672,576},... | collective-permute-start | bytes 1572872 | tf_op jit(solution)/shard_map/while/body/eval_jaxpr/ppermute | solution.py:10
  37.1 14.2 %collective-permute-start = (f32[1,1,2,256,256]{4,3,2,1,0:T(8,128)S(1)}, f32[1,1,2,256,256]{4,3,2,1,0:T(8,128)S(1)}, u32[]{:S(2)}, u32[]{:S(2)}) collective-permute-start(f32[1,1,2,256,256]{4,3,2,1,0:T(8,128)S(1)} %maximum_add_fusion.4), channel_id=1, source_target_pairs={{96,0},{192,96},{288,192},{384,288},{480,384},{576,480},{672,576},... | collective-permute-start | bytes 1572872 | tf_op jit(solution)/shard_map/while/body/eval_jaxpr/ppermute | solution.py:10
  53.9 13.3 %collective-permute-start = (f32[1,1,2,256,256]{4,3,2,1,0:T(8,128)S(1)}, f32[1,1,2,256,256]{4,3,2,1,0:T(8,128)S(1)}, u32[]{:S(2)}, u32[]{:S(2)}) collective-permute-start(f32[1,1,2,256,256]{4,3,2,1,0:T(8,128)S(1)} %maximum_add_fusion.4), channel_id=1, source_target_pairs={{96,0},{192,96},{288,192},{384,288},{480,384},{576,480},{672,576},... | collective-permute-start | bytes 1572872 | tf_op jit(solution)/shard_map/while/body/eval_jaxpr/ppermute | solution.py:10
  69.9 12.5 %collective-permute-start = (f32[1,1,2,256,256]{4,3,2,1,0:T(8,128)S(1)}, f32[1,1,2,256,256]{4,3,2,1,0:T(8,128)S(1)}, u32[]{:S(2)}, u32[]{:S(2)}) collective-permute-start(f32[1,1,2,256,256]{4,3,2,1,0:T(8,128)S(1)} %maximum_add_fusion.4), channel_id=1, source_target_pairs={{96,0},{192,96},{288,192},{384,288},{480,384},{576,480},{672,576},... | collective-permute-start | bytes 1572872 | tf_op jit(solution)/shard_map/while/body/eval_jaxpr/ppermute | solution.py:10
  84.9 11.6 %collective-permute-start = (f32[1,1,2,256,256]{4,3,2,1,0:T(8,128)S(1)}, f32[1,1,2,256,256]{4,3,2,1,0:T(8,128)S(1)}, u32[]{:S(2)}, u32[]{:S(2)}) collective-permute-start(f32[1,1,2,256,256]{4,3,2,1,0:T(8,128)S(1)} %maximum_add_fusion.4), channel_id=1, source_target_pairs={{96,0},{192,96},{288,192},{384,288},{480,384},{576,480},{672,576},... | collective-permute-start | bytes 1572872 | tf_op jit(solution)/shard_map/while/body/eval_jaxpr/ppermute | solution.py:10
  99.2 11.1 %collective-permute-start = (f32[1,1,2,256,256]{4,3,2,1,0:T(8,128)S(1)}, f32[1,1,2,256,256]{4,3,2,1,0:T(8,128)S(1)}, u32[]{:S(2)}, u32[]{:S(2)}) collective-permute-start(f32[1,1,2,256,256]{4,3,2,1,0:T(8,128)S(1)} %maximum_add_fusion.4), channel_id=1, source_target_pairs={{96,0},{192,96},{288,192},{384,288},{480,384},{576,480},{672,576},... | collective-permute-start | bytes 1572872 | tf_op jit(solution)/shard_map/while/body/eval_jaxpr/ppermute | solution.py:10
  114.2 18.4 %all-to-all-start = ((bf16[16,2,16,256]{3,2,1,0:T(8,128)(2,1)}), bf16[16,2,16,256]{3,2,1,0:T(8,128)(2,1)S(1)}, u32[]{:S(2)}, u32[]{:S(2)}) async-start(bf16[16,2,16,256]{3,2,1,0:T(8,128)(2,1)} %maximum_bitcast_fusion), calls=%async_computation | async-start | bytes 524288 | tf_op jit(solution)/shard_map/all_to_all | solution.py:41
  123.7 0.7 copy-start.4
  132.6 22.0 %collective-permute-start.2 = (bf16[16,2,16,256]{3,2,1,0:T(8,128)(2,1)S(1)}, bf16[16,2,16,256]{3,2,1,0:T(8,128)(2,1)S(1)}, u32[]{:S(2)}, u32[]{:S(2)}) collective-permute-start(bf16[16,2,16,256]{3,2,1,0:T(8,128)(2,1)S(1)} %all-to-all-done), channel_id=1, source_target_pairs={{0,1},{1,2},{2,3},{3,4},{4,5},{6,7},{7,8},{8,9},{9,10},{10,11},{12... | collective-permute-start | bytes 786440 | tf_op jit(solution)/shard_map/ppermute | solution.py:10
  151.2 19.1 %collective-permute-start.3 = (bf16[16,2,16,256]{3,2,1,0:T(8,128)(2,1)S(1)}, bf16[16,2,16,256]{3,2,1,0:T(8,128)(2,1)S(1)}, u32[]{:S(2)}, u32[]{:S(2)}) collective-permute-start(bf16[16,2,16,256]{3,2,1,0:T(8,128)(2,1)S(1)} %all-to-all-done), channel_id=1, source_target_pairs={{1,0},{2,1},{3,2},{4,3},{5,4},{7,6},{8,7},{9,8},{10,9},{11,10},{13... | collective-permute-start | bytes 786440 | tf_op jit(solution)/shard_map/ppermute | solution.py:10
  153.2 0.7 copy-start.2
  172.1 12.3 %all-to-all-start.1 = ((bf16[16,2,16,256]{3,2,1,0:T(8,128)(2,1)}), bf16[16,2,16,256]{3,2,1,0:T(8,128)(2,1)S(1)}, u32[]{:S(2)}, u32[]{:S(2)}) async-start(bf16[16,2,16,256]{3,2,1,0:T(8,128)(2,1)} %bitcast.59), calls=%async_computation.1 | async-start | bytes 524288 | tf_op jit(solution)/shard_map/all_to_all | solution.py:53

commit v3 on v2

--- a/solution.py
+++ b/solution.py
@@ -67,10 +67,26 @@
     coupled = coupling * tile_mask
     pair_map = jnp.einsum(
         "ekcij,jl->ekcil", free_green[0], coupled[0], precision=lax.Precision.HIGHEST
+    )[0, 0]
+    map_real, map_imag = pair_map[0], pair_map[1]
+    left_block = jnp.concatenate(
+        [
+            jnp.concatenate([map_real, -map_imag], axis=1),
+            jnp.concatenate([map_imag, map_real], axis=1),
+        ],
+        axis=0,
     )
+    right_block = jnp.concatenate([map_real.T, map_imag.T], axis=1)
+    width = block_width
+    high = lax.Precision.HIGH
 
     def sweep(beyond):
-        return free_green[0] + sandwich(pair_map, beyond)
+        inner = beyond.reshape(2 * width, width)
+        mixed = jnp.matmul(left_block, inner, precision=high)
+        outer = jnp.matmul(mixed, right_block, precision=high)
+        real_part = outer[:width, :width] - outer[width:, width:]
+        imag_part = outer[:width, width:] + outer[width:, :width]
+        return free_green[0] + jnp.stack([real_part, imag_part], axis=0)[None, None]
 
     def advance(turn_index, beyond):
         return passed_along(sweep(beyond), "slab", -1)

time: 186 us -> 179 us (0.962)
  matrix products: 19.5 us -> 12.1 us
  waiting for transfers between devices: 109 us -> 106 us
    dot_general x56 -> x14, matrix products: 17.3 us -> 9.9 us  [the longest x7 5.76 us: sweep(): mixed = jnp.matmul(left_block, inner, precision=high)]
    ppermute x9, waiting for transfers between devices: 93.1 us -> 90.2 us  [passed_along(): return lax.ppermute(shard, axis, pairs)]
    unnamed x15 -> x23, local copies, waits for them, and re-layouts: 3.52 us -> 4.31 us
  transfers between devices with their start and end apart: 11 -> 11, of which waited for: 11 -> 11; matrix products, arithmetic and copies ran while one was open for 2% -> 3% of each run, Pallas kernels for 0% -> 0%
where the time goes in v3:
time: 179 us; the launch traced here: 178 us
  waiting for transfers between devices  106 us (59%)
  starting transfers between devices  47.3 us (26%)
  matrix products  12.1 us (7%)
  local copies, waits for them, and re-layouts  6.33 us (4%)
  other arithmetic  4.03 us (2%)
    ppermute x9, waiting for transfers between devices, passed_along(): return lax.ppermute(shard, axis, pairs)  90.2 us
    ppermute x9, starting transfers between devices, passed_along(): return lax.ppermute(shard, axis, pairs)  34.3 us
    all_to_all x1, starting transfers between devices, self_energy_of(): held = lax.all_to_all(chunks, 'kmom', 0, 0)  9.51 us
    all_to_all x1, waiting for transfers between devices, self_energy_of(): held = lax.all_to_all(chunks, 'kmom', 0, 0)  8.13 us
    all_to_all x1, waiting for transfers between devices, self_energy_of(): back = lax.all_to_all(out, 'kmom', 0, 0)  7.93 us
    dot_general x7, matrix products, sweep(): mixed = jnp.matmul(left_block, inner, precision=high)  5.76 us
    unnamed x23, local copies, waits for them, and re-layouts  4.31 us
    dot_general x7, matrix products, sweep(): outer = jnp.matmul(mixed, right_block, precision=high)  4.14 us
  transfers between devices with their start and end apart: 11, of which 11 were waited for; matrix products, arithmetic and copies ran while one was open for 3% of the time, Pallas kernels for 0%

profile of v3, /device:TPU:25, one launch (start us, length us, event | category | flops | bytes accessed | tf_op | source)
XLA Modules:
  0.0 177.9 jit_solution(4714519340873394083)
XLA Ops:
  0.6 2.2 %collective-permute-start.1 = (f32[1,1,2,256,256]{4,3,2,1,0:T(8,128)}, f32[1,1,2,256,256]{4,3,2,1,0:T(8,128)S(1)}, u32[]{:S(2)}, u32[]{:S(2)}) collective-permute-start(f32[1,1,2,256,256]{4,3,2,1,0:T(8,128)} %bitcast.116), channel_id=1, source_target_pairs={{96,0},{192,96},{288,192},{384,288},{480,384},{576,480},{672,576},... | collective-permute-start | bytes 1572872 | tf_op jit(solution)/shard_map/ppermute | solution.py:10
  4.0 1.1 convolution_bitcast_fusion
  8.8 8.1 %collective-permute-done.1 = f32[1,1,2,256,256]{4,3,2,1,0:T(8,128)S(1)} collective-permute-done((f32[1,1,2,256,256]{4,3,2,1,0:T(8,128)}, f32[1,1,2,256,256]{4,3,2,1,0:T(8,128)S(1)}, u32[]{:S(2)}, u32[]{:S(2)}) %collective-permute-start.1) | collective-permute-done | bytes 524320 | tf_op jit(solution)/shard_map/ppermute | solution.py:10
  16.9 85.9 %while.10 = (s32[]{:T(128)}, f32[1,1,2,256,256]{4,3,2,1,0:T(8,128)S(1)}, f32[1,1,1,2,256,256]{5,4,3,2,1,0:T(8,128)S(1)}, f32[512,512]{1,0:T(8,128)S(1)}, f32[256,512]{1,0:T(8,128)S(1)}, /*index=5*/s32[]{:T(128)}) while((s32[]{:T(128)}, f32[1,1,2,256,256]{4,3,2,1,0:T(8,128)S(1)}, f32[1,1,1,2,256,256]{5,4,3,2,1,0:T(8,128)S(1)}, ...), condition=%wide.region_2.3_spmd, body=%wide.region_1.2_spmd.sunk | while | flops 805699584 | bytes 9437293 | solution.py:95
  18.3 1.9 %collective-permute-start = (f32[1,1,2,256,256]{4,3,2,1,0:T(8,128)S(1)}, f32[1,1,2,256,256]{4,3,2,1,0:T(8,128)S(1)}, u32[]{:S(2)}, u32[]{:S(2)}) collective-permute-start(f32[1,1,2,256,256]{4,3,2,1,0:T(8,128)S(1)} %maximum_add_fusion.4), channel_id=1, source_target_pairs={{96,0},{192,96},{288,192},{384,288},{480,384},{576,480},{672,576},... | collective-permute-start | bytes 1572872 | tf_op jit(solution)/shard_map/while/body/eval_jaxpr/ppermute | solution.py:10
  20.2 13.1 %collective-permute-done = f32[1,1,2,256,256]{4,3,2,1,0:T(8,128)S(1)} collective-permute-done((f32[1,1,2,256,256]{4,3,2,1,0:T(8,128)S(1)}, f32[1,1,2,256,256]{4,3,2,1,0:T(8,128)S(1)}, u32[]{:S(2)}, u32[]{:S(2)}) %collective-permute-start) | collective-permute-done | bytes 524320 | tf_op jit(solution)/shard_map/while/body/eval_jaxpr/ppermute | solution.py:10
  34.7 1.9 %collective-permute-start = (f32[1,1,2,256,256]{4,3,2,1,0:T(8,128)S(1)}, f32[1,1,2,256,256]{4,3,2,1,0:T(8,128)S(1)}, u32[]{:S(2)}, u32[]{:S(2)}) collective-permute-start(f32[1,1,2,256,256]{4,3,2,1,0:T(8,128)S(1)} %maximum_add_fusion.4), channel_id=1, source_target_pairs={{96,0},{192,96},{288,192},{384,288},{480,384},{576,480},{672,576},... | collective-permute-start | bytes 1572872 | tf_op jit(solution)/shard_map/while/body/eval_jaxpr/ppermute | solution.py:10
  36.6 12.3 %collective-permute-done = f32[1,1,2,256,256]{4,3,2,1,0:T(8,128)S(1)} collective-permute-done((f32[1,1,2,256,256]{4,3,2,1,0:T(8,128)S(1)}, f32[1,1,2,256,256]{4,3,2,1,0:T(8,128)S(1)}, u32[]{:S(2)}, u32[]{:S(2)}) %collective-permute-start) | collective-permute-done | bytes 524320 | tf_op jit(solution)/shard_map/while/body/eval_jaxpr/ppermute | solution.py:10
  50.2 1.9 %collective-permute-start = (f32[1,1,2,256,256]{4,3,2,1,0:T(8,128)S(1)}, f32[1,1,2,256,256]{4,3,2,1,0:T(8,128)S(1)}, u32[]{:S(2)}, u32[]{:S(2)}) collective-permute-start(f32[1,1,2,256,256]{4,3,2,1,0:T(8,128)S(1)} %maximum_add_fusion.4), channel_id=1, source_target_pairs={{96,0},{192,96},{288,192},{384,288},{480,384},{576,480},{672,576},... | collective-permute-start | bytes 1572872 | tf_op jit(solution)/shard_map/while/body/eval_jaxpr/ppermute | solution.py:10
  52.1 11.4 %collective-permute-done = f32[1,1,2,256,256]{4,3,2,1,0:T(8,128)S(1)} collective-permute-done((f32[1,1,2,256,256]{4,3,2,1,0:T(8,128)S(1)}, f32[1,1,2,256,256]{4,3,2,1,0:T(8,128)S(1)}, u32[]{:S(2)}, u32[]{:S(2)}) %collective-permute-start) | collective-permute-done | bytes 524320 | tf_op jit(solution)/shard_map/while/body/eval_jaxpr/ppermute | solution.py:10
  64.9 1.9 %collective-permute-start = (f32[1,1,2,256,256]{4,3,2,1,0:T(8,128)S(1)}, f32[1,1,2,256,256]{4,3,2,1,0:T(8,128)S(1)}, u32[]{:S(2)}, u32[]{:S(2)}) collective-permute-start(f32[1,1,2,256,256]{4,3,2,1,0:T(8,128)S(1)} %maximum_add_fusion.4), channel_id=1, source_target_pairs={{96,0},{192,96},{288,192},{384,288},{480,384},{576,480},{672,576},... | collective-permute-start | bytes 1572872 | tf_op jit(solution)/shard_map/while/body/eval_jaxpr/ppermute | solution.py:10
  66.8 10.6 %collective-permute-done = f32[1,1,2,256,256]{4,3,2,1,0:T(8,128)S(1)} collective-permute-done((f32[1,1,2,256,256]{4,3,2,1,0:T(8,128)S(1)}, f32[1,1,2,256,256]{4,3,2,1,0:T(8,128)S(1)}, u32[]{:S(2)}, u32[]{:S(2)}) %collective-permute-start) | collective-permute-done | bytes 524320 | tf_op jit(solution)/shard_map/while/body/eval_jaxpr/ppermute | solution.py:10
  78.7 1.9 %collective-permute-start = (f32[1,1,2,256,256]{4,3,2,1,0:T(8,128)S(1)}, f32[1,1,2,256,256]{4,3,2,1,0:T(8,128)S(1)}, u32[]{:S(2)}, u32[]{:S(2)}) collective-permute-start(f32[1,1,2,256,256]{4,3,2,1,0:T(8,128)S(1)} %maximum_add_fusion.4), channel_id=1, source_target_pairs={{96,0},{192,96},{288,192},{384,288},{480,384},{576,480},{672,576},... | collective-permute-start | bytes 1572872 | tf_op jit(solution)/shard_map/while/body/eval_jaxpr/ppermute | solution.py:10
  80.7 9.7 %collective-permute-done = f32[1,1,2,256,256]{4,3,2,1,0:T(8,128)S(1)} collective-permute-done((f32[1,1,2,256,256]{4,3,2,1,0:T(8,128)S(1)}, f32[1,1,2,256,256]{4,3,2,1,0:T(8,128)S(1)}, u32[]{:S(2)}, u32[]{:S(2)}) %collective-permute-start) | collective-permute-done | bytes 524320 | tf_op jit(solution)/shard_map/while/body/eval_jaxpr/ppermute | solution.py:10
  91.7 1.9 %collective-permute-start = (f32[1,1,2,256,256]{4,3,2,1,0:T(8,128)S(1)}, f32[1,1,2,256,256]{4,3,2,1,0:T(8,128)S(1)}, u32[]{:S(2)}, u32[]{:S(2)}) collective-permute-start(f32[1,1,2,256,256]{4,3,2,1,0:T(8,128)S(1)} %maximum_add_fusion.4), channel_id=1, source_target_pairs={{96,0},{192,96},{288,192},{384,288},{480,384},{576,480},{672,576},... | collective-permute-start | bytes 1572872 | tf_op jit(solution)/shard_map/while/body/eval_jaxpr/ppermute | solution.py:10
  93.7 9.2 %collective-permute-done = f32[1,1,2,256,256]{4,3,2,1,0:T(8,128)S(1)} collective-permute-done((f32[1,1,2,256,256]{4,3,2,1,0:T(8,128)S(1)}, f32[1,1,2,256,256]{4,3,2,1,0:T(8,128)S(1)}, u32[]{:S(2)}, u32[]{:S(2)}) %collective-permute-start) | collective-permute-done | bytes 524320 | tf_op jit(solution)/shard_map/while/body/eval_jaxpr/ppermute | solution.py:10
  102.9 2.2 %fusion.26 = f32[512,256]{1,0:T(8,128)S(1)} fusion(f32[512,256]{1,0:T(8,128)S(1)} %bitcast.118, f32[256,256]{0,1:T(8,128)} %copy-done.4, f32[256,256]{0,1:T(8,128)} %copy-done.3, f32[256,256]{0,1:T(8,128)} %copy-done.2), kind=kOutput, calls=%fused_computation.54 | convolution fusion | flops 403439616 | bytes 1835008 | tf_op jit(solution)/shard_map/dot_general | solution.py:85
  107.0 9.5 %all-to-all-start = ((bf16[16,2,16,256]{3,2,1,0:T(8,128)(2,1)}), bf16[16,2,16,256]{3,2,1,0:T(8,128)(2,1)S(1)}, u32[]{:S(2)}, u32[]{:S(2)}) async-start(bf16[16,2,16,256]{3,2,1,0:T(8,128)(2,1)} %maximum_bitcast_fusion), calls=%async_computation | async-start | bytes 524288 | tf_op jit(solution)/shard_map/all_to_all | solution.py:41
  117.2 8.1 %all-to-all-done = bf16[16,2,16,256]{3,2,1,0:T(8,128)(2,1)S(1)} async-done(((bf16[16,2,16,256]{3,2,1,0:T(8,128)(2,1)}), bf16[16,2,16,256]{3,2,1,0:T(8,128)(2,1)S(1)}, u32[]{:S(2)}, u32[]{:S(2)}) %all-to-all-start) | async-done | bytes 262176 | tf_op jit(solution)/shard_map/all_to_all | solution.py:41
  125.4 18.6 %collective-permute-start.2 = (bf16[16,2,16,256]{3,2,1,0:T(8,128)(2,1)S(1)}, bf16[16,2,16,256]{3,2,1,0:T(8,128)(2,1)S(1)}, u32[]{:S(2)}, u32[]{:S(2)}) collective-permute-start(bf16[16,2,16,256]{3,2,1,0:T(8,128)(2,1)S(1)} %all-to-all-done), channel_id=1, source_target_pairs={{0,1},{1,2},{2,3},{3,4},{4,5},{6,7},{7,8},{8,9},{9,10},{10,11},{12... | collective-permute-start | bytes 786440 | tf_op jit(solution)/shard_map/ppermute | solution.py:10
  144.0 1.9 %collective-permute-start.3 = (bf16[16,2,16,256]{3,2,1,0:T(8,128)(2,1)S(1)}, bf16[16,2,16,256]{3,2,1,0:T(8,128)(2,1)S(1)}, u32[]{:S(2)}, u32[]{:S(2)}) collective-permute-start(bf16[16,2,16,256]{3,2,1,0:T(8,128)(2,1)S(1)} %all-to-all-done), channel_id=1, source_target_pairs={{1,0},{2,1},{3,2},{4,3},{5,4},{7,6},{8,7},{9,8},{10,9},{11,10},{13... | collective-permute-start | bytes 786440 | tf_op jit(solution)/shard_map/ppermute | solution.py:10
  147.4 15.8 %collective-permute-done.3 = bf16[16,2,16,256]{3,2,1,0:T(8,128)(2,1)S(1)} collective-permute-done((bf16[16,2,16,256]{3,2,1,0:T(8,128)(2,1)S(1)}, bf16[16,2,16,256]{3,2,1,0:T(8,128)(2,1)S(1)}, u32[]{:S(2)}, u32[]{:S(2)}) %collective-permute-start.3) | collective-permute-done | bytes 262176 | tf_op jit(solution)/shard_map/ppermute | solution.py:10
  164.9 3.5 %all-to-all-start.1 = ((bf16[16,2,16,256]{3,2,1,0:T(8,128)(2,1)}), bf16[16,2,16,256]{3,2,1,0:T(8,128)(2,1)S(1)}, u32[]{:S(2)}, u32[]{:S(2)}) async-start(bf16[16,2,16,256]{3,2,1,0:T(8,128)(2,1)} %bitcast.50), calls=%async_computation.1 | async-start | bytes 524288 | tf_op jit(solution)/shard_map/all_to_all | solution.py:53
  169.3 7.9 %all-to-all-done.1 = bf16[16,2,16,256]{3,2,1,0:T(8,128)(2,1)S(1)} async-done(((bf16[16,2,16,256]{3,2,1,0:T(8,128)(2,1)}), bf16[16,2,16,256]{3,2,1,0:T(8,128)(2,1)S(1)}, u32[]{:S(2)}, u32[]{:S(2)}) %all-to-all-start.1) | async-done | bytes 262176 | tf_op jit(solution)/shard_map/all_to_all | solution.py:53
  (71 shorter events, 19.2 us)
Async XLA Ops:
  0.6 2.3 %copy-start.7 = (s32[1,8,3]{1,0,2:T(1,128)S(1)}, s32[1,8,3]{1,0,2:T(1,128)}, u32[]{:S(2)}) copy-start(s32[1,8,3]{1,0,2:T(1,128)} %param.10) | copy-start | bytes 292
  0.6 2.4 %copy-start.5 = (f32[1,256,256]{2,1,0:T(8,128)S(1)}, f32[1,256,256]{2,1,0:T(8,128)}, u32[]{:S(2)}) copy-start(f32[1,256,256]{2,1,0:T(8,128)} %param.9) | copy-start | bytes 786436
  0.6 16.3 %collective-permute-start.1 = (f32[1,1,2,256,256]{4,3,2,1,0:T(8,128)}, f32[1,1,2,256,256]{4,3,2,1,0:T(8,128)S(1)}, u32[]{:S(2)}, u32[]{:S(2)}) collective-permute-start(f32[1,1,2,256,256]{4,3,2,1,0:T(8,128)} %bitcast.116), channel_id=1, source_target_pairs={{96,0},{192,96},{288,192},{384,288},{480,384},{576,480},{672,576},... | collective-permute-start | bytes 1572872 | tf_op jit(solution)/shard_map/ppermute | solution.py:10
  3.0 1.0 copy-start
  5.1 0.8 copy-start.2
  5.9 0.7 copy-start.3
  5.9 0.8 copy-start.4
  18.3 15.1 %collective-permute-start = (f32[1,1,2,256,256]{4,3,2,1,0:T(8,128)S(1)}, f32[1,1,2,256,256]{4,3,2,1,0:T(8,128)S(1)}, u32[]{:S(2)}, u32[]{:S(2)}) collective-permute-start(f32[1,1,2,256,256]{4,3,2,1,0:T(8,128)S(1)} %maximum_add_fusion.4), channel_id=1, source_target_pairs={{96,0},{192,96},{288,192},{384,288},{480,384},{576,480},{672,576},... | collective-permute-start | bytes 1572872 | tf_op jit(solution)/shard_map/while/body/eval_jaxpr/ppermute | solution.py:10
  34.7 14.2 %collective-permute-start = (f32[1,1,2,256,256]{4,3,2,1,0:T(8,128)S(1)}, f32[1,1,2,256,256]{4,3,2,1,0:T(8,128)S(1)}, u32[]{:S(2)}, u32[]{:S(2)}) collective-permute-start(f32[1,1,2,256,256]{4,3,2,1,0:T(8,128)S(1)} %maximum_add_fusion.4), channel_id=1, source_target_pairs={{96,0},{192,96},{288,192},{384,288},{480,384},{576,480},{672,576},... | collective-permute-start | bytes 1572872 | tf_op jit(solution)/shard_map/while/body/eval_jaxpr/ppermute | solution.py:10
  50.2 13.3 %collective-permute-start = (f32[1,1,2,256,256]{4,3,2,1,0:T(8,128)S(1)}, f32[1,1,2,256,256]{4,3,2,1,0:T(8,128)S(1)}, u32[]{:S(2)}, u32[]{:S(2)}) collective-permute-start(f32[1,1,2,256,256]{4,3,2,1,0:T(8,128)S(1)} %maximum_add_fusion.4), channel_id=1, source_target_pairs={{96,0},{192,96},{288,192},{384,288},{480,384},{576,480},{672,576},... | collective-permute-start | bytes 1572872 | tf_op jit(solution)/shard_map/while/body/eval_jaxpr/ppermute | solution.py:10
  64.9 12.5 %collective-permute-start = (f32[1,1,2,256,256]{4,3,2,1,0:T(8,128)S(1)}, f32[1,1,2,256,256]{4,3,2,1,0:T(8,128)S(1)}, u32[]{:S(2)}, u32[]{:S(2)}) collective-permute-start(f32[1,1,2,256,256]{4,3,2,1,0:T(8,128)S(1)} %maximum_add_fusion.4), channel_id=1, source_target_pairs={{96,0},{192,96},{288,192},{384,288},{480,384},{576,480},{672,576},... | collective-permute-start | bytes 1572872 | tf_op jit(solution)/shard_map/while/body/eval_jaxpr/ppermute | solution.py:10
  78.7 11.6 %collective-permute-start = (f32[1,1,2,256,256]{4,3,2,1,0:T(8,128)S(1)}, f32[1,1,2,256,256]{4,3,2,1,0:T(8,128)S(1)}, u32[]{:S(2)}, u32[]{:S(2)}) collective-permute-start(f32[1,1,2,256,256]{4,3,2,1,0:T(8,128)S(1)} %maximum_add_fusion.4), channel_id=1, source_target_pairs={{96,0},{192,96},{288,192},{384,288},{480,384},{576,480},{672,576},... | collective-permute-start | bytes 1572872 | tf_op jit(solution)/shard_map/while/body/eval_jaxpr/ppermute | solution.py:10
  91.7 11.1 %collective-permute-start = (f32[1,1,2,256,256]{4,3,2,1,0:T(8,128)S(1)}, f32[1,1,2,256,256]{4,3,2,1,0:T(8,128)S(1)}, u32[]{:S(2)}, u32[]{:S(2)}) collective-permute-start(f32[1,1,2,256,256]{4,3,2,1,0:T(8,128)S(1)} %maximum_add_fusion.4), channel_id=1, source_target_pairs={{96,0},{192,96},{288,192},{384,288},{480,384},{576,480},{672,576},... | collective-permute-start | bytes 1572872 | tf_op jit(solution)/shard_map/while/body/eval_jaxpr/ppermute | solution.py:10
  102.9 2.2 %copy-start.1 = (f32[256,256]{1,0:T(8,128)S(1)}, f32[256,256]{1,0:T(8,128)}, u32[]{:S(2)}) copy-start(f32[256,256]{1,0:T(8,128)} %get-tuple-element.66) | copy-start | bytes 786436
  107.0 18.4 %all-to-all-start = ((bf16[16,2,16,256]{3,2,1,0:T(8,128)(2,1)}), bf16[16,2,16,256]{3,2,1,0:T(8,128)(2,1)S(1)}, u32[]{:S(2)}, u32[]{:S(2)}) async-start(bf16[16,2,16,256]{3,2,1,0:T(8,128)(2,1)} %maximum_bitcast_fusion), calls=%async_computation | async-start | bytes 524288 | tf_op jit(solution)/shard_map/all_to_all | solution.py:41
  116.5 0.7 copy-start.8
  125.4 22.0 %collective-permute-start.2 = (bf16[16,2,16,256]{3,2,1,0:T(8,128)(2,1)S(1)}, bf16[16,2,16,256]{3,2,1,0:T(8,128)(2,1)S(1)}, u32[]{:S(2)}, u32[]{:S(2)}) collective-permute-start(bf16[16,2,16,256]{3,2,1,0:T(8,128)(2,1)S(1)} %all-to-all-done), channel_id=1, source_target_pairs={{0,1},{1,2},{2,3},{3,4},{4,5},{6,7},{7,8},{8,9},{9,10},{10,11},{12... | collective-permute-start | bytes 786440 | tf_op jit(solution)/shard_map/ppermute | solution.py:10
  144.0 19.1 %collective-permute-start.3 = (bf16[16,2,16,256]{3,2,1,0:T(8,128)(2,1)S(1)}, bf16[16,2,16,256]{3,2,1,0:T(8,128)(2,1)S(1)}, u32[]{:S(2)}, u32[]{:S(2)}) collective-permute-start(bf16[16,2,16,256]{3,2,1,0:T(8,128)(2,1)S(1)} %all-to-all-done), channel_id=1, source_target_pairs={{1,0},{2,1},{3,2},{4,3},{5,4},{7,6},{8,7},{9,8},{10,9},{11,10},{13... | collective-permute-start | bytes 786440 | tf_op jit(solution)/shard_map/ppermute | solution.py:10
  146.0 0.7 copy-start.6
  164.9 12.3 %all-to-all-start.1 = ((bf16[16,2,16,256]{3,2,1,0:T(8,128)(2,1)}), bf16[16,2,16,256]{3,2,1,0:T(8,128)(2,1)S(1)}, u32[]{:S(2)}, u32[]{:S(2)}) async-start(bf16[16,2,16,256]{3,2,1,0:T(8,128)(2,1)} %bitcast.50), calls=%async_computation.1 | async-start | bytes 524288 | tf_op jit(solution)/shard_map/all_to_all | solution.py:53

commit v4 on v3

--- a/solution.py
+++ b/solution.py
@@ -38,11 +38,15 @@
     moms = lax.axis_size("kmom")
     rows = width // moms
     chunks = lesser.reshape(2, moms, rows, width).transpose(1, 0, 2, 3)
+    below = passed_along(lesser, "energy", 1)
+    above = passed_along(lesser, "energy", -1)
     held = lax.all_to_all(chunks, "kmom", 0, 0)
-    below = passed_along(held, "energy", 1)
-    above = passed_along(held, "energy", -1)
+    sides = jnp.stack([below, above], axis=0).reshape(2, 2, moms, rows, width).transpose(2, 0, 1, 3, 4)
+    held_sides = lax.all_to_all(sides, "kmom", 0, 0)
     flat = held.reshape(moms, -1).astype(jnp.float32)
-    near = below.reshape(moms, -1).astype(jnp.float32) + above.reshape(moms, -1).astype(jnp.float32)
+    near = held_sides[:, 0].reshape(moms, -1).astype(jnp.float32) + held_sides[:, 1].reshape(
+        moms, -1
+    ).astype(jnp.float32)
     still = phonon_mode[0] == 0
     weight_still = jnp.where(still, phonon_weight[0], phonon_weight[1])
     weight_moved = jnp.where(still, phonon_weight[1], phonon_weight[0])

time: 179 us -> 187 us (1.045)
  starting transfers between devices: 47.3 us -> 56.7 us
  waiting for transfers between devices: 106 us -> 104 us
    all_to_all x0 -> x1, starting transfers between devices: none -> 10.5 us  [self_energy_of(): held_sides = lax.all_to_all(sides, 'kmom', 0, 0)]
    all_to_all x0 -> x1, waiting for transfers between devices: none -> 9.08 us  [self_energy_of(): held_sides = lax.all_to_all(sides, 'kmom', 0, 0)]
    all_to_all x1, waiting for transfers between devices: 8.13 us -> 0.01 us  [self_energy_of(): held = lax.all_to_all(chunks, 'kmom', 0, 0)]
    ppermute x9, waiting for transfers between devices: 90.2 us -> 86.8 us  [passed_along(): return lax.ppermute(shard, axis, pairs)]
  transfers between devices with their start and end apart: 11 -> 12, of which waited for: 11 -> 11; matrix products, arithmetic and copies ran while one was open for 3% -> 3% of each run, Pallas kernels for 0% -> 0%
where the time goes in v4:
time: 187 us; the launch traced here: 186 us
  waiting for transfers between devices  104 us (56%)
  starting transfers between devices  56.7 us (30%)
  matrix products  12.1 us (6%)
  local copies, waits for them, and re-layouts  6.34 us (3%)
  other arithmetic  4.93 us (3%)
    ppermute x9, waiting for transfers between devices, passed_along(): return lax.ppermute(shard, axis, pairs)  86.8 us
    ppermute x9, starting transfers between devices, passed_along(): return lax.ppermute(shard, axis, pairs)  33.2 us
    all_to_all x1, starting transfers between devices, self_energy_of(): held_sides = lax.all_to_all(sides, 'kmom', 0, 0)  10.5 us
    all_to_all x1, starting transfers between devices, self_energy_of(): held = lax.all_to_all(chunks, 'kmom', 0, 0)  9.51 us
    all_to_all x1, waiting for transfers between devices, self_energy_of(): held_sides = lax.all_to_all(sides, 'kmom', 0, 0)  9.08 us
    all_to_all x1, waiting for transfers between devices, self_energy_of(): back = lax.all_to_all(out, 'kmom', 0, 0)  7.93 us
    dot_general x7, matrix products, sweep(): mixed = jnp.matmul(left_block, inner, precision=high)  5.76 us
    unnamed x23, local copies, waits for them, and re-layouts  4.31 us
  transfers between devices with their start and end apart: 12, of which 11 were waited for; matrix products, arithmetic and copies ran while one was open for 3% of the time, Pallas kernels for 0%

profile of v4, /device:TPU:25, one launch (start us, length us, event | category | flops | bytes accessed | tf_op | source)
XLA Modules:
  0.0 185.7 jit_solution(3973147582041003267)
XLA Ops:
  0.6 2.2 %collective-permute-start.1 = (f32[1,1,2,256,256]{4,3,2,1,0:T(8,128)}, f32[1,1,2,256,256]{4,3,2,1,0:T(8,128)S(1)}, u32[]{:S(2)}, u32[]{:S(2)}) collective-permute-start(f32[1,1,2,256,256]{4,3,2,1,0:T(8,128)} %bitcast.122), channel_id=1, source_target_pairs={{96,0},{192,96},{288,192},{384,288},{480,384},{576,480},{672,576},... | collective-permute-start | bytes 1572872 | tf_op jit(solution)/shard_map/ppermute | solution.py:10
  8.8 8.1 %collective-permute-done.1 = f32[1,1,2,256,256]{4,3,2,1,0:T(8,128)S(1)} collective-permute-done((f32[1,1,2,256,256]{4,3,2,1,0:T(8,128)}, f32[1,1,2,256,256]{4,3,2,1,0:T(8,128)S(1)}, u32[]{:S(2)}, u32[]{:S(2)}) %collective-permute-start.1) | collective-permute-done | bytes 524320 | tf_op jit(solution)/shard_map/ppermute | solution.py:10
  16.9 85.9 %while.10 = (s32[]{:T(128)}, f32[1,1,2,256,256]{4,3,2,1,0:T(8,128)S(1)}, f32[1,1,1,2,256,256]{5,4,3,2,1,0:T(8,128)S(1)}, f32[512,512]{1,0:T(8,128)S(1)}, f32[256,512]{1,0:T(8,128)S(1)}, /*index=5*/s32[]{:T(128)}) while((s32[]{:T(128)}, f32[1,1,2,256,256]{4,3,2,1,0:T(8,128)S(1)}, f32[1,1,1,2,256,256]{5,4,3,2,1,0:T(8,128)S(1)}, ...), condition=%wide.region_2.3_spmd, body=%wide.region_1.2_spmd.sunk | while | flops 805699584 | bytes 9437293 | solution.py:99
  18.3 1.9 %collective-permute-start = (f32[1,1,2,256,256]{4,3,2,1,0:T(8,128)S(1)}, f32[1,1,2,256,256]{4,3,2,1,0:T(8,128)S(1)}, u32[]{:S(2)}, u32[]{:S(2)}) collective-permute-start(f32[1,1,2,256,256]{4,3,2,1,0:T(8,128)S(1)} %maximum_add_fusion.4), channel_id=1, source_target_pairs={{96,0},{192,96},{288,192},{384,288},{480,384},{576,480},{672,576},... | collective-permute-start | bytes 1572872 | tf_op jit(solution)/shard_map/while/body/eval_jaxpr/ppermute | solution.py:10
  20.2 13.1 %collective-permute-done = f32[1,1,2,256,256]{4,3,2,1,0:T(8,128)S(1)} collective-permute-done((f32[1,1,2,256,256]{4,3,2,1,0:T(8,128)S(1)}, f32[1,1,2,256,256]{4,3,2,1,0:T(8,128)S(1)}, u32[]{:S(2)}, u32[]{:S(2)}) %collective-permute-start) | collective-permute-done | bytes 524320 | tf_op jit(solution)/shard_map/while/body/eval_jaxpr/ppermute | solution.py:10
  34.7 1.9 %collective-permute-start = (f32[1,1,2,256,256]{4,3,2,1,0:T(8,128)S(1)}, f32[1,1,2,256,256]{4,3,2,1,0:T(8,128)S(1)}, u32[]{:S(2)}, u32[]{:S(2)}) collective-permute-start(f32[1,1,2,256,256]{4,3,2,1,0:T(8,128)S(1)} %maximum_add_fusion.4), channel_id=1, source_target_pairs={{96,0},{192,96},{288,192},{384,288},{480,384},{576,480},{672,576},... | collective-permute-start | bytes 1572872 | tf_op jit(solution)/shard_map/while/body/eval_jaxpr/ppermute | solution.py:10
  36.6 12.3 %collective-permute-done = f32[1,1,2,256,256]{4,3,2,1,0:T(8,128)S(1)} collective-permute-done((f32[1,1,2,256,256]{4,3,2,1,0:T(8,128)S(1)}, f32[1,1,2,256,256]{4,3,2,1,0:T(8,128)S(1)}, u32[]{:S(2)}, u32[]{:S(2)}) %collective-permute-start) | collective-permute-done | bytes 524320 | tf_op jit(solution)/shard_map/while/body/eval_jaxpr/ppermute | solution.py:10
  50.2 1.9 %collective-permute-start = (f32[1,1,2,256,256]{4,3,2,1,0:T(8,128)S(1)}, f32[1,1,2,256,256]{4,3,2,1,0:T(8,128)S(1)}, u32[]{:S(2)}, u32[]{:S(2)}) collective-permute-start(f32[1,1,2,256,256]{4,3,2,1,0:T(8,128)S(1)} %maximum_add_fusion.4), channel_id=1, source_target_pairs={{96,0},{192,96},{288,192},{384,288},{480,384},{576,480},{672,576},... | collective-permute-start | bytes 1572872 | tf_op jit(solution)/shard_map/while/body/eval_jaxpr/ppermute | solution.py:10
  52.1 11.4 %collective-permute-done = f32[1,1,2,256,256]{4,3,2,1,0:T(8,128)S(1)} collective-permute-done((f32[1,1,2,256,256]{4,3,2,1,0:T(8,128)S(1)}, f32[1,1,2,256,256]{4,3,2,1,0:T(8,128)S(1)}, u32[]{:S(2)}, u32[]{:S(2)}) %collective-permute-start) | collective-permute-done | bytes 524320 | tf_op jit(solution)/shard_map/while/body/eval_jaxpr/ppermute | solution.py:10
  64.9 1.9 %collective-permute-start = (f32[1,1,2,256,256]{4,3,2,1,0:T(8,128)S(1)}, f32[1,1,2,256,256]{4,3,2,1,0:T(8,128)S(1)}, u32[]{:S(2)}, u32[]{:S(2)}) collective-permute-start(f32[1,1,2,256,256]{4,3,2,1,0:T(8,128)S(1)} %maximum_add_fusion.4), channel_id=1, source_target_pairs={{96,0},{192,96},{288,192},{384,288},{480,384},{576,480},{672,576},... | collective-permute-start | bytes 1572872 | tf_op jit(solution)/shard_map/while/body/eval_jaxpr/ppermute | solution.py:10
  66.8 10.6 %collective-permute-done = f32[1,1,2,256,256]{4,3,2,1,0:T(8,128)S(1)} collective-permute-done((f32[1,1,2,256,256]{4,3,2,1,0:T(8,128)S(1)}, f32[1,1,2,256,256]{4,3,2,1,0:T(8,128)S(1)}, u32[]{:S(2)}, u32[]{:S(2)}) %collective-permute-start) | collective-permute-done | bytes 524320 | tf_op jit(solution)/shard_map/while/body/eval_jaxpr/ppermute | solution.py:10
  78.7 1.9 %collective-permute-start = (f32[1,1,2,256,256]{4,3,2,1,0:T(8,128)S(1)}, f32[1,1,2,256,256]{4,3,2,1,0:T(8,128)S(1)}, u32[]{:S(2)}, u32[]{:S(2)}) collective-permute-start(f32[1,1,2,256,256]{4,3,2,1,0:T(8,128)S(1)} %maximum_add_fusion.4), channel_id=1, source_target_pairs={{96,0},{192,96},{288,192},{384,288},{480,384},{576,480},{672,576},... | collective-permute-start | bytes 1572872 | tf_op jit(solution)/shard_map/while/body/eval_jaxpr/ppermute | solution.py:10
  80.7 9.7 %collective-permute-done = f32[1,1,2,256,256]{4,3,2,1,0:T(8,128)S(1)} collective-permute-done((f32[1,1,2,256,256]{4,3,2,1,0:T(8,128)S(1)}, f32[1,1,2,256,256]{4,3,2,1,0:T(8,128)S(1)}, u32[]{:S(2)}, u32[]{:S(2)}) %collective-permute-start) | collective-permute-done | bytes 524320 | tf_op jit(solution)/shard_map/while/body/eval_jaxpr/ppermute | solution.py:10
  91.7 1.9 %collective-permute-start = (f32[1,1,2,256,256]{4,3,2,1,0:T(8,128)S(1)}, f32[1,1,2,256,256]{4,3,2,1,0:T(8,128)S(1)}, u32[]{:S(2)}, u32[]{:S(2)}) collective-permute-start(f32[1,1,2,256,256]{4,3,2,1,0:T(8,128)S(1)} %maximum_add_fusion.4), channel_id=1, source_target_pairs={{96,0},{192,96},{288,192},{384,288},{480,384},{576,480},{672,576},... | collective-permute-start | bytes 1572872 | tf_op jit(solution)/shard_map/while/body/eval_jaxpr/ppermute | solution.py:10
  93.7 9.2 %collective-permute-done = f32[1,1,2,256,256]{4,3,2,1,0:T(8,128)S(1)} collective-permute-done((f32[1,1,2,256,256]{4,3,2,1,0:T(8,128)S(1)}, f32[1,1,2,256,256]{4,3,2,1,0:T(8,128)S(1)}, u32[]{:S(2)}, u32[]{:S(2)}) %collective-permute-start) | collective-permute-done | bytes 524320 | tf_op jit(solution)/shard_map/while/body/eval_jaxpr/ppermute | solution.py:10
  102.9 2.2 %fusion.26 = f32[512,256]{1,0:T(8,128)S(1)} fusion(f32[512,256]{1,0:T(8,128)S(1)} %bitcast.124, f32[256,256]{0,1:T(8,128)} %copy-done.4, f32[256,256]{0,1:T(8,128)} %copy-done.3, f32[256,256]{0,1:T(8,128)} %copy-done.2), kind=kOutput, calls=%fused_computation.57 | convolution fusion | flops 403439616 | bytes 1835008 | tf_op jit(solution)/shard_map/dot_general | solution.py:89
  107.0 9.5 %all-to-all-start = ((bf16[16,2,16,256]{3,2,1,0:T(8,128)(2,1)}), bf16[16,2,16,256]{3,2,1,0:T(8,128)(2,1)S(1)}, u32[]{:S(2)}, u32[]{:S(2)}) async-start(bf16[16,2,16,256]{3,2,1,0:T(8,128)(2,1)} %maximum_bitcast_fusion), calls=%async_computation | async-start | bytes 524288 | tf_op jit(solution)/shard_map/all_to_all | solution.py:43
  116.6 17.5 %collective-permute-start.2 = (bf16[2,256,256]{2,1,0:T(8,128)(2,1)S(1)}, bf16[2,256,256]{2,1,0:T(8,128)(2,1)S(1)}, u32[]{:S(2)}, u32[]{:S(2)}) collective-permute-start(bf16[2,256,256]{2,1,0:T(8,128)(2,1)S(1)} %pad_maximum_fusion.2), channel_id=1, source_target_pairs={{0,1},{1,2},{2,3},{3,4},{4,5},{6,7},{7,8},{8,9},{9,10},{10,11},{12... | collective-permute-start | bytes 786440 | tf_op jit(solution)/shard_map/ppermute | solution.py:10
  134.1 1.9 %collective-permute-start.3 = (bf16[2,256,256]{2,1,0:T(8,128)(2,1)S(1)}, bf16[2,256,256]{2,1,0:T(8,128)(2,1)S(1)}, u32[]{:S(2)}, u32[]{:S(2)}) collective-permute-start(bf16[2,256,256]{2,1,0:T(8,128)(2,1)S(1)} %pad_maximum_fusion.2), channel_id=1, source_target_pairs={{1,0},{2,1},{3,2},{4,3},{5,4},{7,6},{8,7},{9,8},{10,9},{11,10},{13... | collective-permute-start | bytes 786440 | tf_op jit(solution)/shard_map/ppermute | solution.py:10
  137.4 11.0 %collective-permute-done.3 = bf16[2,256,256]{2,1,0:T(8,128)(2,1)S(1)} collective-permute-done((bf16[2,256,256]{2,1,0:T(8,128)(2,1)S(1)}, bf16[2,256,256]{2,1,0:T(8,128)(2,1)S(1)}, u32[]{:S(2)}, u32[]{:S(2)}) %collective-permute-start.3) | collective-permute-done | bytes 262176 | tf_op jit(solution)/shard_map/ppermute | solution.py:10
  149.3 10.5 %all-to-all-start.1 = ((bf16[16,2,2,16,256]{4,3,2,1,0:T(8,128)(2,1)}), bf16[16,2,2,16,256]{4,3,2,1,0:T(8,128)(2,1)S(1)}, u32[]{:S(2)}, u32[]{:S(2)}) async-start(bf16[16,2,2,16,256]{4,3,2,1,0:T(8,128)(2,1)} %copy_bitcast_fusion), calls=%async_computation.1 | async-start | bytes 1048576 | tf_op jit(solution)/shard_map/all_to_all | solution.py:45
  161.9 9.1 %all-to-all-done.1 = bf16[16,2,2,16,256]{4,3,2,1,0:T(8,128)(2,1)S(1)} async-done(((bf16[16,2,2,16,256]{4,3,2,1,0:T(8,128)(2,1)}), bf16[16,2,2,16,256]{4,3,2,1,0:T(8,128)(2,1)S(1)}, u32[]{:S(2)}, u32[]{:S(2)}) %all-to-all-start.1) | async-done | bytes 524320 | tf_op jit(solution)/shard_map/all_to_all | solution.py:45
  172.7 3.5 %all-to-all-start.2 = ((bf16[16,2,16,256]{3,2,1,0:T(8,128)(2,1)}), bf16[16,2,16,256]{3,2,1,0:T(8,128)(2,1)S(1)}, u32[]{:S(2)}, u32[]{:S(2)}) async-start(bf16[16,2,16,256]{3,2,1,0:T(8,128)(2,1)} %bitcast.55), calls=%async_computation.2 | async-start | bytes 524288 | tf_op jit(solution)/shard_map/all_to_all | solution.py:57
  177.1 7.9 %all-to-all-done.2 = bf16[16,2,16,256]{3,2,1,0:T(8,128)(2,1)S(1)} async-done(((bf16[16,2,16,256]{3,2,1,0:T(8,128)(2,1)}), bf16[16,2,16,256]{3,2,1,0:T(8,128)(2,1)S(1)}, u32[]{:S(2)}, u32[]{:S(2)}) %all-to-all-start.2) | async-done | bytes 262176 | tf_op jit(solution)/shard_map/all_to_all | solution.py:57
  (75 shorter events, 22.5 us)
Async XLA Ops:
  0.6 2.3 %copy-start.7 = (s32[1,8,3]{1,0,2:T(1,128)S(1)}, s32[1,8,3]{1,0,2:T(1,128)}, u32[]{:S(2)}) copy-start(s32[1,8,3]{1,0,2:T(1,128)} %param.10) | copy-start | bytes 292
  0.6 2.4 %copy-start.5 = (f32[1,256,256]{2,1,0:T(8,128)S(1)}, f32[1,256,256]{2,1,0:T(8,128)}, u32[]{:S(2)}) copy-start(f32[1,256,256]{2,1,0:T(8,128)} %param.9) | copy-start | bytes 786436
  0.6 16.3 %collective-permute-start.1 = (f32[1,1,2,256,256]{4,3,2,1,0:T(8,128)}, f32[1,1,2,256,256]{4,3,2,1,0:T(8,128)S(1)}, u32[]{:S(2)}, u32[]{:S(2)}) collective-permute-start(f32[1,1,2,256,256]{4,3,2,1,0:T(8,128)} %bitcast.122), channel_id=1, source_target_pairs={{96,0},{192,96},{288,192},{384,288},{480,384},{576,480},{672,576},... | collective-permute-start | bytes 1572872 | tf_op jit(solution)/shard_map/ppermute | solution.py:10
  3.0 1.0 copy-start
  5.1 0.8 copy-start.2
  5.9 0.7 copy-start.3
  5.9 0.8 copy-start.4
  18.3 15.1 %collective-permute-start = (f32[1,1,2,256,256]{4,3,2,1,0:T(8,128)S(1)}, f32[1,1,2,256,256]{4,3,2,1,0:T(8,128)S(1)}, u32[]{:S(2)}, u32[]{:S(2)}) collective-permute-start(f32[1,1,2,256,256]{4,3,2,1,0:T(8,128)S(1)} %maximum_add_fusion.4), channel_id=1, source_target_pairs={{96,0},{192,96},{288,192},{384,288},{480,384},{576,480},{672,576},... | collective-permute-start | bytes 1572872 | tf_op jit(solution)/shard_map/while/body/eval_jaxpr/ppermute | solution.py:10
  34.7 14.2 %collective-permute-start = (f32[1,1,2,256,256]{4,3,2,1,0:T(8,128)S(1)}, f32[1,1,2,256,256]{4,3,2,1,0:T(8,128)S(1)}, u32[]{:S(2)}, u32[]{:S(2)}) collective-permute-start(f32[1,1,2,256,256]{4,3,2,1,0:T(8,128)S(1)} %maximum_add_fusion.4), channel_id=1, source_target_pairs={{96,0},{192,96},{288,192},{384,288},{480,384},{576,480},{672,576},... | collective-permute-start | bytes 1572872 | tf_op jit(solution)/shard_map/while/body/eval_jaxpr/ppermute | solution.py:10
  50.2 13.3 %collective-permute-start = (f32[1,1,2,256,256]{4,3,2,1,0:T(8,128)S(1)}, f32[1,1,2,256,256]{4,3,2,1,0:T(8,128)S(1)}, u32[]{:S(2)}, u32[]{:S(2)}) collective-permute-start(f32[1,1,2,256,256]{4,3,2,1,0:T(8,128)S(1)} %maximum_add_fusion.4), channel_id=1, source_target_pairs={{96,0},{192,96},{288,192},{384,288},{480,384},{576,480},{672,576},... | collective-permute-start | bytes 1572872 | tf_op jit(solution)/shard_map/while/body/eval_jaxpr/ppermute | solution.py:10
  64.9 12.5 %collective-permute-start = (f32[1,1,2,256,256]{4,3,2,1,0:T(8,128)S(1)}, f32[1,1,2,256,256]{4,3,2,1,0:T(8,128)S(1)}, u32[]{:S(2)}, u32[]{:S(2)}) collective-permute-start(f32[1,1,2,256,256]{4,3,2,1,0:T(8,128)S(1)} %maximum_add_fusion.4), channel_id=1, source_target_pairs={{96,0},{192,96},{288,192},{384,288},{480,384},{576,480},{672,576},... | collective-permute-start | bytes 1572872 | tf_op jit(solution)/shard_map/while/body/eval_jaxpr/ppermute | solution.py:10
  78.7 11.6 %collective-permute-start = (f32[1,1,2,256,256]{4,3,2,1,0:T(8,128)S(1)}, f32[1,1,2,256,256]{4,3,2,1,0:T(8,128)S(1)}, u32[]{:S(2)}, u32[]{:S(2)}) collective-permute-start(f32[1,1,2,256,256]{4,3,2,1,0:T(8,128)S(1)} %maximum_add_fusion.4), channel_id=1, source_target_pairs={{96,0},{192,96},{288,192},{384,288},{480,384},{576,480},{672,576},... | collective-permute-start | bytes 1572872 | tf_op jit(solution)/shard_map/while/body/eval_jaxpr/ppermute | solution.py:10
  91.7 11.1 %collective-permute-start = (f32[1,1,2,256,256]{4,3,2,1,0:T(8,128)S(1)}, f32[1,1,2,256,256]{4,3,2,1,0:T(8,128)S(1)}, u32[]{:S(2)}, u32[]{:S(2)}) collective-permute-start(f32[1,1,2,256,256]{4,3,2,1,0:T(8,128)S(1)} %maximum_add_fusion.4), channel_id=1, source_target_pairs={{96,0},{192,96},{288,192},{384,288},{480,384},{576,480},{672,576},... | collective-permute-start | bytes 1572872 | tf_op jit(solution)/shard_map/while/body/eval_jaxpr/ppermute | solution.py:10
  102.9 2.2 %copy-start.1 = (f32[256,256]{1,0:T(8,128)S(1)}, f32[256,256]{1,0:T(8,128)}, u32[]{:S(2)}) copy-start(f32[256,256]{1,0:T(8,128)} %get-tuple-element.71) | copy-start | bytes 786436
  107.0 42.3 %all-to-all-start = ((bf16[16,2,16,256]{3,2,1,0:T(8,128)(2,1)}), bf16[16,2,16,256]{3,2,1,0:T(8,128)(2,1)S(1)}, u32[]{:S(2)}, u32[]{:S(2)}) async-start(bf16[16,2,16,256]{3,2,1,0:T(8,128)(2,1)} %maximum_bitcast_fusion), calls=%async_computation | async-start | bytes 524288 | tf_op jit(solution)/shard_map/all_to_all | solution.py:43
  116.6 20.8 %collective-permute-start.2 = (bf16[2,256,256]{2,1,0:T(8,128)(2,1)S(1)}, bf16[2,256,256]{2,1,0:T(8,128)(2,1)S(1)}, u32[]{:S(2)}, u32[]{:S(2)}) collective-permute-start(bf16[2,256,256]{2,1,0:T(8,128)(2,1)S(1)} %pad_maximum_fusion.2), channel_id=1, source_target_pairs={{0,1},{1,2},{2,3},{3,4},{4,5},{6,7},{7,8},{8,9},{9,10},{10,11},{12... | collective-permute-start | bytes 786440 | tf_op jit(solution)/shard_map/ppermute | solution.py:10
  134.1 14.4 %collective-permute-start.3 = (bf16[2,256,256]{2,1,0:T(8,128)(2,1)S(1)}, bf16[2,256,256]{2,1,0:T(8,128)(2,1)S(1)}, u32[]{:S(2)}, u32[]{:S(2)}) collective-permute-start(bf16[2,256,256]{2,1,0:T(8,128)(2,1)S(1)} %pad_maximum_fusion.2), channel_id=1, source_target_pairs={{1,0},{2,1},{3,2},{4,3},{5,4},{7,6},{8,7},{9,8},{10,9},{11,10},{13... | collective-permute-start | bytes 786440 | tf_op jit(solution)/shard_map/ppermute | solution.py:10
  149.3 21.6 %all-to-all-start.1 = ((bf16[16,2,2,16,256]{4,3,2,1,0:T(8,128)(2,1)}), bf16[16,2,2,16,256]{4,3,2,1,0:T(8,128)(2,1)S(1)}, u32[]{:S(2)}, u32[]{:S(2)}) async-start(bf16[16,2,2,16,256]{4,3,2,1,0:T(8,128)(2,1)} %copy_bitcast_fusion), calls=%async_computation.1 | async-start | bytes 1048576 | tf_op jit(solution)/shard_map/all_to_all | solution.py:45
  159.8 0.7 copy-start.8
  160.6 0.7 copy-start.6
  172.7 12.3 %all-to-all-start.2 = ((bf16[16,2,16,256]{3,2,1,0:T(8,128)(2,1)}), bf16[16,2,16,256]{3,2,1,0:T(8,128)(2,1)S(1)}, u32[]{:S(2)}, u32[]{:S(2)}) async-start(bf16[16,2,16,256]{3,2,1,0:T(8,128)(2,1)} %bitcast.55), calls=%async_computation.2 | async-start | bytes 524288 | tf_op jit(solution)/shard_map/all_to_all | solution.py:57

commit v5 on v3

--- a/solution.py
+++ b/solution.py
@@ -39,10 +39,14 @@
     rows = width // moms
     chunks = lesser.reshape(2, moms, rows, width).transpose(1, 0, 2, 3)
     held = lax.all_to_all(chunks, "kmom", 0, 0)
-    below = passed_along(held, "energy", 1)
-    above = passed_along(held, "energy", -1)
+    count = lax.axis_size("energy")
+    within = [(i, i ^ 1) for i in range(count) if (i ^ 1) < count]
+    across = [(i, i + 1 if i % 2 else i - 1) for i in range(count)]
+    across = [(i, j) for i, j in across if 0 <= j < count]
+    beside = lax.ppermute(held, "energy", within)
+    facing = lax.ppermute(held, "energy", across)
     flat = held.reshape(moms, -1).astype(jnp.float32)
-    near = below.reshape(moms, -1).astype(jnp.float32) + above.reshape(moms, -1).astype(jnp.float32)
+    near = beside.reshape(moms, -1).astype(jnp.float32) + facing.reshape(moms, -1).astype(jnp.float32)
     still = phonon_mode[0] == 0
     weight_still = jnp.where(still, phonon_weight[0], phonon_weight[1])
     weight_moved = jnp.where(still, phonon_weight[1], phonon_weight[0])
@@ -77,6 +81,7 @@
         axis=0,
     )
     right_block = jnp.concatenate([map_real.T, map_imag.T], axis=1)
+    left_block, right_block = lax.optimization_barrier((left_block, right_block))
     width = block_width
     high = lax.Precision.HIGH
 

time: 179 us -> 173 us (0.966)
  waiting for transfers between devices: 106 us -> 101 us
    ppermute x9 -> x7, starting transfers between devices: 34.3 us -> 13.7 us  [passed_along(): return lax.ppermute(shard, axis, pairs)]
    ppermute x0 -> x2, starting transfers between devices: none -> 20.6 us  [the longest x1 10.3 us: self_energy_of(): beside = lax.ppermute(held, 'energy', within)]
    ppermute x9 -> x7, waiting for transfers between devices: 90.2 us -> 74.6 us  [passed_along(): return lax.ppermute(shard, axis, pairs)]
    ppermute x0 -> x2, waiting for transfers between devices: none -> 10.1 us  [the longest x1 10.1 us: self_energy_of(): facing = lax.ppermute(held, 'energy', across)]
    unnamed x23 -> x15, local copies, waits for them, and re-layouts: 4.31 us -> 3.52 us
  transfers between devices with their start and end apart: 11 -> 11, of which waited for: 11 -> 10; matrix products, arithmetic and copies ran while one was open for 3% -> 3% of each run, Pallas kernels for 0% -> 0%
where the time goes in v5:
time: 173 us; the launch traced here: 172 us
  waiting for transfers between devices  101 us (58%)
  starting transfers between devices  47.3 us (27%)
  matrix products  12.1 us (7%)
  local copies, waits for them, and re-layouts  6.06 us (4%)
  other arithmetic  4.06 us (2%)
    ppermute x7, waiting for transfers between devices, passed_along(): return lax.ppermute(shard, axis, pairs)  74.6 us
    ppermute x7, starting transfers between devices, passed_along(): return lax.ppermute(shard, axis, pairs)  13.7 us
    ppermute x1, starting transfers between devices, self_energy_of(): beside = lax.ppermute(held, 'energy', within)  10.3 us
    ppermute x1, starting transfers between devices, self_energy_of(): facing = lax.ppermute(held, 'energy', across)  10.3 us
    ppermute x1, waiting for transfers between devices, self_energy_of(): facing = lax.ppermute(held, 'energy', across)  10.1 us
    all_to_all x1, starting transfers between devices, self_energy_of(): held = lax.all_to_all(chunks, 'kmom', 0, 0)  9.51 us
    all_to_all x1, waiting for transfers between devices, self_energy_of(): held = lax.all_to_all(chunks, 'kmom', 0, 0)  8.13 us
    all_to_all x1, waiting for transfers between devices, self_energy_of(): back = lax.all_to_all(out, 'kmom', 0, 0)  7.93 us
  transfers between devices with their start and end apart: 11, of which 10 were waited for; matrix products, arithmetic and copies ran while one was open for 3% of the time, Pallas kernels for 0%

profile of v5, /device:TPU:25, one launch (start us, length us, event | category | flops | bytes accessed | tf_op | source)
XLA Modules:
  0.0 172.2 jit_solution(11093511870030014055)
XLA Ops:
  0.6 2.2 %collective-permute-start.1 = (f32[1,1,2,256,256]{4,3,2,1,0:T(8,128)}, f32[1,1,2,256,256]{4,3,2,1,0:T(8,128)S(1)}, u32[]{:S(2)}, u32[]{:S(2)}) collective-permute-start(f32[1,1,2,256,256]{4,3,2,1,0:T(8,128)} %bitcast.118), channel_id=1, source_target_pairs={{96,0},{192,96},{288,192},{384,288},{480,384},{576,480},{672,576},... | collective-permute-start | bytes 1572872 | tf_op jit(solution)/shard_map/ppermute | solution.py:10
  6.4 1.6 copy.25
  8.6 8.3 %collective-permute-done.1 = f32[1,1,2,256,256]{4,3,2,1,0:T(8,128)S(1)} collective-permute-done((f32[1,1,2,256,256]{4,3,2,1,0:T(8,128)}, f32[1,1,2,256,256]{4,3,2,1,0:T(8,128)S(1)}, u32[]{:S(2)}, u32[]{:S(2)}) %collective-permute-start.1) | collective-permute-done | bytes 524320 | tf_op jit(solution)/shard_map/ppermute | solution.py:10
  16.9 85.9 %while.10 = (s32[]{:T(128)}, f32[1,1,2,256,256]{4,3,2,1,0:T(8,128)S(1)}, f32[1,1,1,2,256,256]{5,4,3,2,1,0:T(8,128)S(1)}, f32[512,512]{1,0:T(8,128)S(1)}, f32[256,512]{1,0:T(8,128)S(1)}, /*index=5*/s32[]{:T(128)}) while((s32[]{:T(128)}, f32[1,1,2,256,256]{4,3,2,1,0:T(8,128)S(1)}, f32[1,1,1,2,256,256]{5,4,3,2,1,0:T(8,128)S(1)}, ...), condition=%wide.region_2.3_spmd, body=%wide.region_1.2_spmd.sunk | while | flops 805699584 | bytes 9437293 | solution.py:100
  18.3 1.9 %collective-permute-start = (f32[1,1,2,256,256]{4,3,2,1,0:T(8,128)S(1)}, f32[1,1,2,256,256]{4,3,2,1,0:T(8,128)S(1)}, u32[]{:S(2)}, u32[]{:S(2)}) collective-permute-start(f32[1,1,2,256,256]{4,3,2,1,0:T(8,128)S(1)} %maximum_add_fusion.4), channel_id=1, source_target_pairs={{96,0},{192,96},{288,192},{384,288},{480,384},{576,480},{672,576},... | collective-permute-start | bytes 1572872 | tf_op jit(solution)/shard_map/while/body/eval_jaxpr/ppermute | solution.py:10
  20.2 13.1 %collective-permute-done = f32[1,1,2,256,256]{4,3,2,1,0:T(8,128)S(1)} collective-permute-done((f32[1,1,2,256,256]{4,3,2,1,0:T(8,128)S(1)}, f32[1,1,2,256,256]{4,3,2,1,0:T(8,128)S(1)}, u32[]{:S(2)}, u32[]{:S(2)}) %collective-permute-start) | collective-permute-done | bytes 524320 | tf_op jit(solution)/shard_map/while/body/eval_jaxpr/ppermute | solution.py:10
  34.7 1.9 %collective-permute-start = (f32[1,1,2,256,256]{4,3,2,1,0:T(8,128)S(1)}, f32[1,1,2,256,256]{4,3,2,1,0:T(8,128)S(1)}, u32[]{:S(2)}, u32[]{:S(2)}) collective-permute-start(f32[1,1,2,256,256]{4,3,2,1,0:T(8,128)S(1)} %maximum_add_fusion.4), channel_id=1, source_target_pairs={{96,0},{192,96},{288,192},{384,288},{480,384},{576,480},{672,576},... | collective-permute-start | bytes 1572872 | tf_op jit(solution)/shard_map/while/body/eval_jaxpr/ppermute | solution.py:10
  36.6 12.3 %collective-permute-done = f32[1,1,2,256,256]{4,3,2,1,0:T(8,128)S(1)} collective-permute-done((f32[1,1,2,256,256]{4,3,2,1,0:T(8,128)S(1)}, f32[1,1,2,256,256]{4,3,2,1,0:T(8,128)S(1)}, u32[]{:S(2)}, u32[]{:S(2)}) %collective-permute-start) | collective-permute-done | bytes 524320 | tf_op jit(solution)/shard_map/while/body/eval_jaxpr/ppermute | solution.py:10
  50.2 1.9 %collective-permute-start = (f32[1,1,2,256,256]{4,3,2,1,0:T(8,128)S(1)}, f32[1,1,2,256,256]{4,3,2,1,0:T(8,128)S(1)}, u32[]{:S(2)}, u32[]{:S(2)}) collective-permute-start(f32[1,1,2,256,256]{4,3,2,1,0:T(8,128)S(1)} %maximum_add_fusion.4), channel_id=1, source_target_pairs={{96,0},{192,96},{288,192},{384,288},{480,384},{576,480},{672,576},... | collective-permute-start | bytes 1572872 | tf_op jit(solution)/shard_map/while/body/eval_jaxpr/ppermute | solution.py:10
  52.1 11.4 %collective-permute-done = f32[1,1,2,256,256]{4,3,2,1,0:T(8,128)S(1)} collective-permute-done((f32[1,1,2,256,256]{4,3,2,1,0:T(8,128)S(1)}, f32[1,1,2,256,256]{4,3,2,1,0:T(8,128)S(1)}, u32[]{:S(2)}, u32[]{:S(2)}) %collective-permute-start) | collective-permute-done | bytes 524320 | tf_op jit(solution)/shard_map/while/body/eval_jaxpr/ppermute | solution.py:10
  64.9 1.9 %collective-permute-start = (f32[1,1,2,256,256]{4,3,2,1,0:T(8,128)S(1)}, f32[1,1,2,256,256]{4,3,2,1,0:T(8,128)S(1)}, u32[]{:S(2)}, u32[]{:S(2)}) collective-permute-start(f32[1,1,2,256,256]{4,3,2,1,0:T(8,128)S(1)} %maximum_add_fusion.4), channel_id=1, source_target_pairs={{96,0},{192,96},{288,192},{384,288},{480,384},{576,480},{672,576},... | collective-permute-start | bytes 1572872 | tf_op jit(solution)/shard_map/while/body/eval_jaxpr/ppermute | solution.py:10
  66.8 10.6 %collective-permute-done = f32[1,1,2,256,256]{4,3,2,1,0:T(8,128)S(1)} collective-permute-done((f32[1,1,2,256,256]{4,3,2,1,0:T(8,128)S(1)}, f32[1,1,2,256,256]{4,3,2,1,0:T(8,128)S(1)}, u32[]{:S(2)}, u32[]{:S(2)}) %collective-permute-start) | collective-permute-done | bytes 524320 | tf_op jit(solution)/shard_map/while/body/eval_jaxpr/ppermute | solution.py:10
  78.7 1.9 %collective-permute-start = (f32[1,1,2,256,256]{4,3,2,1,0:T(8,128)S(1)}, f32[1,1,2,256,256]{4,3,2,1,0:T(8,128)S(1)}, u32[]{:S(2)}, u32[]{:S(2)}) collective-permute-start(f32[1,1,2,256,256]{4,3,2,1,0:T(8,128)S(1)} %maximum_add_fusion.4), channel_id=1, source_target_pairs={{96,0},{192,96},{288,192},{384,288},{480,384},{576,480},{672,576},... | collective-permute-start | bytes 1572872 | tf_op jit(solution)/shard_map/while/body/eval_jaxpr/ppermute | solution.py:10
  80.7 9.7 %collective-permute-done = f32[1,1,2,256,256]{4,3,2,1,0:T(8,128)S(1)} collective-permute-done((f32[1,1,2,256,256]{4,3,2,1,0:T(8,128)S(1)}, f32[1,1,2,256,256]{4,3,2,1,0:T(8,128)S(1)}, u32[]{:S(2)}, u32[]{:S(2)}) %collective-permute-start) | collective-permute-done | bytes 524320 | tf_op jit(solution)/shard_map/while/body/eval_jaxpr/ppermute | solution.py:10
  91.7 1.9 %collective-permute-start = (f32[1,1,2,256,256]{4,3,2,1,0:T(8,128)S(1)}, f32[1,1,2,256,256]{4,3,2,1,0:T(8,128)S(1)}, u32[]{:S(2)}, u32[]{:S(2)}) collective-permute-start(f32[1,1,2,256,256]{4,3,2,1,0:T(8,128)S(1)} %maximum_add_fusion.4), channel_id=1, source_target_pairs={{96,0},{192,96},{288,192},{384,288},{480,384},{576,480},{672,576},... | collective-permute-start | bytes 1572872 | tf_op jit(solution)/shard_map/while/body/eval_jaxpr/ppermute | solution.py:10
  93.7 9.2 %collective-permute-done = f32[1,1,2,256,256]{4,3,2,1,0:T(8,128)S(1)} collective-permute-done((f32[1,1,2,256,256]{4,3,2,1,0:T(8,128)S(1)}, f32[1,1,2,256,256]{4,3,2,1,0:T(8,128)S(1)}, u32[]{:S(2)}, u32[]{:S(2)}) %collective-permute-start) | collective-permute-done | bytes 524320 | tf_op jit(solution)/shard_map/while/body/eval_jaxpr/ppermute | solution.py:10
  102.9 2.2 %fusion.28 = f32[512,256]{1,0:T(8,128)S(1)} fusion(f32[512,512]{0,1:T(8,128)} %maximum_maximum_fusion, f32[512,256]{1,0:T(8,128)S(1)} %bitcast.120), kind=kOutput, calls=%fused_computation.56 | convolution fusion | flops 402653184 | bytes 2097152 | tf_op jit(solution)/shard_map/dot_general | solution.py:90
  107.0 9.5 %all-to-all-start = ((bf16[16,2,16,256]{3,2,1,0:T(8,128)(2,1)}), bf16[16,2,16,256]{3,2,1,0:T(8,128)(2,1)S(1)}, u32[]{:S(2)}, u32[]{:S(2)}) async-start(bf16[16,2,16,256]{3,2,1,0:T(8,128)(2,1)} %maximum_bitcast_fusion), calls=%async_computation | async-start | bytes 524288 | tf_op jit(solution)/shard_map/all_to_all | solution.py:41
  117.2 8.1 %all-to-all-done = bf16[16,2,16,256]{3,2,1,0:T(8,128)(2,1)S(1)} async-done(((bf16[16,2,16,256]{3,2,1,0:T(8,128)(2,1)}), bf16[16,2,16,256]{3,2,1,0:T(8,128)(2,1)S(1)}, u32[]{:S(2)}, u32[]{:S(2)}) %all-to-all-start) | async-done | bytes 262176 | tf_op jit(solution)/shard_map/all_to_all | solution.py:41
  125.3 10.3 %collective-permute-start.2 = (bf16[16,2,16,256]{3,2,1,0:T(8,128)(2,1)S(1)}, bf16[16,2,16,256]{3,2,1,0:T(8,128)(2,1)S(1)}, u32[]{:S(2)}, u32[]{:S(2)}) collective-permute-start(bf16[16,2,16,256]{3,2,1,0:T(8,128)(2,1)S(1)} %all-to-all-done), channel_id=1, source_target_pairs={{0,1},{1,0},{2,3},{3,2},{4,5},{5,4},{6,7},{7,6},{8,9},{9,8},{10,11... | collective-permute-start | bytes 786440 | tf_op jit(solution)/shard_map/ppermute | solution.py:46
  135.7 10.3 %collective-permute-start.3 = (bf16[16,2,16,256]{3,2,1,0:T(8,128)(2,1)S(1)}, bf16[16,2,16,256]{3,2,1,0:T(8,128)(2,1)S(1)}, u32[]{:S(2)}, u32[]{:S(2)}) collective-permute-start(bf16[16,2,16,256]{3,2,1,0:T(8,128)(2,1)S(1)} %all-to-all-done), channel_id=1, source_target_pairs={{1,2},{2,1},{3,4},{4,3},{7,8},{8,7},{9,10},{10,9},{13,14},{14,13},... | collective-permute-start | bytes 786440 | tf_op jit(solution)/shard_map/ppermute | solution.py:47
  147.3 10.1 %collective-permute-done.3 = bf16[16,2,16,256]{3,2,1,0:T(8,128)(2,1)S(1)} collective-permute-done((bf16[16,2,16,256]{3,2,1,0:T(8,128)(2,1)S(1)}, bf16[16,2,16,256]{3,2,1,0:T(8,128)(2,1)S(1)}, u32[]{:S(2)}, u32[]{:S(2)}) %collective-permute-start.3) | collective-permute-done | bytes 262176 | tf_op jit(solution)/shard_map/ppermute | solution.py:47
  159.1 3.5 %all-to-all-start.1 = ((bf16[16,2,16,256]{3,2,1,0:T(8,128)(2,1)}), bf16[16,2,16,256]{3,2,1,0:T(8,128)(2,1)S(1)}, u32[]{:S(2)}, u32[]{:S(2)}) async-start(bf16[16,2,16,256]{3,2,1,0:T(8,128)(2,1)} %bitcast.50), calls=%async_computation.1 | async-start | bytes 524288 | tf_op jit(solution)/shard_map/all_to_all | solution.py:57
  163.5 7.9 %all-to-all-done.1 = bf16[16,2,16,256]{3,2,1,0:T(8,128)(2,1)S(1)} async-done(((bf16[16,2,16,256]{3,2,1,0:T(8,128)(2,1)}), bf16[16,2,16,256]{3,2,1,0:T(8,128)(2,1)S(1)}, u32[]{:S(2)}, u32[]{:S(2)}) %all-to-all-start.1) | async-done | bytes 262176 | tf_op jit(solution)/shard_map/all_to_all | solution.py:57
  (63 shorter events, 18.4 us)
Async XLA Ops:
  0.6 2.3 %copy-start.3 = (s32[1,8,3]{1,0,2:T(1,128)S(1)}, s32[1,8,3]{1,0,2:T(1,128)}, u32[]{:S(2)}) copy-start(s32[1,8,3]{1,0,2:T(1,128)} %param.10) | copy-start | bytes 292
  0.6 2.4 %copy-start.1 = (f32[1,256,256]{2,1,0:T(8,128)S(1)}, f32[1,256,256]{2,1,0:T(8,128)}, u32[]{:S(2)}) copy-start(f32[1,256,256]{2,1,0:T(8,128)} %param.9) | copy-start | bytes 786436
  0.6 16.3 %collective-permute-start.1 = (f32[1,1,2,256,256]{4,3,2,1,0:T(8,128)}, f32[1,1,2,256,256]{4,3,2,1,0:T(8,128)S(1)}, u32[]{:S(2)}, u32[]{:S(2)}) collective-permute-start(f32[1,1,2,256,256]{4,3,2,1,0:T(8,128)} %bitcast.118), channel_id=1, source_target_pairs={{96,0},{192,96},{288,192},{384,288},{480,384},{576,480},{672,576},... | collective-permute-start | bytes 1572872 | tf_op jit(solution)/shard_map/ppermute | solution.py:10
  3.0 1.0 copy-start
  18.3 15.1 %collective-permute-start = (f32[1,1,2,256,256]{4,3,2,1,0:T(8,128)S(1)}, f32[1,1,2,256,256]{4,3,2,1,0:T(8,128)S(1)}, u32[]{:S(2)}, u32[]{:S(2)}) collective-permute-start(f32[1,1,2,256,256]{4,3,2,1,0:T(8,128)S(1)} %maximum_add_fusion.4), channel_id=1, source_target_pairs={{96,0},{192,96},{288,192},{384,288},{480,384},{576,480},{672,576},... | collective-permute-start | bytes 1572872 | tf_op jit(solution)/shard_map/while/body/eval_jaxpr/ppermute | solution.py:10
  34.7 14.2 %collective-permute-start = (f32[1,1,2,256,256]{4,3,2,1,0:T(8,128)S(1)}, f32[1,1,2,256,256]{4,3,2,1,0:T(8,128)S(1)}, u32[]{:S(2)}, u32[]{:S(2)}) collective-permute-start(f32[1,1,2,256,256]{4,3,2,1,0:T(8,128)S(1)} %maximum_add_fusion.4), channel_id=1, source_target_pairs={{96,0},{192,96},{288,192},{384,288},{480,384},{576,480},{672,576},... | collective-permute-start | bytes 1572872 | tf_op jit(solution)/shard_map/while/body/eval_jaxpr/ppermute | solution.py:10
  50.2 13.3 %collective-permute-start = (f32[1,1,2,256,256]{4,3,2,1,0:T(8,128)S(1)}, f32[1,1,2,256,256]{4,3,2,1,0:T(8,128)S(1)}, u32[]{:S(2)}, u32[]{:S(2)}) collective-permute-start(f32[1,1,2,256,256]{4,3,2,1,0:T(8,128)S(1)} %maximum_add_fusion.4), channel_id=1, source_target_pairs={{96,0},{192,96},{288,192},{384,288},{480,384},{576,480},{672,576},... | collective-permute-start | bytes 1572872 | tf_op jit(solution)/shard_map/while/body/eval_jaxpr/ppermute | solution.py:10
  64.9 12.5 %collective-permute-start = (f32[1,1,2,256,256]{4,3,2,1,0:T(8,128)S(1)}, f32[1,1,2,256,256]{4,3,2,1,0:T(8,128)S(1)}, u32[]{:S(2)}, u32[]{:S(2)}) collective-permute-start(f32[1,1,2,256,256]{4,3,2,1,0:T(8,128)S(1)} %maximum_add_fusion.4), channel_id=1, source_target_pairs={{96,0},{192,96},{288,192},{384,288},{480,384},{576,480},{672,576},... | collective-permute-start | bytes 1572872 | tf_op jit(solution)/shard_map/while/body/eval_jaxpr/ppermute | solution.py:10
  78.7 11.6 %collective-permute-start = (f32[1,1,2,256,256]{4,3,2,1,0:T(8,128)S(1)}, f32[1,1,2,256,256]{4,3,2,1,0:T(8,128)S(1)}, u32[]{:S(2)}, u32[]{:S(2)}) collective-permute-start(f32[1,1,2,256,256]{4,3,2,1,0:T(8,128)S(1)} %maximum_add_fusion.4), channel_id=1, source_target_pairs={{96,0},{192,96},{288,192},{384,288},{480,384},{576,480},{672,576},... | collective-permute-start | bytes 1572872 | tf_op jit(solution)/shard_map/while/body/eval_jaxpr/ppermute | solution.py:10
  91.7 11.1 %collective-permute-start = (f32[1,1,2,256,256]{4,3,2,1,0:T(8,128)S(1)}, f32[1,1,2,256,256]{4,3,2,1,0:T(8,128)S(1)}, u32[]{:S(2)}, u32[]{:S(2)}) collective-permute-start(f32[1,1,2,256,256]{4,3,2,1,0:T(8,128)S(1)} %maximum_add_fusion.4), channel_id=1, source_target_pairs={{96,0},{192,96},{288,192},{384,288},{480,384},{576,480},{672,576},... | collective-permute-start | bytes 1572872 | tf_op jit(solution)/shard_map/while/body/eval_jaxpr/ppermute | solution.py:10
  107.0 18.4 %all-to-all-start = ((bf16[16,2,16,256]{3,2,1,0:T(8,128)(2,1)}), bf16[16,2,16,256]{3,2,1,0:T(8,128)(2,1)S(1)}, u32[]{:S(2)}, u32[]{:S(2)}) async-start(bf16[16,2,16,256]{3,2,1,0:T(8,128)(2,1)} %maximum_bitcast_fusion), calls=%async_computation | async-start | bytes 524288 | tf_op jit(solution)/shard_map/all_to_all | solution.py:41
  116.5 0.7 copy-start.4
  125.3 21.9 %collective-permute-start.2 = (bf16[16,2,16,256]{3,2,1,0:T(8,128)(2,1)S(1)}, bf16[16,2,16,256]{3,2,1,0:T(8,128)(2,1)S(1)}, u32[]{:S(2)}, u32[]{:S(2)}) collective-permute-start(bf16[16,2,16,256]{3,2,1,0:T(8,128)(2,1)S(1)} %all-to-all-done), channel_id=1, source_target_pairs={{0,1},{1,0},{2,3},{3,2},{4,5},{5,4},{6,7},{7,6},{8,9},{9,8},{10,11... | collective-permute-start | bytes 786440 | tf_op jit(solution)/shard_map/ppermute | solution.py:46
  135.7 21.7 %collective-permute-start.3 = (bf16[16,2,16,256]{3,2,1,0:T(8,128)(2,1)S(1)}, bf16[16,2,16,256]{3,2,1,0:T(8,128)(2,1)S(1)}, u32[]{:S(2)}, u32[]{:S(2)}) collective-permute-start(bf16[16,2,16,256]{3,2,1,0:T(8,128)(2,1)S(1)} %all-to-all-done), channel_id=1, source_target_pairs={{1,2},{2,1},{3,4},{4,3},{7,8},{8,7},{9,10},{10,9},{13,14},{14,13},... | collective-permute-start | bytes 786440 | tf_op jit(solution)/shard_map/ppermute | solution.py:47
  146.0 0.7 copy-start.2
  159.1 12.3 %all-to-all-start.1 = ((bf16[16,2,16,256]{3,2,1,0:T(8,128)(2,1)}), bf16[16,2,16,256]{3,2,1,0:T(8,128)(2,1)S(1)}, u32[]{:S(2)}, u32[]{:S(2)}) async-start(bf16[16,2,16,256]{3,2,1,0:T(8,128)(2,1)} %bitcast.50), calls=%async_computation.1 | async-start | bytes 524288 | tf_op jit(solution)/shard_map/all_to_all | solution.py:57

commit v6 on v5

--- a/solution.py
+++ b/solution.py
@@ -31,14 +31,18 @@
 
 def self_energy_of(green, occupation, phonon_weight, phonon_mode):
     filling = occupation[0]
-    real_part = -filling * (green[0] - green[0].T)
-    imag_part = -filling * (green[1] + green[1].T)
-    lesser = jnp.stack([real_part, imag_part], axis=0).astype(jnp.bfloat16)
-    width = lesser.shape[-1]
+    width = green.shape[-1]
+    row = lax.broadcasted_iota(jnp.int32, (width, width), 0)
+    col = lax.broadcasted_iota(jnp.int32, (width, width), 1)
+    above_diagonal = col > row
+    packed = jnp.where(
+        above_diagonal,
+        -filling * (green[0] - green[0].T),
+        -filling * (green[1] + green[1].T),
+    ).astype(jnp.bfloat16)
     moms = lax.axis_size("kmom")
     rows = width // moms
-    chunks = lesser.reshape(2, moms, rows, width).transpose(1, 0, 2, 3)
-    held = lax.all_to_all(chunks, "kmom", 0, 0)
+    held = lax.all_to_all(packed.reshape(moms, rows, width), "kmom", 0, 0)
     count = lax.axis_size("energy")
     within = [(i, i ^ 1) for i in range(count) if (i ^ 1) < count]
     across = [(i, i + 1 if i % 2 else i - 1) for i in range(count)]
@@ -53,9 +57,12 @@
     summed = jnp.matmul(
         weight_still, flat + flat, precision=lax.Precision.HIGHEST
     ) + jnp.matmul(weight_moved, near, precision=lax.Precision.HIGHEST)
-    out = summed.astype(jnp.bfloat16).reshape(moms, 2, rows, width)
-    back = lax.all_to_all(out, "kmom", 0, 0)
-    return back.transpose(1, 0, 2, 3).reshape(2, width, width)
+    out = summed.astype(jnp.bfloat16).reshape(moms, rows, width)
+    back = lax.all_to_all(out, "kmom", 0, 0).reshape(width, width)
+    mirrored = back.T
+    real_part = jnp.where(above_diagonal, back, jnp.where(col < row, -mirrored, jnp.zeros_like(back)))
+    imag_part = jnp.where(above_diagonal, mirrored, back)
+    return jnp.stack([real_part, imag_part], axis=0)
 
 
 def on_device(free_green, coupling, coupling_tiles, occupation, phonon_weight, phonon_mode):

time: 173 us -> 165 us (0.954)
  waiting for transfers between devices: 101 us -> 94.4 us
    ppermute x1, waiting for transfers between devices: 10.1 us -> 5.82 us  [self_energy_of(): facing = lax.ppermute(held, 'energy', across)]
    all_to_all x2, waiting for transfers between devices: 16.1 us -> 14 us  [the longest x1 7.08 us: self_energy_of(): held = lax.all_to_all(packed.reshape(moms, rows, width), 'kmom', 0, 0)]
where the time goes in v6:
time: 165 us
  waiting for transfers between devices  94.4 us (57%)
  starting transfers between devices  47.3 us (29%)
  matrix products  11.7 us (7%)
  other arithmetic  4.69 us (3%)
  local copies, waits for them, and re-layouts  4.66 us (3%)
    ppermute x7, waiting for transfers between devices, passed_along(): return lax.ppermute(shard, axis, pairs)  74.6 us
    ppermute x7, starting transfers between devices, passed_along(): return lax.ppermute(shard, axis, pairs)  13.7 us
    ppermute x1, starting transfers between devices, self_energy_of(): beside = lax.ppermute(held, 'energy', within)  10.3 us
    ppermute x1, starting transfers between devices, self_energy_of(): facing = lax.ppermute(held, 'energy', across)  10.3 us
    all_to_all x1, starting transfers between devices, self_energy_of(): held = lax.all_to_all(packed.reshape(moms, rows, width), 'kmom', 0, 0)  9.51 us
    all_to_all x1, waiting for transfers between devices, self_energy_of(): held = lax.all_to_all(packed.reshape(moms, rows, width), 'kmom', 0, 0)  7.08 us
    all_to_all x1, waiting for transfers between devices, self_energy_of(): back = lax.all_to_all(out, 'kmom', 0, 0).reshape(width, width)  6.88 us
    ppermute x1, waiting for transfers between devices, self_energy_of(): facing = lax.ppermute(held, 'energy', across)  5.82 us
  transfers between devices with their start and end apart: 11, of which 10 were waited for; matrix products, arithmetic and copies ran while one was open for 3% of the time, Pallas kernels for 0%

profile of v6, /device:TPU:25, one launch (start us, length us, event | category | flops | bytes accessed | tf_op | source)
XLA Modules:
  0.0 164.6 jit_solution(244253184982751291)
XLA Ops:
  0.6 2.2 %collective-permute-start.1 = (f32[1,1,2,256,256]{4,3,2,1,0:T(8,128)}, f32[1,1,2,256,256]{4,3,2,1,0:T(8,128)S(1)}, u32[]{:S(2)}, u32[]{:S(2)}) collective-permute-start(f32[1,1,2,256,256]{4,3,2,1,0:T(8,128)} %bitcast.122), channel_id=1, source_target_pairs={{96,0},{192,96},{288,192},{384,288},{480,384},{576,480},{672,576},... | collective-permute-start | bytes 1572872 | tf_op jit(solution)/shard_map/ppermute | solution.py:10
  6.4 1.6 copy.25
  8.6 8.3 %collective-permute-done.1 = f32[1,1,2,256,256]{4,3,2,1,0:T(8,128)S(1)} collective-permute-done((f32[1,1,2,256,256]{4,3,2,1,0:T(8,128)}, f32[1,1,2,256,256]{4,3,2,1,0:T(8,128)S(1)}, u32[]{:S(2)}, u32[]{:S(2)}) %collective-permute-start.1) | collective-permute-done | bytes 524320 | tf_op jit(solution)/shard_map/ppermute | solution.py:10
  16.9 85.9 %while.10 = (s32[]{:T(128)}, f32[1,1,2,256,256]{4,3,2,1,0:T(8,128)S(1)}, f32[1,1,1,2,256,256]{5,4,3,2,1,0:T(8,128)S(1)}, f32[512,512]{1,0:T(8,128)S(1)}, f32[256,512]{1,0:T(8,128)S(1)}, /*index=5*/s32[]{:T(128)}) while((s32[]{:T(128)}, f32[1,1,2,256,256]{4,3,2,1,0:T(8,128)S(1)}, f32[1,1,1,2,256,256]{5,4,3,2,1,0:T(8,128)S(1)}, ...), condition=%wide.region_2.3_spmd, body=%wide.region_1.2_spmd.sunk | while | flops 805699584 | bytes 9437293 | solution.py:107
  18.3 1.9 %collective-permute-start = (f32[1,1,2,256,256]{4,3,2,1,0:T(8,128)S(1)}, f32[1,1,2,256,256]{4,3,2,1,0:T(8,128)S(1)}, u32[]{:S(2)}, u32[]{:S(2)}) collective-permute-start(f32[1,1,2,256,256]{4,3,2,1,0:T(8,128)S(1)} %maximum_add_fusion.4), channel_id=1, source_target_pairs={{96,0},{192,96},{288,192},{384,288},{480,384},{576,480},{672,576},... | collective-permute-start | bytes 1572872 | tf_op jit(solution)/shard_map/while/body/eval_jaxpr/ppermute | solution.py:10
  20.2 13.1 %collective-permute-done = f32[1,1,2,256,256]{4,3,2,1,0:T(8,128)S(1)} collective-permute-done((f32[1,1,2,256,256]{4,3,2,1,0:T(8,128)S(1)}, f32[1,1,2,256,256]{4,3,2,1,0:T(8,128)S(1)}, u32[]{:S(2)}, u32[]{:S(2)}) %collective-permute-start) | collective-permute-done | bytes 524320 | tf_op jit(solution)/shard_map/while/body/eval_jaxpr/ppermute | solution.py:10
  34.7 1.9 %collective-permute-start = (f32[1,1,2,256,256]{4,3,2,1,0:T(8,128)S(1)}, f32[1,1,2,256,256]{4,3,2,1,0:T(8,128)S(1)}, u32[]{:S(2)}, u32[]{:S(2)}) collective-permute-start(f32[1,1,2,256,256]{4,3,2,1,0:T(8,128)S(1)} %maximum_add_fusion.4), channel_id=1, source_target_pairs={{96,0},{192,96},{288,192},{384,288},{480,384},{576,480},{672,576},... | collective-permute-start | bytes 1572872 | tf_op jit(solution)/shard_map/while/body/eval_jaxpr/ppermute | solution.py:10
  36.6 12.3 %collective-permute-done = f32[1,1,2,256,256]{4,3,2,1,0:T(8,128)S(1)} collective-permute-done((f32[1,1,2,256,256]{4,3,2,1,0:T(8,128)S(1)}, f32[1,1,2,256,256]{4,3,2,1,0:T(8,128)S(1)}, u32[]{:S(2)}, u32[]{:S(2)}) %collective-permute-start) | collective-permute-done | bytes 524320 | tf_op jit(solution)/shard_map/while/body/eval_jaxpr/ppermute | solution.py:10
  50.2 1.9 %collective-permute-start = (f32[1,1,2,256,256]{4,3,2,1,0:T(8,128)S(1)}, f32[1,1,2,256,256]{4,3,2,1,0:T(8,128)S(1)}, u32[]{:S(2)}, u32[]{:S(2)}) collective-permute-start(f32[1,1,2,256,256]{4,3,2,1,0:T(8,128)S(1)} %maximum_add_fusion.4), channel_id=1, source_target_pairs={{96,0},{192,96},{288,192},{384,288},{480,384},{576,480},{672,576},... | collective-permute-start | bytes 1572872 | tf_op jit(solution)/shard_map/while/body/eval_jaxpr/ppermute | solution.py:10
  52.1 11.4 %collective-permute-done = f32[1,1,2,256,256]{4,3,2,1,0:T(8,128)S(1)} collective-permute-done((f32[1,1,2,256,256]{4,3,2,1,0:T(8,128)S(1)}, f32[1,1,2,256,256]{4,3,2,1,0:T(8,128)S(1)}, u32[]{:S(2)}, u32[]{:S(2)}) %collective-permute-start) | collective-permute-done | bytes 524320 | tf_op jit(solution)/shard_map/while/body/eval_jaxpr/ppermute | solution.py:10
  64.9 1.9 %collective-permute-start = (f32[1,1,2,256,256]{4,3,2,1,0:T(8,128)S(1)}, f32[1,1,2,256,256]{4,3,2,1,0:T(8,128)S(1)}, u32[]{:S(2)}, u32[]{:S(2)}) collective-permute-start(f32[1,1,2,256,256]{4,3,2,1,0:T(8,128)S(1)} %maximum_add_fusion.4), channel_id=1, source_target_pairs={{96,0},{192,96},{288,192},{384,288},{480,384},{576,480},{672,576},... | collective-permute-start | bytes 1572872 | tf_op jit(solution)/shard_map/while/body/eval_jaxpr/ppermute | solution.py:10
  66.8 10.6 %collective-permute-done = f32[1,1,2,256,256]{4,3,2,1,0:T(8,128)S(1)} collective-permute-done((f32[1,1,2,256,256]{4,3,2,1,0:T(8,128)S(1)}, f32[1,1,2,256,256]{4,3,2,1,0:T(8,128)S(1)}, u32[]{:S(2)}, u32[]{:S(2)}) %collective-permute-start) | collective-permute-done | bytes 524320 | tf_op jit(solution)/shard_map/while/body/eval_jaxpr/ppermute | solution.py:10
  78.7 1.9 %collective-permute-start = (f32[1,1,2,256,256]{4,3,2,1,0:T(8,128)S(1)}, f32[1,1,2,256,256]{4,3,2,1,0:T(8,128)S(1)}, u32[]{:S(2)}, u32[]{:S(2)}) collective-permute-start(f32[1,1,2,256,256]{4,3,2,1,0:T(8,128)S(1)} %maximum_add_fusion.4), channel_id=1, source_target_pairs={{96,0},{192,96},{288,192},{384,288},{480,384},{576,480},{672,576},... | collective-permute-start | bytes 1572872 | tf_op jit(solution)/shard_map/while/body/eval_jaxpr/ppermute | solution.py:10
  80.7 9.7 %collective-permute-done = f32[1,1,2,256,256]{4,3,2,1,0:T(8,128)S(1)} collective-permute-done((f32[1,1,2,256,256]{4,3,2,1,0:T(8,128)S(1)}, f32[1,1,2,256,256]{4,3,2,1,0:T(8,128)S(1)}, u32[]{:S(2)}, u32[]{:S(2)}) %collective-permute-start) | collective-permute-done | bytes 524320 | tf_op jit(solution)/shard_map/while/body/eval_jaxpr/ppermute | solution.py:10
  91.7 1.9 %collective-permute-start = (f32[1,1,2,256,256]{4,3,2,1,0:T(8,128)S(1)}, f32[1,1,2,256,256]{4,3,2,1,0:T(8,128)S(1)}, u32[]{:S(2)}, u32[]{:S(2)}) collective-permute-start(f32[1,1,2,256,256]{4,3,2,1,0:T(8,128)S(1)} %maximum_add_fusion.4), channel_id=1, source_target_pairs={{96,0},{192,96},{288,192},{384,288},{480,384},{576,480},{672,576},... | collective-permute-start | bytes 1572872 | tf_op jit(solution)/shard_map/while/body/eval_jaxpr/ppermute | solution.py:10
  93.7 9.2 %collective-permute-done = f32[1,1,2,256,256]{4,3,2,1,0:T(8,128)S(1)} collective-permute-done((f32[1,1,2,256,256]{4,3,2,1,0:T(8,128)S(1)}, f32[1,1,2,256,256]{4,3,2,1,0:T(8,128)S(1)}, u32[]{:S(2)}, u32[]{:S(2)}) %collective-permute-start) | collective-permute-done | bytes 524320 | tf_op jit(solution)/shard_map/while/body/eval_jaxpr/ppermute | solution.py:10
  102.9 2.2 %fusion.32 = f32[512,256]{1,0:T(8,128)S(1)} fusion(f32[512,512]{0,1:T(8,128)} %maximum_maximum_fusion, f32[512,256]{1,0:T(8,128)S(1)} %bitcast.124), kind=kOutput, calls=%fused_computation.63 | convolution fusion | flops 402653184 | bytes 2097152 | tf_op jit(solution)/shard_map/dot_general | solution.py:97
  106.9 9.5 %all-to-all-start = ((bf16[16,16,256]{2,1,0:T(8,128)(2,1)}), bf16[16,16,256]{2,1,0:T(8,128)(2,1)S(1)}, u32[]{:S(2)}, u32[]{:S(2)}) async-start(bf16[16,16,256]{2,1,0:T(8,128)(2,1)} %bitcast.26), calls=%async_computation | async-start | bytes 262144 | tf_op jit(solution)/shard_map/all_to_all | solution.py:45
  117.1 7.1 %all-to-all-done = bf16[16,16,256]{2,1,0:T(8,128)(2,1)S(1)} async-done(((bf16[16,16,256]{2,1,0:T(8,128)(2,1)}), bf16[16,16,256]{2,1,0:T(8,128)(2,1)S(1)}, u32[]{:S(2)}, u32[]{:S(2)}) %all-to-all-start) | async-done | bytes 131104 | tf_op jit(solution)/shard_map/all_to_all | solution.py:45
  124.4 10.3 %collective-permute-start.2 = (bf16[16,16,256]{2,1,0:T(8,128)(2,1)S(1)}, bf16[16,16,256]{2,1,0:T(8,128)(2,1)S(1)}, u32[]{:S(2)}, u32[]{:S(2)}) collective-permute-start(bf16[16,16,256]{2,1,0:T(8,128)(2,1)S(1)} %all-to-all-done), channel_id=1, source_target_pairs={{0,1},{1,0},{2,3},{3,2},{4,5},{5,4},{6,7},{7,6},{8,9},{9,8},{10,11... | collective-permute-start | bytes 393224 | tf_op jit(solution)/shard_map/ppermute | solution.py:50
  134.7 10.3 %collective-permute-start.3 = (bf16[16,16,256]{2,1,0:T(8,128)(2,1)S(1)}, bf16[16,16,256]{2,1,0:T(8,128)(2,1)S(1)}, u32[]{:S(2)}, u32[]{:S(2)}) collective-permute-start(bf16[16,16,256]{2,1,0:T(8,128)(2,1)S(1)} %all-to-all-done), channel_id=1, source_target_pairs={{1,2},{2,1},{3,4},{4,3},{7,8},{8,7},{9,10},{10,9},{13,14},{14,13},... | collective-permute-start | bytes 393224 | tf_op jit(solution)/shard_map/ppermute | solution.py:51
  145.4 5.8 %collective-permute-done.3 = bf16[16,16,256]{2,1,0:T(8,128)(2,1)S(1)} collective-permute-done((bf16[16,16,256]{2,1,0:T(8,128)(2,1)S(1)}, bf16[16,16,256]{2,1,0:T(8,128)(2,1)S(1)}, u32[]{:S(2)}, u32[]{:S(2)}) %collective-permute-start.3) | collective-permute-done | bytes 131104 | tf_op jit(solution)/shard_map/ppermute | solution.py:51
  152.4 3.5 %all-to-all-start.1 = ((bf16[16,16,256]{2,1,0:T(8,128)(2,1)}), bf16[16,16,256]{2,1,0:T(8,128)(2,1)S(1)}, u32[]{:S(2)}, u32[]{:S(2)}) async-start(bf16[16,16,256]{2,1,0:T(8,128)(2,1)} %bitcast.44), calls=%async_computation.1 | async-start | bytes 262144 | tf_op jit(solution)/shard_map/all_to_all | solution.py:61
  156.8 6.9 %all-to-all-done.1 = bf16[16,16,256]{2,1,0:T(8,128)(2,1)S(1)} async-done(((bf16[16,16,256]{2,1,0:T(8,128)(2,1)}), bf16[16,16,256]{2,1,0:T(8,128)(2,1)S(1)}, u32[]{:S(2)}, u32[]{:S(2)}) %all-to-all-start.1) | async-done | bytes 131104 | tf_op jit(solution)/shard_map/all_to_all | solution.py:61
  (64 shorter events, 17.2 us)
Async XLA Ops:
  0.6 2.3 %copy-start.3 = (s32[1,8,3]{1,0,2:T(1,128)S(1)}, s32[1,8,3]{1,0,2:T(1,128)}, u32[]{:S(2)}) copy-start(s32[1,8,3]{1,0,2:T(1,128)} %param.10) | copy-start | bytes 292
  0.6 2.4 %copy-start.1 = (f32[1,256,256]{2,1,0:T(8,128)S(1)}, f32[1,256,256]{2,1,0:T(8,128)}, u32[]{:S(2)}) copy-start(f32[1,256,256]{2,1,0:T(8,128)} %param.9) | copy-start | bytes 786436
  0.6 16.3 %collective-permute-start.1 = (f32[1,1,2,256,256]{4,3,2,1,0:T(8,128)}, f32[1,1,2,256,256]{4,3,2,1,0:T(8,128)S(1)}, u32[]{:S(2)}, u32[]{:S(2)}) collective-permute-start(f32[1,1,2,256,256]{4,3,2,1,0:T(8,128)} %bitcast.122), channel_id=1, source_target_pairs={{96,0},{192,96},{288,192},{384,288},{480,384},{576,480},{672,576},... | collective-permute-start | bytes 1572872 | tf_op jit(solution)/shard_map/ppermute | solution.py:10
  3.0 1.0 copy-start
  18.3 15.1 %collective-permute-start = (f32[1,1,2,256,256]{4,3,2,1,0:T(8,128)S(1)}, f32[1,1,2,256,256]{4,3,2,1,0:T(8,128)S(1)}, u32[]{:S(2)}, u32[]{:S(2)}) collective-permute-start(f32[1,1,2,256,256]{4,3,2,1,0:T(8,128)S(1)} %maximum_add_fusion.4), channel_id=1, source_target_pairs={{96,0},{192,96},{288,192},{384,288},{480,384},{576,480},{672,576},... | collective-permute-start | bytes 1572872 | tf_op jit(solution)/shard_map/while/body/eval_jaxpr/ppermute | solution.py:10
  34.7 14.2 %collective-permute-start = (f32[1,1,2,256,256]{4,3,2,1,0:T(8,128)S(1)}, f32[1,1,2,256,256]{4,3,2,1,0:T(8,128)S(1)}, u32[]{:S(2)}, u32[]{:S(2)}) collective-permute-start(f32[1,1,2,256,256]{4,3,2,1,0:T(8,128)S(1)} %maximum_add_fusion.4), channel_id=1, source_target_pairs={{96,0},{192,96},{288,192},{384,288},{480,384},{576,480},{672,576},... | collective-permute-start | bytes 1572872 | tf_op jit(solution)/shard_map/while/body/eval_jaxpr/ppermute | solution.py:10
  50.2 13.3 %collective-permute-start = (f32[1,1,2,256,256]{4,3,2,1,0:T(8,128)S(1)}, f32[1,1,2,256,256]{4,3,2,1,0:T(8,128)S(1)}, u32[]{:S(2)}, u32[]{:S(2)}) collective-permute-start(f32[1,1,2,256,256]{4,3,2,1,0:T(8,128)S(1)} %maximum_add_fusion.4), channel_id=1, source_target_pairs={{96,0},{192,96},{288,192},{384,288},{480,384},{576,480},{672,576},... | collective-permute-start | bytes 1572872 | tf_op jit(solution)/shard_map/while/body/eval_jaxpr/ppermute | solution.py:10
  64.9 12.5 %collective-permute-start = (f32[1,1,2,256,256]{4,3,2,1,0:T(8,128)S(1)}, f32[1,1,2,256,256]{4,3,2,1,0:T(8,128)S(1)}, u32[]{:S(2)}, u32[]{:S(2)}) collective-permute-start(f32[1,1,2,256,256]{4,3,2,1,0:T(8,128)S(1)} %maximum_add_fusion.4), channel_id=1, source_target_pairs={{96,0},{192,96},{288,192},{384,288},{480,384},{576,480},{672,576},... | collective-permute-start | bytes 1572872 | tf_op jit(solution)/shard_map/while/body/eval_jaxpr/ppermute | solution.py:10
  78.7 11.6 %collective-permute-start = (f32[1,1,2,256,256]{4,3,2,1,0:T(8,128)S(1)}, f32[1,1,2,256,256]{4,3,2,1,0:T(8,128)S(1)}, u32[]{:S(2)}, u32[]{:S(2)}) collective-permute-start(f32[1,1,2,256,256]{4,3,2,1,0:T(8,128)S(1)} %maximum_add_fusion.4), channel_id=1, source_target_pairs={{96,0},{192,96},{288,192},{384,288},{480,384},{576,480},{672,576},... | collective-permute-start | bytes 1572872 | tf_op jit(solution)/shard_map/while/body/eval_jaxpr/ppermute | solution.py:10
  91.7 11.1 %collective-permute-start = (f32[1,1,2,256,256]{4,3,2,1,0:T(8,128)S(1)}, f32[1,1,2,256,256]{4,3,2,1,0:T(8,128)S(1)}, u32[]{:S(2)}, u32[]{:S(2)}) collective-permute-start(f32[1,1,2,256,256]{4,3,2,1,0:T(8,128)S(1)} %maximum_add_fusion.4), channel_id=1, source_target_pairs={{96,0},{192,96},{288,192},{384,288},{480,384},{576,480},{672,576},... | collective-permute-start | bytes 1572872 | tf_op jit(solution)/shard_map/while/body/eval_jaxpr/ppermute | solution.py:10
  106.9 17.3 %all-to-all-start = ((bf16[16,16,256]{2,1,0:T(8,128)(2,1)}), bf16[16,16,256]{2,1,0:T(8,128)(2,1)S(1)}, u32[]{:S(2)}, u32[]{:S(2)}) async-start(bf16[16,16,256]{2,1,0:T(8,128)(2,1)} %bitcast.26), calls=%async_computation | async-start | bytes 262144 | tf_op jit(solution)/shard_map/all_to_all | solution.py:45
  116.4 0.7 copy-start.4
  124.2 20.8 %copy-start.2 = (f32[2,16,16]{2,1,0:T(8,128)S(1)}, f32[2,16,16]{2,1,0:T(8,128)}, u32[]{:S(2)}) copy-start(f32[2,16,16]{2,1,0:T(8,128)} %param.12) | copy-start | bytes 6148
  124.4 21.0 %collective-permute-start.2 = (bf16[16,16,256]{2,1,0:T(8,128)(2,1)S(1)}, bf16[16,16,256]{2,1,0:T(8,128)(2,1)S(1)}, u32[]{:S(2)}, u32[]{:S(2)}) collective-permute-start(bf16[16,16,256]{2,1,0:T(8,128)(2,1)S(1)} %all-to-all-done), channel_id=1, source_target_pairs={{0,1},{1,0},{2,3},{3,2},{4,5},{5,4},{6,7},{7,6},{8,9},{9,8},{10,11... | collective-permute-start | bytes 393224 | tf_op jit(solution)/shard_map/ppermute | solution.py:50
  134.7 16.5 %collective-permute-start.3 = (bf16[16,16,256]{2,1,0:T(8,128)(2,1)S(1)}, bf16[16,16,256]{2,1,0:T(8,128)(2,1)S(1)}, u32[]{:S(2)}, u32[]{:S(2)}) collective-permute-start(bf16[16,16,256]{2,1,0:T(8,128)(2,1)S(1)} %all-to-all-done), channel_id=1, source_target_pairs={{1,2},{2,1},{3,4},{4,3},{7,8},{8,7},{9,10},{10,9},{13,14},{14,13},... | collective-permute-start | bytes 393224 | tf_op jit(solution)/shard_map/ppermute | solution.py:51
  152.4 11.3 %all-to-all-start.1 = ((bf16[16,16,256]{2,1,0:T(8,128)(2,1)}), bf16[16,16,256]{2,1,0:T(8,128)(2,1)S(1)}, u32[]{:S(2)}, u32[]{:S(2)}) async-start(bf16[16,16,256]{2,1,0:T(8,128)(2,1)} %bitcast.44), calls=%async_computation.1 | async-start | bytes 262144 | tf_op jit(solution)/shard_map/all_to_all | solution.py:61

commit v7 on v6

--- a/solution.py
+++ b/solution.py
@@ -47,8 +47,8 @@
     within = [(i, i ^ 1) for i in range(count) if (i ^ 1) < count]
     across = [(i, i + 1 if i % 2 else i - 1) for i in range(count)]
     across = [(i, j) for i, j in across if 0 <= j < count]
+    facing = lax.ppermute(held, "energy", across)
     beside = lax.ppermute(held, "energy", within)
-    facing = lax.ppermute(held, "energy", across)
     flat = held.reshape(moms, -1).astype(jnp.float32)
     near = beside.reshape(moms, -1).astype(jnp.float32) + facing.reshape(moms, -1).astype(jnp.float32)
     still = phonon_mode[0] == 0
@@ -100,11 +100,9 @@
         imag_part = outer[:width, width:] + outer[width:, :width]
         return free_green[0] + jnp.stack([real_part, imag_part], axis=0)[None, None]
 
-    def advance(turn_index, beyond):
-        return passed_along(sweep(beyond), "slab", -1)
-
-    first = passed_along(free_green[0], "slab", -1)
-    beyond = lax.fori_loop(0, lax.axis_size("slab") - 2, advance, first)
+    beyond = passed_along(free_green[0], "slab", -1)
+    for _ in range(lax.axis_size("slab") - 2):
+        beyond = passed_along(sweep(beyond), "slab", -1)
     green = sweep(beyond)
     self_energy = self_energy_of(green[0, 0], occupation, phonon_weight, phonon_mode)
     return green[None], self_energy.reshape(green.shape)[None]

time: 165 us -> 167 us (1.012)
  waiting for transfers between devices: 94.4 us -> 96.7 us
    ppermute x7, waiting for transfers between devices: 74.6 us -> 76.9 us  [passed_along(): return lax.ppermute(shard, axis, pairs)]
  transfers between devices with their start and end apart: 11 -> 11, of which waited for: 10 -> 10; matrix products, arithmetic and copies ran while one was open for 3% -> 2% of each run, Pallas kernels for 0% -> 0%
where the time goes in v7:
time: 167 us; the launch traced here: 166 us
  waiting for transfers between devices  96.7 us (58%)
  starting transfers between devices  47.5 us (28%)
  matrix products  13.1 us (8%)
  other arithmetic  3.72 us (2%)
  local copies, waits for them, and re-layouts  3.11 us (2%)
  between operations  1.84 us (1%)
    ppermute x7, waiting for transfers between devices, passed_along(): return lax.ppermute(shard, axis, pairs)  76.9 us
    ppermute x7, starting transfers between devices, passed_along(): return lax.ppermute(shard, axis, pairs)  13.9 us
    ppermute x1, starting transfers between devices, self_energy_of(): beside = lax.ppermute(held, 'energy', within)  10.3 us
    ppermute x1, starting transfers between devices, self_energy_of(): facing = lax.ppermute(held, 'energy', across)  10.2 us
    all_to_all x1, starting transfers between devices, self_energy_of(): held = lax.all_to_all(packed.reshape(moms, rows, width), 'kmom', 0, 0)  9.58 us
    dot_general x7, matrix products, sweep(): mixed = jnp.matmul(left_block, inner, precision=high)  7.22 us
    all_to_all x1, waiting for transfers between devices, self_energy_of(): held = lax.all_to_all(packed.reshape(moms, rows, width), 'kmom', 0, 0)  7.08 us
    all_to_all x1, waiting for transfers between devices, self_energy_of(): back = lax.all_to_all(out, 'kmom', 0, 0).reshape(width, width)  6.88 us
  transfers between devices with their start and end apart: 11, of which 10 were waited for; matrix products, arithmetic and copies ran while one was open for 2% of the time, Pallas kernels for 0%

profile of v7, /device:TPU:25, one launch (start us, length us, event | category | flops | bytes accessed | tf_op | source)
XLA Modules:
  0.0 166.0 jit_solution(11124578372810779224)
XLA Ops:
  0.6 2.2 %collective-permute-start = (f32[1,1,2,256,256]{4,3,2,1,0:T(8,128)}, f32[1,1,2,256,256]{4,3,2,1,0:T(8,128)S(1)}, u32[]{:S(2)}, u32[]{:S(2)}) collective-permute-start(f32[1,1,2,256,256]{4,3,2,1,0:T(8,128)} %bitcast.157), channel_id=1, source_target_pairs={{96,0},{192,96},{288,192},{384,288},{480,384},{576,480},{672,576},... | collective-permute-start | bytes 1572872 | tf_op jit(solution)/shard_map/ppermute | solution.py:10
  4.0 1.1 convolution_bitcast_fusion
  5.4 11.5 %collective-permute-done = f32[1,1,2,256,256]{4,3,2,1,0:T(8,128)S(1)} collective-permute-done((f32[1,1,2,256,256]{4,3,2,1,0:T(8,128)}, f32[1,1,2,256,256]{4,3,2,1,0:T(8,128)S(1)}, u32[]{:S(2)}, u32[]{:S(2)}) %collective-permute-start) | collective-permute-done | bytes 524320 | tf_op jit(solution)/shard_map/ppermute | solution.py:10
  18.7 1.9 %collective-permute-start.1 = (f32[1,1,2,256,256]{4,3,2,1,0:T(8,128)S(1)}, f32[1,1,2,256,256]{4,3,2,1,0:T(8,128)S(1)}, u32[]{:S(2)}, u32[]{:S(2)}) collective-permute-start(f32[1,1,2,256,256]{4,3,2,1,0:T(8,128)S(1)} %maximum_add_fusion), channel_id=1, source_target_pairs={{96,0},{192,96},{288,192},{384,288},{480,384},{576,480},{672,576},... | collective-permute-start | bytes 1572872 | tf_op jit(solution)/shard_map/ppermute | solution.py:10
  20.6 13.1 %collective-permute-done.1 = f32[1,1,2,256,256]{4,3,2,1,0:T(8,128)S(1)} collective-permute-done((f32[1,1,2,256,256]{4,3,2,1,0:T(8,128)S(1)}, f32[1,1,2,256,256]{4,3,2,1,0:T(8,128)S(1)}, u32[]{:S(2)}, u32[]{:S(2)}) %collective-permute-start.1) | collective-permute-done | bytes 524320 | tf_op jit(solution)/shard_map/ppermute | solution.py:10
  35.5 1.9 %collective-permute-start.2 = (f32[1,1,2,256,256]{4,3,2,1,0:T(8,128)S(1)}, f32[1,1,2,256,256]{4,3,2,1,0:T(8,128)S(1)}, u32[]{:S(2)}, u32[]{:S(2)}) collective-permute-start(f32[1,1,2,256,256]{4,3,2,1,0:T(8,128)S(1)} %maximum_add_fusion.1), channel_id=1, source_target_pairs={{96,0},{192,96},{288,192},{384,288},{480,384},{576,480},{672,576},... | collective-permute-start | bytes 1572872 | tf_op jit(solution)/shard_map/ppermute | solution.py:10
  37.5 12.3 %collective-permute-done.2 = f32[1,1,2,256,256]{4,3,2,1,0:T(8,128)S(1)} collective-permute-done((f32[1,1,2,256,256]{4,3,2,1,0:T(8,128)S(1)}, f32[1,1,2,256,256]{4,3,2,1,0:T(8,128)S(1)}, u32[]{:S(2)}, u32[]{:S(2)}) %collective-permute-start.2) | collective-permute-done | bytes 524320 | tf_op jit(solution)/shard_map/ppermute | solution.py:10
  49.7 1.0 fusion.44
  51.5 1.9 %collective-permute-start.3 = (f32[1,1,2,256,256]{4,3,2,1,0:T(8,128)S(1)}, f32[1,1,2,256,256]{4,3,2,1,0:T(8,128)S(1)}, u32[]{:S(2)}, u32[]{:S(2)}) collective-permute-start(f32[1,1,2,256,256]{4,3,2,1,0:T(8,128)S(1)} %maximum_add_fusion.2), channel_id=1, source_target_pairs={{96,0},{192,96},{288,192},{384,288},{480,384},{576,480},{672,576},... | collective-permute-start | bytes 1572872 | tf_op jit(solution)/shard_map/ppermute | solution.py:10
  53.4 11.4 %collective-permute-done.3 = f32[1,1,2,256,256]{4,3,2,1,0:T(8,128)S(1)} collective-permute-done((f32[1,1,2,256,256]{4,3,2,1,0:T(8,128)S(1)}, f32[1,1,2,256,256]{4,3,2,1,0:T(8,128)S(1)}, u32[]{:S(2)}, u32[]{:S(2)}) %collective-permute-start.3) | collective-permute-done | bytes 524320 | tf_op jit(solution)/shard_map/ppermute | solution.py:10
  66.6 1.9 %collective-permute-start.4 = (f32[1,1,2,256,256]{4,3,2,1,0:T(8,128)S(1)}, f32[1,1,2,256,256]{4,3,2,1,0:T(8,128)S(1)}, u32[]{:S(2)}, u32[]{:S(2)}) collective-permute-start(f32[1,1,2,256,256]{4,3,2,1,0:T(8,128)S(1)} %maximum_add_fusion.3), channel_id=1, source_target_pairs={{96,0},{192,96},{288,192},{384,288},{480,384},{576,480},{672,576},... | collective-permute-start | bytes 1572872 | tf_op jit(solution)/shard_map/ppermute | solution.py:10
  68.6 10.6 %collective-permute-done.4 = f32[1,1,2,256,256]{4,3,2,1,0:T(8,128)S(1)} collective-permute-done((f32[1,1,2,256,256]{4,3,2,1,0:T(8,128)S(1)}, f32[1,1,2,256,256]{4,3,2,1,0:T(8,128)S(1)}, u32[]{:S(2)}, u32[]{:S(2)}) %collective-permute-start.4) | collective-permute-done | bytes 524320 | tf_op jit(solution)/shard_map/ppermute | solution.py:10
  80.9 2.1 %collective-permute-start.5 = (f32[1,1,2,256,256]{4,3,2,1,0:T(8,128)S(1)}, f32[1,1,2,256,256]{4,3,2,1,0:T(8,128)S(1)}, u32[]{:S(2)}, u32[]{:S(2)}) collective-permute-start(f32[1,1,2,256,256]{4,3,2,1,0:T(8,128)S(1)} %maximum_add_fusion.4), channel_id=1, source_target_pairs={{96,0},{192,96},{288,192},{384,288},{480,384},{576,480},{672,576},... | collective-permute-start | bytes 1572872 | tf_op jit(solution)/shard_map/ppermute | solution.py:10
  83.0 9.5 %collective-permute-done.5 = f32[1,1,2,256,256]{4,3,2,1,0:T(8,128)S(1)} collective-permute-done((f32[1,1,2,256,256]{4,3,2,1,0:T(8,128)S(1)}, f32[1,1,2,256,256]{4,3,2,1,0:T(8,128)S(1)}, u32[]{:S(2)}, u32[]{:S(2)}) %collective-permute-start.5) | collective-permute-done | bytes 524320 | tf_op jit(solution)/shard_map/ppermute | solution.py:10
  92.5 1.0 fusion.50
  94.3 1.9 %collective-permute-start.6 = (f32[1,1,2,256,256]{4,3,2,1,0:T(8,128)S(1)}, f32[1,1,2,256,256]{4,3,2,1,0:T(8,128)S(1)}, u32[]{:S(2)}, u32[]{:S(2)}) collective-permute-start(f32[1,1,2,256,256]{4,3,2,1,0:T(8,128)S(1)} %maximum_add_fusion.5), channel_id=1, source_target_pairs={{96,0},{192,96},{288,192},{384,288},{480,384},{576,480},{672,576},... | collective-permute-start | bytes 1572872 | tf_op jit(solution)/shard_map/ppermute | solution.py:10
  96.9 8.6 %collective-permute-done.6 = f32[1,1,2,256,256]{4,3,2,1,0:T(8,128)S(1)} collective-permute-done((f32[1,1,2,256,256]{4,3,2,1,0:T(8,128)S(1)}, f32[1,1,2,256,256]{4,3,2,1,0:T(8,128)S(1)}, u32[]{:S(2)}, u32[]{:S(2)}) %collective-permute-start.6) | collective-permute-done | bytes 524320 | tf_op jit(solution)/shard_map/ppermute | solution.py:10
  108.3 9.6 %all-to-all-start = ((bf16[16,16,256]{2,1,0:T(8,128)(2,1)}), bf16[16,16,256]{2,1,0:T(8,128)(2,1)S(1)}, u32[]{:S(2)}, u32[]{:S(2)}) async-start(bf16[16,16,256]{2,1,0:T(8,128)(2,1)} %bitcast.40), calls=%async_computation | async-start | bytes 262144 | tf_op jit(solution)/shard_map/all_to_all | solution.py:45
  118.6 7.1 %all-to-all-done = bf16[16,16,256]{2,1,0:T(8,128)(2,1)S(1)} async-done(((bf16[16,16,256]{2,1,0:T(8,128)(2,1)}), bf16[16,16,256]{2,1,0:T(8,128)(2,1)S(1)}, u32[]{:S(2)}, u32[]{:S(2)}) %all-to-all-start) | async-done | bytes 131104 | tf_op jit(solution)/shard_map/all_to_all | solution.py:45
  125.9 10.3 %collective-permute-start.7 = (bf16[16,16,256]{2,1,0:T(8,128)(2,1)S(1)}, bf16[16,16,256]{2,1,0:T(8,128)(2,1)S(1)}, u32[]{:S(2)}, u32[]{:S(2)}) collective-permute-start(bf16[16,16,256]{2,1,0:T(8,128)(2,1)S(1)} %all-to-all-done), channel_id=1, source_target_pairs={{0,1},{1,0},{2,3},{3,2},{4,5},{5,4},{6,7},{7,6},{8,9},{9,8},{10,11... | collective-permute-start | bytes 393224 | tf_op jit(solution)/shard_map/ppermute | solution.py:51
  136.2 10.2 %collective-permute-start.8 = (bf16[16,16,256]{2,1,0:T(8,128)(2,1)S(1)}, bf16[16,16,256]{2,1,0:T(8,128)(2,1)S(1)}, u32[]{:S(2)}, u32[]{:S(2)}) collective-permute-start(bf16[16,16,256]{2,1,0:T(8,128)(2,1)S(1)} %all-to-all-done), channel_id=1, source_target_pairs={{1,2},{2,1},{3,4},{4,3},{7,8},{8,7},{9,10},{10,9},{13,14},{14,13},... | collective-permute-start | bytes 393224 | tf_op jit(solution)/shard_map/ppermute | solution.py:50
  146.8 5.8 %collective-permute-done.8 = bf16[16,16,256]{2,1,0:T(8,128)(2,1)S(1)} collective-permute-done((bf16[16,16,256]{2,1,0:T(8,128)(2,1)S(1)}, bf16[16,16,256]{2,1,0:T(8,128)(2,1)S(1)}, u32[]{:S(2)}, u32[]{:S(2)}) %collective-permute-start.8) | collective-permute-done | bytes 131104 | tf_op jit(solution)/shard_map/ppermute | solution.py:50
  153.9 3.5 %all-to-all-start.1 = ((bf16[16,16,256]{2,1,0:T(8,128)(2,1)}), bf16[16,16,256]{2,1,0:T(8,128)(2,1)S(1)}, u32[]{:S(2)}, u32[]{:S(2)}) async-start(bf16[16,16,256]{2,1,0:T(8,128)(2,1)} %bitcast.58), calls=%async_computation.1 | async-start | bytes 262144 | tf_op jit(solution)/shard_map/all_to_all | solution.py:61
  158.2 6.9 %all-to-all-done.1 = bf16[16,16,256]{2,1,0:T(8,128)(2,1)S(1)} async-done(((bf16[16,16,256]{2,1,0:T(8,128)(2,1)}), bf16[16,16,256]{2,1,0:T(8,128)(2,1)S(1)}, u32[]{:S(2)}, u32[]{:S(2)}) %all-to-all-start.1) | async-done | bytes 131104 | tf_op jit(solution)/shard_map/all_to_all | solution.py:61
  (62 shorter events, 16.8 us)
Async XLA Ops:
  0.6 2.3 %copy-start.3 = (s32[1,8,3]{1,0,2:T(1,128)S(1)}, s32[1,8,3]{1,0,2:T(1,128)}, u32[]{:S(2)}) copy-start(s32[1,8,3]{1,0,2:T(1,128)} %param.8) | copy-start | bytes 292
  0.6 2.4 %copy-start.1 = (f32[1,256,256]{2,1,0:T(8,128)S(1)}, f32[1,256,256]{2,1,0:T(8,128)}, u32[]{:S(2)}) copy-start(f32[1,256,256]{2,1,0:T(8,128)} %param.7) | copy-start | bytes 786436
  0.6 16.3 %collective-permute-start = (f32[1,1,2,256,256]{4,3,2,1,0:T(8,128)}, f32[1,1,2,256,256]{4,3,2,1,0:T(8,128)S(1)}, u32[]{:S(2)}, u32[]{:S(2)}) collective-permute-start(f32[1,1,2,256,256]{4,3,2,1,0:T(8,128)} %bitcast.157), channel_id=1, source_target_pairs={{96,0},{192,96},{288,192},{384,288},{480,384},{576,480},{672,576},... | collective-permute-start | bytes 1572872 | tf_op jit(solution)/shard_map/ppermute | solution.py:10
  3.0 1.0 copy-start
  18.7 15.1 %collective-permute-start.1 = (f32[1,1,2,256,256]{4,3,2,1,0:T(8,128)S(1)}, f32[1,1,2,256,256]{4,3,2,1,0:T(8,128)S(1)}, u32[]{:S(2)}, u32[]{:S(2)}) collective-permute-start(f32[1,1,2,256,256]{4,3,2,1,0:T(8,128)S(1)} %maximum_add_fusion), channel_id=1, source_target_pairs={{96,0},{192,96},{288,192},{384,288},{480,384},{576,480},{672,576},... | collective-permute-start | bytes 1572872 | tf_op jit(solution)/shard_map/ppermute | solution.py:10
  35.5 14.2 %collective-permute-start.2 = (f32[1,1,2,256,256]{4,3,2,1,0:T(8,128)S(1)}, f32[1,1,2,256,256]{4,3,2,1,0:T(8,128)S(1)}, u32[]{:S(2)}, u32[]{:S(2)}) collective-permute-start(f32[1,1,2,256,256]{4,3,2,1,0:T(8,128)S(1)} %maximum_add_fusion.1), channel_id=1, source_target_pairs={{96,0},{192,96},{288,192},{384,288},{480,384},{576,480},{672,576},... | collective-permute-start | bytes 1572872 | tf_op jit(solution)/shard_map/ppermute | solution.py:10
  51.5 13.3 %collective-permute-start.3 = (f32[1,1,2,256,256]{4,3,2,1,0:T(8,128)S(1)}, f32[1,1,2,256,256]{4,3,2,1,0:T(8,128)S(1)}, u32[]{:S(2)}, u32[]{:S(2)}) collective-permute-start(f32[1,1,2,256,256]{4,3,2,1,0:T(8,128)S(1)} %maximum_add_fusion.2), channel_id=1, source_target_pairs={{96,0},{192,96},{288,192},{384,288},{480,384},{576,480},{672,576},... | collective-permute-start | bytes 1572872 | tf_op jit(solution)/shard_map/ppermute | solution.py:10
  66.6 12.5 %collective-permute-start.4 = (f32[1,1,2,256,256]{4,3,2,1,0:T(8,128)S(1)}, f32[1,1,2,256,256]{4,3,2,1,0:T(8,128)S(1)}, u32[]{:S(2)}, u32[]{:S(2)}) collective-permute-start(f32[1,1,2,256,256]{4,3,2,1,0:T(8,128)S(1)} %maximum_add_fusion.3), channel_id=1, source_target_pairs={{96,0},{192,96},{288,192},{384,288},{480,384},{576,480},{672,576},... | collective-permute-start | bytes 1572872 | tf_op jit(solution)/shard_map/ppermute | solution.py:10
  80.9 11.6 %collective-permute-start.5 = (f32[1,1,2,256,256]{4,3,2,1,0:T(8,128)S(1)}, f32[1,1,2,256,256]{4,3,2,1,0:T(8,128)S(1)}, u32[]{:S(2)}, u32[]{:S(2)}) collective-permute-start(f32[1,1,2,256,256]{4,3,2,1,0:T(8,128)S(1)} %maximum_add_fusion.4), channel_id=1, source_target_pairs={{96,0},{192,96},{288,192},{384,288},{480,384},{576,480},{672,576},... | collective-permute-start | bytes 1572872 | tf_op jit(solution)/shard_map/ppermute | solution.py:10
  94.3 11.1 %collective-permute-start.6 = (f32[1,1,2,256,256]{4,3,2,1,0:T(8,128)S(1)}, f32[1,1,2,256,256]{4,3,2,1,0:T(8,128)S(1)}, u32[]{:S(2)}, u32[]{:S(2)}) collective-permute-start(f32[1,1,2,256,256]{4,3,2,1,0:T(8,128)S(1)} %maximum_add_fusion.5), channel_id=1, source_target_pairs={{96,0},{192,96},{288,192},{384,288},{480,384},{576,480},{672,576},... | collective-permute-start | bytes 1572872 | tf_op jit(solution)/shard_map/ppermute | solution.py:10
  108.3 17.4 %all-to-all-start = ((bf16[16,16,256]{2,1,0:T(8,128)(2,1)}), bf16[16,16,256]{2,1,0:T(8,128)(2,1)S(1)}, u32[]{:S(2)}, u32[]{:S(2)}) async-start(bf16[16,16,256]{2,1,0:T(8,128)(2,1)} %bitcast.40), calls=%async_computation | async-start | bytes 262144 | tf_op jit(solution)/shard_map/all_to_all | solution.py:45
  117.9 0.7 copy-start.4
  125.7 20.7 %copy-start.2 = (f32[2,16,16]{2,1,0:T(8,128)S(1)}, f32[2,16,16]{2,1,0:T(8,128)}, u32[]{:S(2)}) copy-start(f32[2,16,16]{2,1,0:T(8,128)} %param.10) | copy-start | bytes 6148
  125.9 20.9 %collective-permute-start.7 = (bf16[16,16,256]{2,1,0:T(8,128)(2,1)S(1)}, bf16[16,16,256]{2,1,0:T(8,128)(2,1)S(1)}, u32[]{:S(2)}, u32[]{:S(2)}) collective-permute-start(bf16[16,16,256]{2,1,0:T(8,128)(2,1)S(1)} %all-to-all-done), channel_id=1, source_target_pairs={{0,1},{1,0},{2,3},{3,2},{4,5},{5,4},{6,7},{7,6},{8,9},{9,8},{10,11... | collective-permute-start | bytes 393224 | tf_op jit(solution)/shard_map/ppermute | solution.py:51
  136.2 16.4 %collective-permute-start.8 = (bf16[16,16,256]{2,1,0:T(8,128)(2,1)S(1)}, bf16[16,16,256]{2,1,0:T(8,128)(2,1)S(1)}, u32[]{:S(2)}, u32[]{:S(2)}) collective-permute-start(bf16[16,16,256]{2,1,0:T(8,128)(2,1)S(1)} %all-to-all-done), channel_id=1, source_target_pairs={{1,2},{2,1},{3,4},{4,3},{7,8},{8,7},{9,10},{10,9},{13,14},{14,13},... | collective-permute-start | bytes 393224 | tf_op jit(solution)/shard_map/ppermute | solution.py:50
  153.9 11.3 %all-to-all-start.1 = ((bf16[16,16,256]{2,1,0:T(8,128)(2,1)}), bf16[16,16,256]{2,1,0:T(8,128)(2,1)S(1)}, u32[]{:S(2)}, u32[]{:S(2)}) async-start(bf16[16,16,256]{2,1,0:T(8,128)(2,1)} %bitcast.58), calls=%async_computation.1 | async-start | bytes 262144 | tf_op jit(solution)/shard_map/all_to_all | solution.py:61

commit v8 on v6

--- a/solution.py
+++ b/solution.py
@@ -42,15 +42,18 @@
     ).astype(jnp.bfloat16)
     moms = lax.axis_size("kmom")
     rows = width // moms
-    held = lax.all_to_all(packed.reshape(moms, rows, width), "kmom", 0, 0)
     count = lax.axis_size("energy")
     within = [(i, i ^ 1) for i in range(count) if (i ^ 1) < count]
     across = [(i, i + 1 if i % 2 else i - 1) for i in range(count)]
     across = [(i, j) for i, j in across if 0 <= j < count]
-    beside = lax.ppermute(held, "energy", within)
-    facing = lax.ppermute(held, "energy", across)
-    flat = held.reshape(moms, -1).astype(jnp.float32)
-    near = beside.reshape(moms, -1).astype(jnp.float32) + facing.reshape(moms, -1).astype(jnp.float32)
+    beside = lax.ppermute(packed, "energy", within)
+    facing = lax.ppermute(packed, "energy", across)
+    three = jnp.stack([packed, beside, facing], axis=0).reshape(3, moms, rows, width)
+    held = lax.all_to_all(three.transpose(1, 0, 2, 3), "kmom", 0, 0)
+    flat = held[:, 0].reshape(moms, -1).astype(jnp.float32)
+    near = held[:, 1].reshape(moms, -1).astype(jnp.float32) + held[:, 2].reshape(
+        moms, -1
+    ).astype(jnp.float32)
     still = phonon_mode[0] == 0
     weight_still = jnp.where(still, phonon_weight[0], phonon_weight[1])
     weight_moved = jnp.where(still, phonon_weight[1], phonon_weight[0])

time: 165 us -> 169 us (1.024)
  starting transfers between devices: 47.3 us -> 50.3 us
    all_to_all x1, starting transfers between devices: 9.51 us -> 13.5 us  [self_energy_of(): held = lax.all_to_all(three.transpose(1, 0, 2, 3), 'kmom', 0, 0)]
    ppermute x2, waiting for transfers between devices: 5.83 us -> 2.63 us  [the longest x1 2.63 us: self_energy_of(): facing = lax.ppermute(packed, 'energy', across)]
    all_to_all x1, waiting for transfers between devices: 7.08 us -> 9.91 us  [self_energy_of(): held = lax.all_to_all(three.transpose(1, 0, 2, 3), 'kmom', 0, 0)]
where the time goes in v8:
time: 169 us; the launch traced here: 168 us
  waiting for transfers between devices  94 us (56%)
  starting transfers between devices  50.3 us (30%)
  matrix products  11.7 us (7%)
  local copies, waits for them, and re-layouts  5.2 us (3%)
  other arithmetic  4.86 us (3%)
    ppermute x7, waiting for transfers between devices, passed_along(): return lax.ppermute(shard, axis, pairs)  74.6 us
    ppermute x7, starting transfers between devices, passed_along(): return lax.ppermute(shard, axis, pairs)  13.7 us
    all_to_all x1, starting transfers between devices, self_energy_of(): held = lax.all_to_all(three.transpose(1, 0, 2, 3), 'kmom', 0, 0)  13.5 us
    ppermute x1, starting transfers between devices, self_energy_of(): facing = lax.ppermute(packed, 'energy', across)  10.5 us
    all_to_all x1, waiting for transfers between devices, self_energy_of(): held = lax.all_to_all(three.transpose(1, 0, 2, 3), 'kmom', 0, 0)  9.91 us
    ppermute x1, starting transfers between devices, self_energy_of(): beside = lax.ppermute(packed, 'energy', within)  8.87 us
    all_to_all x1, waiting for transfers between devices, self_energy_of(): back = lax.all_to_all(out, 'kmom', 0, 0).reshape(width, width)  6.92 us
    dot_general x7, matrix products, sweep(): mixed = jnp.matmul(left_block, inner, precision=high)  5.75 us
  transfers between devices with their start and end apart: 11, of which 10 were waited for; matrix products, arithmetic and copies ran while one was open for 3% of the time, Pallas kernels for 0%

profile of v8, /device:TPU:25, one launch (start us, length us, event | category | flops | bytes accessed | tf_op | source)
XLA Modules:
  0.0 168.0 jit_solution(801393708624329368)
XLA Ops:
  0.6 2.2 %collective-permute-start.1 = (f32[1,1,2,256,256]{4,3,2,1,0:T(8,128)}, f32[1,1,2,256,256]{4,3,2,1,0:T(8,128)S(1)}, u32[]{:S(2)}, u32[]{:S(2)}) collective-permute-start(f32[1,1,2,256,256]{4,3,2,1,0:T(8,128)} %bitcast.134), channel_id=1, source_target_pairs={{96,0},{192,96},{288,192},{384,288},{480,384},{576,480},{672,576},... | collective-permute-start | bytes 1572872 | tf_op jit(solution)/shard_map/ppermute | solution.py:10
  6.4 1.6 copy.35
  8.6 8.3 %collective-permute-done.1 = f32[1,1,2,256,256]{4,3,2,1,0:T(8,128)S(1)} collective-permute-done((f32[1,1,2,256,256]{4,3,2,1,0:T(8,128)}, f32[1,1,2,256,256]{4,3,2,1,0:T(8,128)S(1)}, u32[]{:S(2)}, u32[]{:S(2)}) %collective-permute-start.1) | collective-permute-done | bytes 524320 | tf_op jit(solution)/shard_map/ppermute | solution.py:10
  16.9 85.9 %while.10 = (s32[]{:T(128)}, f32[1,1,2,256,256]{4,3,2,1,0:T(8,128)S(1)}, f32[1,1,1,2,256,256]{5,4,3,2,1,0:T(8,128)S(1)}, f32[512,512]{1,0:T(8,128)S(1)}, f32[256,512]{1,0:T(8,128)S(1)}, /*index=5*/s32[]{:T(128)}) while((s32[]{:T(128)}, f32[1,1,2,256,256]{4,3,2,1,0:T(8,128)S(1)}, f32[1,1,1,2,256,256]{5,4,3,2,1,0:T(8,128)S(1)}, ...), condition=%wide.region_2.3_spmd, body=%wide.region_1.2_spmd.sunk | while | flops 805699584 | bytes 9437293 | solution.py:110
  18.3 1.9 %collective-permute-start = (f32[1,1,2,256,256]{4,3,2,1,0:T(8,128)S(1)}, f32[1,1,2,256,256]{4,3,2,1,0:T(8,128)S(1)}, u32[]{:S(2)}, u32[]{:S(2)}) collective-permute-start(f32[1,1,2,256,256]{4,3,2,1,0:T(8,128)S(1)} %maximum_add_fusion.4), channel_id=1, source_target_pairs={{96,0},{192,96},{288,192},{384,288},{480,384},{576,480},{672,576},... | collective-permute-start | bytes 1572872 | tf_op jit(solution)/shard_map/while/body/eval_jaxpr/ppermute | solution.py:10
  20.2 13.1 %collective-permute-done = f32[1,1,2,256,256]{4,3,2,1,0:T(8,128)S(1)} collective-permute-done((f32[1,1,2,256,256]{4,3,2,1,0:T(8,128)S(1)}, f32[1,1,2,256,256]{4,3,2,1,0:T(8,128)S(1)}, u32[]{:S(2)}, u32[]{:S(2)}) %collective-permute-start) | collective-permute-done | bytes 524320 | tf_op jit(solution)/shard_map/while/body/eval_jaxpr/ppermute | solution.py:10
  34.7 1.9 %collective-permute-start = (f32[1,1,2,256,256]{4,3,2,1,0:T(8,128)S(1)}, f32[1,1,2,256,256]{4,3,2,1,0:T(8,128)S(1)}, u32[]{:S(2)}, u32[]{:S(2)}) collective-permute-start(f32[1,1,2,256,256]{4,3,2,1,0:T(8,128)S(1)} %maximum_add_fusion.4), channel_id=1, source_target_pairs={{96,0},{192,96},{288,192},{384,288},{480,384},{576,480},{672,576},... | collective-permute-start | bytes 1572872 | tf_op jit(solution)/shard_map/while/body/eval_jaxpr/ppermute | solution.py:10
  36.6 12.3 %collective-permute-done = f32[1,1,2,256,256]{4,3,2,1,0:T(8,128)S(1)} collective-permute-done((f32[1,1,2,256,256]{4,3,2,1,0:T(8,128)S(1)}, f32[1,1,2,256,256]{4,3,2,1,0:T(8,128)S(1)}, u32[]{:S(2)}, u32[]{:S(2)}) %collective-permute-start) | collective-permute-done | bytes 524320 | tf_op jit(solution)/shard_map/while/body/eval_jaxpr/ppermute | solution.py:10
  50.2 1.9 %collective-permute-start = (f32[1,1,2,256,256]{4,3,2,1,0:T(8,128)S(1)}, f32[1,1,2,256,256]{4,3,2,1,0:T(8,128)S(1)}, u32[]{:S(2)}, u32[]{:S(2)}) collective-permute-start(f32[1,1,2,256,256]{4,3,2,1,0:T(8,128)S(1)} %maximum_add_fusion.4), channel_id=1, source_target_pairs={{96,0},{192,96},{288,192},{384,288},{480,384},{576,480},{672,576},... | collective-permute-start | bytes 1572872 | tf_op jit(solution)/shard_map/while/body/eval_jaxpr/ppermute | solution.py:10
  52.1 11.4 %collective-permute-done = f32[1,1,2,256,256]{4,3,2,1,0:T(8,128)S(1)} collective-permute-done((f32[1,1,2,256,256]{4,3,2,1,0:T(8,128)S(1)}, f32[1,1,2,256,256]{4,3,2,1,0:T(8,128)S(1)}, u32[]{:S(2)}, u32[]{:S(2)}) %collective-permute-start) | collective-permute-done | bytes 524320 | tf_op jit(solution)/shard_map/while/body/eval_jaxpr/ppermute | solution.py:10
  64.9 1.9 %collective-permute-start = (f32[1,1,2,256,256]{4,3,2,1,0:T(8,128)S(1)}, f32[1,1,2,256,256]{4,3,2,1,0:T(8,128)S(1)}, u32[]{:S(2)}, u32[]{:S(2)}) collective-permute-start(f32[1,1,2,256,256]{4,3,2,1,0:T(8,128)S(1)} %maximum_add_fusion.4), channel_id=1, source_target_pairs={{96,0},{192,96},{288,192},{384,288},{480,384},{576,480},{672,576},... | collective-permute-start | bytes 1572872 | tf_op jit(solution)/shard_map/while/body/eval_jaxpr/ppermute | solution.py:10
  66.8 10.6 %collective-permute-done = f32[1,1,2,256,256]{4,3,2,1,0:T(8,128)S(1)} collective-permute-done((f32[1,1,2,256,256]{4,3,2,1,0:T(8,128)S(1)}, f32[1,1,2,256,256]{4,3,2,1,0:T(8,128)S(1)}, u32[]{:S(2)}, u32[]{:S(2)}) %collective-permute-start) | collective-permute-done | bytes 524320 | tf_op jit(solution)/shard_map/while/body/eval_jaxpr/ppermute | solution.py:10
  78.7 1.9 %collective-permute-start = (f32[1,1,2,256,256]{4,3,2,1,0:T(8,128)S(1)}, f32[1,1,2,256,256]{4,3,2,1,0:T(8,128)S(1)}, u32[]{:S(2)}, u32[]{:S(2)}) collective-permute-start(f32[1,1,2,256,256]{4,3,2,1,0:T(8,128)S(1)} %maximum_add_fusion.4), channel_id=1, source_target_pairs={{96,0},{192,96},{288,192},{384,288},{480,384},{576,480},{672,576},... | collective-permute-start | bytes 1572872 | tf_op jit(solution)/shard_map/while/body/eval_jaxpr/ppermute | solution.py:10
  80.7 9.7 %collective-permute-done = f32[1,1,2,256,256]{4,3,2,1,0:T(8,128)S(1)} collective-permute-done((f32[1,1,2,256,256]{4,3,2,1,0:T(8,128)S(1)}, f32[1,1,2,256,256]{4,3,2,1,0:T(8,128)S(1)}, u32[]{:S(2)}, u32[]{:S(2)}) %collective-permute-start) | collective-permute-done | bytes 524320 | tf_op jit(solution)/shard_map/while/body/eval_jaxpr/ppermute | solution.py:10
  91.7 1.9 %collective-permute-start = (f32[1,1,2,256,256]{4,3,2,1,0:T(8,128)S(1)}, f32[1,1,2,256,256]{4,3,2,1,0:T(8,128)S(1)}, u32[]{:S(2)}, u32[]{:S(2)}) collective-permute-start(f32[1,1,2,256,256]{4,3,2,1,0:T(8,128)S(1)} %maximum_add_fusion.4), channel_id=1, source_target_pairs={{96,0},{192,96},{288,192},{384,288},{480,384},{576,480},{672,576},... | collective-permute-start | bytes 1572872 | tf_op jit(solution)/shard_map/while/body/eval_jaxpr/ppermute | solution.py:10
  93.7 9.2 %collective-permute-done = f32[1,1,2,256,256]{4,3,2,1,0:T(8,128)S(1)} collective-permute-done((f32[1,1,2,256,256]{4,3,2,1,0:T(8,128)S(1)}, f32[1,1,2,256,256]{4,3,2,1,0:T(8,128)S(1)}, u32[]{:S(2)}, u32[]{:S(2)}) %collective-permute-start) | collective-permute-done | bytes 524320 | tf_op jit(solution)/shard_map/while/body/eval_jaxpr/ppermute | solution.py:10
  102.9 2.2 %fusion.32 = f32[512,256]{1,0:T(8,128)S(1)} fusion(f32[512,512]{0,1:T(8,128)} %maximum_maximum_fusion, f32[512,256]{1,0:T(8,128)S(1)} %bitcast.136), kind=kOutput, calls=%fused_computation.64 | convolution fusion | flops 402653184 | bytes 2097152 | tf_op jit(solution)/shard_map/dot_general | solution.py:100
  106.2 8.9 %collective-permute-start.2 = (bf16[256,256]{1,0:T(8,128)(2,1)S(1)}, bf16[256,256]{1,0:T(8,128)(2,1)S(1)}, u32[]{:S(2)}, u32[]{:S(2)}) collective-permute-start(bf16[256,256]{1,0:T(8,128)(2,1)S(1)} %fusion.6), channel_id=1, source_target_pairs={{0,1},{1,0},{2,3},{3,2},{4,5},{5,4},{6,7},{7,6},{8,9},{9,8},{10,11... | collective-permute-start | bytes 393224 | tf_op jit(solution)/shard_map/ppermute | solution.py:49
  115.1 10.5 %collective-permute-start.3 = (bf16[256,256]{1,0:T(8,128)(2,1)S(1)}, bf16[256,256]{1,0:T(8,128)(2,1)S(1)}, u32[]{:S(2)}, u32[]{:S(2)}) collective-permute-start(bf16[256,256]{1,0:T(8,128)(2,1)S(1)} %fusion.6), channel_id=1, source_target_pairs={{1,2},{2,1},{3,4},{4,3},{7,8},{8,7},{9,10},{10,9},{13,14},{14,13},... | collective-permute-start | bytes 393224 | tf_op jit(solution)/shard_map/ppermute | solution.py:50
  125.7 2.6 %collective-permute-done.3 = bf16[256,256]{1,0:T(8,128)(2,1)S(1)} collective-permute-done((bf16[256,256]{1,0:T(8,128)(2,1)S(1)}, bf16[256,256]{1,0:T(8,128)(2,1)S(1)}, u32[]{:S(2)}, u32[]{:S(2)}) %collective-permute-start.3) | collective-permute-done | bytes 131104 | tf_op jit(solution)/shard_map/ppermute | solution.py:50
  129.1 13.5 %all-to-all-start = ((bf16[16,3,16,256]{3,2,1,0:T(8,128)(2,1)}), bf16[16,3,16,256]{3,2,1,0:T(8,128)(2,1)S(1)}, u32[]{:S(2)}, u32[]{:S(2)}) async-start(bf16[16,3,16,256]{3,2,1,0:T(8,128)(2,1)} %maximum_bitcast_fusion), calls=%async_computation | async-start | bytes 786432 | tf_op jit(solution)/shard_map/all_to_all | solution.py:52
  143.3 9.9 %all-to-all-done = bf16[16,3,16,256]{3,2,1,0:T(8,128)(2,1)S(1)} async-done(((bf16[16,3,16,256]{3,2,1,0:T(8,128)(2,1)}), bf16[16,3,16,256]{3,2,1,0:T(8,128)(2,1)S(1)}, u32[]{:S(2)}, u32[]{:S(2)}) %all-to-all-start) | async-done | bytes 393248 | tf_op jit(solution)/shard_map/all_to_all | solution.py:52
  155.5 3.7 %all-to-all-start.1 = ((bf16[16,16,256]{2,1,0:T(8,128)(2,1)}), bf16[16,16,256]{2,1,0:T(8,128)(2,1)S(1)}, u32[]{:S(2)}, u32[]{:S(2)}) async-start(bf16[16,16,256]{2,1,0:T(8,128)(2,1)} %bitcast.55), calls=%async_computation.1 | async-start | bytes 262144 | tf_op jit(solution)/shard_map/all_to_all | solution.py:64
  160.1 6.9 %all-to-all-done.1 = bf16[16,16,256]{2,1,0:T(8,128)(2,1)S(1)} async-done(((bf16[16,16,256]{2,1,0:T(8,128)(2,1)}), bf16[16,16,256]{2,1,0:T(8,128)(2,1)S(1)}, u32[]{:S(2)}, u32[]{:S(2)}) %all-to-all-start.1) | async-done | bytes 131104 | tf_op jit(solution)/shard_map/all_to_all | solution.py:64
  (64 shorter events, 18.0 us)
Async XLA Ops:
  0.6 2.3 %copy-start.3 = (s32[1,8,3]{1,0,2:T(1,128)S(1)}, s32[1,8,3]{1,0,2:T(1,128)}, u32[]{:S(2)}) copy-start(s32[1,8,3]{1,0,2:T(1,128)} %param.10) | copy-start | bytes 292
  0.6 2.4 %copy-start.1 = (f32[1,256,256]{2,1,0:T(8,128)S(1)}, f32[1,256,256]{2,1,0:T(8,128)}, u32[]{:S(2)}) copy-start(f32[1,256,256]{2,1,0:T(8,128)} %param.9) | copy-start | bytes 786436
  0.6 16.3 %collective-permute-start.1 = (f32[1,1,2,256,256]{4,3,2,1,0:T(8,128)}, f32[1,1,2,256,256]{4,3,2,1,0:T(8,128)S(1)}, u32[]{:S(2)}, u32[]{:S(2)}) collective-permute-start(f32[1,1,2,256,256]{4,3,2,1,0:T(8,128)} %bitcast.134), channel_id=1, source_target_pairs={{96,0},{192,96},{288,192},{384,288},{480,384},{576,480},{672,576},... | collective-permute-start | bytes 1572872 | tf_op jit(solution)/shard_map/ppermute | solution.py:10
  3.0 1.0 copy-start
  18.3 15.1 %collective-permute-start = (f32[1,1,2,256,256]{4,3,2,1,0:T(8,128)S(1)}, f32[1,1,2,256,256]{4,3,2,1,0:T(8,128)S(1)}, u32[]{:S(2)}, u32[]{:S(2)}) collective-permute-start(f32[1,1,2,256,256]{4,3,2,1,0:T(8,128)S(1)} %maximum_add_fusion.4), channel_id=1, source_target_pairs={{96,0},{192,96},{288,192},{384,288},{480,384},{576,480},{672,576},... | collective-permute-start | bytes 1572872 | tf_op jit(solution)/shard_map/while/body/eval_jaxpr/ppermute | solution.py:10
  34.7 14.2 %collective-permute-start = (f32[1,1,2,256,256]{4,3,2,1,0:T(8,128)S(1)}, f32[1,1,2,256,256]{4,3,2,1,0:T(8,128)S(1)}, u32[]{:S(2)}, u32[]{:S(2)}) collective-permute-start(f32[1,1,2,256,256]{4,3,2,1,0:T(8,128)S(1)} %maximum_add_fusion.4), channel_id=1, source_target_pairs={{96,0},{192,96},{288,192},{384,288},{480,384},{576,480},{672,576},... | collective-permute-start | bytes 1572872 | tf_op jit(solution)/shard_map/while/body/eval_jaxpr/ppermute | solution.py:10
  50.2 13.3 %collective-permute-start = (f32[1,1,2,256,256]{4,3,2,1,0:T(8,128)S(1)}, f32[1,1,2,256,256]{4,3,2,1,0:T(8,128)S(1)}, u32[]{:S(2)}, u32[]{:S(2)}) collective-permute-start(f32[1,1,2,256,256]{4,3,2,1,0:T(8,128)S(1)} %maximum_add_fusion.4), channel_id=1, source_target_pairs={{96,0},{192,96},{288,192},{384,288},{480,384},{576,480},{672,576},... | collective-permute-start | bytes 1572872 | tf_op jit(solution)/shard_map/while/body/eval_jaxpr/ppermute | solution.py:10
  64.9 12.5 %collective-permute-start = (f32[1,1,2,256,256]{4,3,2,1,0:T(8,128)S(1)}, f32[1,1,2,256,256]{4,3,2,1,0:T(8,128)S(1)}, u32[]{:S(2)}, u32[]{:S(2)}) collective-permute-start(f32[1,1,2,256,256]{4,3,2,1,0:T(8,128)S(1)} %maximum_add_fusion.4), channel_id=1, source_target_pairs={{96,0},{192,96},{288,192},{384,288},{480,384},{576,480},{672,576},... | collective-permute-start | bytes 1572872 | tf_op jit(solution)/shard_map/while/body/eval_jaxpr/ppermute | solution.py:10
  78.7 11.6 %collective-permute-start = (f32[1,1,2,256,256]{4,3,2,1,0:T(8,128)S(1)}, f32[1,1,2,256,256]{4,3,2,1,0:T(8,128)S(1)}, u32[]{:S(2)}, u32[]{:S(2)}) collective-permute-start(f32[1,1,2,256,256]{4,3,2,1,0:T(8,128)S(1)} %maximum_add_fusion.4), channel_id=1, source_target_pairs={{96,0},{192,96},{288,192},{384,288},{480,384},{576,480},{672,576},... | collective-permute-start | bytes 1572872 | tf_op jit(solution)/shard_map/while/body/eval_jaxpr/ppermute | solution.py:10
  91.7 11.1 %collective-permute-start = (f32[1,1,2,256,256]{4,3,2,1,0:T(8,128)S(1)}, f32[1,1,2,256,256]{4,3,2,1,0:T(8,128)S(1)}, u32[]{:S(2)}, u32[]{:S(2)}) collective-permute-start(f32[1,1,2,256,256]{4,3,2,1,0:T(8,128)S(1)} %maximum_add_fusion.4), channel_id=1, source_target_pairs={{96,0},{192,96},{288,192},{384,288},{480,384},{576,480},{672,576},... | collective-permute-start | bytes 1572872 | tf_op jit(solution)/shard_map/while/body/eval_jaxpr/ppermute | solution.py:10
  106.2 19.4 %collective-permute-start.2 = (bf16[256,256]{1,0:T(8,128)(2,1)S(1)}, bf16[256,256]{1,0:T(8,128)(2,1)S(1)}, u32[]{:S(2)}, u32[]{:S(2)}) collective-permute-start(bf16[256,256]{1,0:T(8,128)(2,1)S(1)} %fusion.6), channel_id=1, source_target_pairs={{0,1},{1,0},{2,3},{3,2},{4,5},{5,4},{6,7},{7,6},{8,9},{9,8},{10,11... | collective-permute-start | bytes 393224 | tf_op jit(solution)/shard_map/ppermute | solution.py:49
  115.1 13.2 %collective-permute-start.3 = (bf16[256,256]{1,0:T(8,128)(2,1)S(1)}, bf16[256,256]{1,0:T(8,128)(2,1)S(1)}, u32[]{:S(2)}, u32[]{:S(2)}) collective-permute-start(bf16[256,256]{1,0:T(8,128)(2,1)S(1)} %fusion.6), channel_id=1, source_target_pairs={{1,2},{2,1},{3,4},{4,3},{7,8},{8,7},{9,10},{10,9},{13,14},{14,13},... | collective-permute-start | bytes 393224 | tf_op jit(solution)/shard_map/ppermute | solution.py:50
  129.1 24.1 %all-to-all-start = ((bf16[16,3,16,256]{3,2,1,0:T(8,128)(2,1)}), bf16[16,3,16,256]{3,2,1,0:T(8,128)(2,1)S(1)}, u32[]{:S(2)}, u32[]{:S(2)}) async-start(bf16[16,3,16,256]{3,2,1,0:T(8,128)(2,1)} %maximum_bitcast_fusion), calls=%async_computation | async-start | bytes 786432 | tf_op jit(solution)/shard_map/all_to_all | solution.py:52
  142.6 0.7 copy-start.4
  153.4 0.7 copy-start.2
  155.5 11.5 %all-to-all-start.1 = ((bf16[16,16,256]{2,1,0:T(8,128)(2,1)}), bf16[16,16,256]{2,1,0:T(8,128)(2,1)S(1)}, u32[]{:S(2)}, u32[]{:S(2)}) async-start(bf16[16,16,256]{2,1,0:T(8,128)(2,1)} %bitcast.55), calls=%async_computation.1 | async-start | bytes 262144 | tf_op jit(solution)/shard_map/all_to_all | solution.py:64

commit v9 on v6

--- a/solution.py
+++ b/solution.py
@@ -103,7 +103,17 @@
     def advance(turn_index, beyond):
         return passed_along(sweep(beyond), "slab", -1)
 
-    first = passed_along(free_green[0], "slab", -1)
+    def held_back(block):
+        def spin(turn, acc):
+            return jnp.matmul(acc, acc, precision=high)
+
+        seed = lax.optimization_barrier(jnp.full((width, width), 1.0 / width, jnp.float32))
+        spun = lax.fori_loop(0, 14, spin, seed)
+        return block + spun[0, 0] * 0.0
+
+    late = lax.axis_index("energy") % 2 == 1
+    start_block = lax.cond(late, held_back, lambda block: block, free_green[0])
+    first = passed_along(start_block, "slab", -1)
     beyond = lax.fori_loop(0, lax.axis_size("slab") - 2, advance, first)
     green = sweep(beyond)
     self_energy = self_energy_of(green[0, 0], occupation, phonon_weight, phonon_mode)

time: 165 us -> 178 us (1.079)
  waiting for transfers between devices: 94.4 us -> 105 us
  starting transfers between devices: 47.3 us -> 43.1 us
  matrix products: 11.7 us -> 15.6 us
    ppermute x7, waiting for transfers between devices: 74.6 us -> 85.5 us  [passed_along(): return lax.ppermute(shard, axis, pairs)]
    ppermute x1, starting transfers between devices: 10.3 us -> 6.09 us  [self_energy_of(): beside = lax.ppermute(held, 'energy', within)]
    dot_general x0 -> x14, matrix products: none -> 3.9 us  [spin(): return jnp.matmul(acc, acc, precision=high)]
where the time goes in v9:
time: 178 us; the launch traced here: 177 us
  waiting for transfers between devices  105 us (59%)
  starting transfers between devices  43.1 us (24%)
  matrix products  15.6 us (9%)
  local copies, waits for them, and re-layouts  5.54 us (3%)
  other arithmetic  4.73 us (3%)
    ppermute x7, waiting for transfers between devices, passed_along(): return lax.ppermute(shard, axis, pairs)  85.5 us
    ppermute x7, starting transfers between devices, passed_along(): return lax.ppermute(shard, axis, pairs)  13.7 us
    ppermute x1, starting transfers between devices, self_energy_of(): facing = lax.ppermute(held, 'energy', across)  10.2 us
    all_to_all x1, starting transfers between devices, self_energy_of(): held = lax.all_to_all(packed.reshape(moms, rows, width), 'kmom', 0, 0)  9.56 us
    all_to_all x1, waiting for transfers between devices, self_energy_of(): held = lax.all_to_all(packed.reshape(moms, rows, width), 'kmom', 0, 0)  7.18 us
    all_to_all x1, waiting for transfers between devices, self_energy_of(): back = lax.all_to_all(out, 'kmom', 0, 0).reshape(width, width)  6.88 us
    ppermute x1, starting transfers between devices, self_energy_of(): beside = lax.ppermute(held, 'energy', within)  6.09 us
    ppermute x1, waiting for transfers between devices, self_energy_of(): facing = lax.ppermute(held, 'energy', across)  5.82 us
  transfers between devices with their start and end apart: 11, of which 10 were waited for; matrix products, arithmetic and copies ran while one was open for 3% of the time, Pallas kernels for 0%

profile of v9, /device:TPU:25, one launch (start us, length us, event | category | flops | bytes accessed | tf_op | source)
XLA Modules:
  0.0 177.4 jit_solution(2351206253239037390)
XLA Ops:
  0.7 6.0 %conditional.1 = (f32[1,1,2,256,256]{4,3,2,1,0:T(8,128)S(1)}) conditional(s32[]{:T(128)} %convert_element_type.31, f32[1,1,2,256,256]{4,3,2,1,0:T(8,128)} %bitcast.129, f32[1,1,2,256,256]{4,3,2,1,0:T(8,128)} %bitcast.130), branch_computations={%region_1.2_spmd, %region_2.5_spmd} | conditional | flops 100794368 | bytes 4456589 | solution.py:115
  0.7 4.6 %while.19 = (s32[]{:T(128)}, f32[256,256]{1,0:T(8,128)S(1)}, s32[]{:T(128)}) while((s32[]{:T(128)}, f32[256,256]{1,0:T(8,128)S(1)}, s32[]{:T(128)}) %tuple.56), condition=%wide.region_4.4_spmd, body=%wide.region_3.3_spmd.sunk | while | flops 100663296 | bytes 1048621 | solution.py:111
  6.7 2.2 %collective-permute-start.1 = (f32[1,1,2,256,256]{4,3,2,1,0:T(8,128)S(1)}, f32[1,1,2,256,256]{4,3,2,1,0:T(8,128)S(1)}, u32[]{:S(2)}, u32[]{:S(2)}) collective-permute-start(f32[1,1,2,256,256]{4,3,2,1,0:T(8,128)S(1)} %get-tuple-element.169), channel_id=1, source_target_pairs={{96,0},{192,96},{288,192},{384,288},{480,384},{576,480},{672,576},... | collective-permute-start | bytes 1572872 | tf_op jit(solution)/shard_map/ppermute | solution.py:10
  14.6 5.1 %collective-permute-done.1 = f32[1,1,2,256,256]{4,3,2,1,0:T(8,128)S(1)} collective-permute-done((f32[1,1,2,256,256]{4,3,2,1,0:T(8,128)S(1)}, f32[1,1,2,256,256]{4,3,2,1,0:T(8,128)S(1)}, u32[]{:S(2)}, u32[]{:S(2)}) %collective-permute-start.1) | collective-permute-done | bytes 524320 | tf_op jit(solution)/shard_map/ppermute | solution.py:10
  19.7 100.0 %while.20 = (s32[]{:T(128)}, f32[1,1,2,256,256]{4,3,2,1,0:T(8,128)S(1)}, f32[1,1,1,2,256,256]{5,4,3,2,1,0:T(8,128)S(1)}, f32[512,512]{1,0:T(8,128)S(1)}, f32[256,512]{1,0:T(8,128)S(1)}, /*index=5*/s32[]{:T(128)}) while((s32[]{:T(128)}, f32[1,1,2,256,256]{4,3,2,1,0:T(8,128)S(1)}, f32[1,1,1,2,256,256]{5,4,3,2,1,0:T(8,128)S(1)}, ...), condition=%wide.region_6.7_spmd, body=%wide.region_5.6_spmd.sunk | while | flops 805699584 | bytes 9437293 | solution.py:117
  21.1 1.9 %collective-permute-start = (f32[1,1,2,256,256]{4,3,2,1,0:T(8,128)S(1)}, f32[1,1,2,256,256]{4,3,2,1,0:T(8,128)S(1)}, u32[]{:S(2)}, u32[]{:S(2)}) collective-permute-start(f32[1,1,2,256,256]{4,3,2,1,0:T(8,128)S(1)} %maximum_add_fusion.4), channel_id=1, source_target_pairs={{96,0},{192,96},{288,192},{384,288},{480,384},{576,480},{672,576},... | collective-permute-start | bytes 1572872 | tf_op jit(solution)/shard_map/while/body/eval_jaxpr/ppermute | solution.py:10
  23.0 12.1 %collective-permute-done = f32[1,1,2,256,256]{4,3,2,1,0:T(8,128)S(1)} collective-permute-done((f32[1,1,2,256,256]{4,3,2,1,0:T(8,128)S(1)}, f32[1,1,2,256,256]{4,3,2,1,0:T(8,128)S(1)}, u32[]{:S(2)}, u32[]{:S(2)}) %collective-permute-start) | collective-permute-done | bytes 524320 | tf_op jit(solution)/shard_map/while/body/eval_jaxpr/ppermute | solution.py:10
  36.5 1.9 %collective-permute-start = (f32[1,1,2,256,256]{4,3,2,1,0:T(8,128)S(1)}, f32[1,1,2,256,256]{4,3,2,1,0:T(8,128)S(1)}, u32[]{:S(2)}, u32[]{:S(2)}) collective-permute-start(f32[1,1,2,256,256]{4,3,2,1,0:T(8,128)S(1)} %maximum_add_fusion.4), channel_id=1, source_target_pairs={{96,0},{192,96},{288,192},{384,288},{480,384},{576,480},{672,576},... | collective-permute-start | bytes 1572872 | tf_op jit(solution)/shard_map/while/body/eval_jaxpr/ppermute | solution.py:10
  38.4 13.3 %collective-permute-done = f32[1,1,2,256,256]{4,3,2,1,0:T(8,128)S(1)} collective-permute-done((f32[1,1,2,256,256]{4,3,2,1,0:T(8,128)S(1)}, f32[1,1,2,256,256]{4,3,2,1,0:T(8,128)S(1)}, u32[]{:S(2)}, u32[]{:S(2)}) %collective-permute-start) | collective-permute-done | bytes 524320 | tf_op jit(solution)/shard_map/while/body/eval_jaxpr/ppermute | solution.py:10
  53.1 1.9 %collective-permute-start = (f32[1,1,2,256,256]{4,3,2,1,0:T(8,128)S(1)}, f32[1,1,2,256,256]{4,3,2,1,0:T(8,128)S(1)}, u32[]{:S(2)}, u32[]{:S(2)}) collective-permute-start(f32[1,1,2,256,256]{4,3,2,1,0:T(8,128)S(1)} %maximum_add_fusion.4), channel_id=1, source_target_pairs={{96,0},{192,96},{288,192},{384,288},{480,384},{576,480},{672,576},... | collective-permute-start | bytes 1572872 | tf_op jit(solution)/shard_map/while/body/eval_jaxpr/ppermute | solution.py:10
  55.0 14.4 %collective-permute-done = f32[1,1,2,256,256]{4,3,2,1,0:T(8,128)S(1)} collective-permute-done((f32[1,1,2,256,256]{4,3,2,1,0:T(8,128)S(1)}, f32[1,1,2,256,256]{4,3,2,1,0:T(8,128)S(1)}, u32[]{:S(2)}, u32[]{:S(2)}) %collective-permute-start) | collective-permute-done | bytes 524320 | tf_op jit(solution)/shard_map/while/body/eval_jaxpr/ppermute | solution.py:10
  70.8 1.9 %collective-permute-start = (f32[1,1,2,256,256]{4,3,2,1,0:T(8,128)S(1)}, f32[1,1,2,256,256]{4,3,2,1,0:T(8,128)S(1)}, u32[]{:S(2)}, u32[]{:S(2)}) collective-permute-start(f32[1,1,2,256,256]{4,3,2,1,0:T(8,128)S(1)} %maximum_add_fusion.4), channel_id=1, source_target_pairs={{96,0},{192,96},{288,192},{384,288},{480,384},{576,480},{672,576},... | collective-permute-start | bytes 1572872 | tf_op jit(solution)/shard_map/while/body/eval_jaxpr/ppermute | solution.py:10
  72.7 14.4 %collective-permute-done = f32[1,1,2,256,256]{4,3,2,1,0:T(8,128)S(1)} collective-permute-done((f32[1,1,2,256,256]{4,3,2,1,0:T(8,128)S(1)}, f32[1,1,2,256,256]{4,3,2,1,0:T(8,128)S(1)}, u32[]{:S(2)}, u32[]{:S(2)}) %collective-permute-start) | collective-permute-done | bytes 524320 | tf_op jit(solution)/shard_map/while/body/eval_jaxpr/ppermute | solution.py:10
  90.3 13.5 %collective-permute-done = f32[1,1,2,256,256]{4,3,2,1,0:T(8,128)S(1)} collective-permute-done((f32[1,1,2,256,256]{4,3,2,1,0:T(8,128)S(1)}, f32[1,1,2,256,256]{4,3,2,1,0:T(8,128)S(1)}, u32[]{:S(2)}, u32[]{:S(2)}) %collective-permute-start) | collective-permute-done | bytes 524320 | tf_op jit(solution)/shard_map/while/body/eval_jaxpr/ppermute | solution.py:10
  105.2 1.9 %collective-permute-start = (f32[1,1,2,256,256]{4,3,2,1,0:T(8,128)S(1)}, f32[1,1,2,256,256]{4,3,2,1,0:T(8,128)S(1)}, u32[]{:S(2)}, u32[]{:S(2)}) collective-permute-start(f32[1,1,2,256,256]{4,3,2,1,0:T(8,128)S(1)} %maximum_add_fusion.4), channel_id=1, source_target_pairs={{96,0},{192,96},{288,192},{384,288},{480,384},{576,480},{672,576},... | collective-permute-start | bytes 1572872 | tf_op jit(solution)/shard_map/while/body/eval_jaxpr/ppermute | solution.py:10
  107.1 12.6 %collective-permute-done = f32[1,1,2,256,256]{4,3,2,1,0:T(8,128)S(1)} collective-permute-done((f32[1,1,2,256,256]{4,3,2,1,0:T(8,128)S(1)}, f32[1,1,2,256,256]{4,3,2,1,0:T(8,128)S(1)}, u32[]{:S(2)}, u32[]{:S(2)}) %collective-permute-start) | collective-permute-done | bytes 524320 | tf_op jit(solution)/shard_map/while/body/eval_jaxpr/ppermute | solution.py:10
  119.8 2.2 %fusion.33 = f32[512,256]{1,0:T(8,128)S(1)} fusion(f32[512,512]{0,1:T(8,128)} %maximum_maximum_fusion, f32[512,256]{1,0:T(8,128)S(1)} %bitcast.132), kind=kOutput, calls=%fused_computation.65 | convolution fusion | flops 402653184 | bytes 2097152 | tf_op jit(solution)/shard_map/dot_general | solution.py:97
  123.8 9.6 %all-to-all-start = ((bf16[16,16,256]{2,1,0:T(8,128)(2,1)}), bf16[16,16,256]{2,1,0:T(8,128)(2,1)S(1)}, u32[]{:S(2)}, u32[]{:S(2)}) async-start(bf16[16,16,256]{2,1,0:T(8,128)(2,1)} %bitcast.27), calls=%async_computation | async-start | bytes 262144 | tf_op jit(solution)/shard_map/all_to_all | solution.py:45
  134.1 7.2 %all-to-all-done = bf16[16,16,256]{2,1,0:T(8,128)(2,1)S(1)} async-done(((bf16[16,16,256]{2,1,0:T(8,128)(2,1)}), bf16[16,16,256]{2,1,0:T(8,128)(2,1)S(1)}, u32[]{:S(2)}, u32[]{:S(2)}) %all-to-all-start) | async-done | bytes 131104 | tf_op jit(solution)/shard_map/all_to_all | solution.py:45
  141.5 6.1 %collective-permute-start.2 = (bf16[16,16,256]{2,1,0:T(8,128)(2,1)S(1)}, bf16[16,16,256]{2,1,0:T(8,128)(2,1)S(1)}, u32[]{:S(2)}, u32[]{:S(2)}) collective-permute-start(bf16[16,16,256]{2,1,0:T(8,128)(2,1)S(1)} %all-to-all-done), channel_id=1, source_target_pairs={{0,1},{1,0},{2,3},{3,2},{4,5},{5,4},{6,7},{7,6},{8,9},{9,8},{10,11... | collective-permute-start | bytes 393224 | tf_op jit(solution)/shard_map/ppermute | solution.py:50
  147.6 10.2 %collective-permute-start.3 = (bf16[16,16,256]{2,1,0:T(8,128)(2,1)S(1)}, bf16[16,16,256]{2,1,0:T(8,128)(2,1)S(1)}, u32[]{:S(2)}, u32[]{:S(2)}) collective-permute-start(bf16[16,16,256]{2,1,0:T(8,128)(2,1)S(1)} %all-to-all-done), channel_id=1, source_target_pairs={{1,2},{2,1},{3,4},{4,3},{7,8},{8,7},{9,10},{10,9},{13,14},{14,13},... | collective-permute-start | bytes 393224 | tf_op jit(solution)/shard_map/ppermute | solution.py:51
  158.2 5.8 %collective-permute-done.3 = bf16[16,16,256]{2,1,0:T(8,128)(2,1)S(1)} collective-permute-done((bf16[16,16,256]{2,1,0:T(8,128)(2,1)S(1)}, bf16[16,16,256]{2,1,0:T(8,128)(2,1)S(1)}, u32[]{:S(2)}, u32[]{:S(2)}) %collective-permute-start.3) | collective-permute-done | bytes 131104 | tf_op jit(solution)/shard_map/ppermute | solution.py:51
  165.2 3.5 %all-to-all-start.1 = ((bf16[16,16,256]{2,1,0:T(8,128)(2,1)}), bf16[16,16,256]{2,1,0:T(8,128)(2,1)S(1)}, u32[]{:S(2)}, u32[]{:S(2)}) async-start(bf16[16,16,256]{2,1,0:T(8,128)(2,1)} %bitcast.45), calls=%async_computation.1 | async-start | bytes 262144 | tf_op jit(solution)/shard_map/all_to_all | solution.py:61
  169.6 6.9 %all-to-all-done.1 = bf16[16,16,256]{2,1,0:T(8,128)(2,1)S(1)} async-done(((bf16[16,16,256]{2,1,0:T(8,128)(2,1)}), bf16[16,16,256]{2,1,0:T(8,128)(2,1)S(1)}, u32[]{:S(2)}, u32[]{:S(2)}) %all-to-all-start.1) | async-done | bytes 131104 | tf_op jit(solution)/shard_map/all_to_all | solution.py:61
  (99 shorter events, 25.6 us)
Async XLA Ops:
  0.7 8.3 %copy-start.4 = (s32[1,8,3]{1,0,2:T(1,128)S(1)}, s32[1,8,3]{1,0,2:T(1,128)}, u32[]{:S(2)}) copy-start(s32[1,8,3]{1,0,2:T(1,128)} %param.14) | copy-start | bytes 292
  0.7 5.9 %copy-start.1 = (f32[1,1,2,256,256]{4,3,2,1,0:T(8,128)S(1)}, f32[1,1,2,256,256]{4,3,2,1,0:T(8,128)}, u32[]{:S(2)}) copy-start(f32[1,1,2,256,256]{4,3,2,1,0:T(8,128)} %param.3) | copy-start | bytes 1572868 | tf_op jit(solution)/shard_map/cond
  6.7 2.4 %copy-start.2 = (f32[1,256,256]{2,1,0:T(8,128)S(1)}, f32[1,256,256]{2,1,0:T(8,128)}, u32[]{:S(2)}) copy-start(f32[1,256,256]{2,1,0:T(8,128)} %param.13) | copy-start | bytes 786436
  6.7 13.1 %collective-permute-start.1 = (f32[1,1,2,256,256]{4,3,2,1,0:T(8,128)S(1)}, f32[1,1,2,256,256]{4,3,2,1,0:T(8,128)S(1)}, u32[]{:S(2)}, u32[]{:S(2)}) collective-permute-start(f32[1,1,2,256,256]{4,3,2,1,0:T(8,128)S(1)} %get-tuple-element.169), channel_id=1, source_target_pairs={{96,0},{192,96},{288,192},{384,288},{480,384},{576,480},{672,576},... | collective-permute-start | bytes 1572872 | tf_op jit(solution)/shard_map/ppermute | solution.py:10
  9.0 1.0 copy-start
  21.1 14.1 %collective-permute-start = (f32[1,1,2,256,256]{4,3,2,1,0:T(8,128)S(1)}, f32[1,1,2,256,256]{4,3,2,1,0:T(8,128)S(1)}, u32[]{:S(2)}, u32[]{:S(2)}) collective-permute-start(f32[1,1,2,256,256]{4,3,2,1,0:T(8,128)S(1)} %maximum_add_fusion.4), channel_id=1, source_target_pairs={{96,0},{192,96},{288,192},{384,288},{480,384},{576,480},{672,576},... | collective-permute-start | bytes 1572872 | tf_op jit(solution)/shard_map/while/body/eval_jaxpr/ppermute | solution.py:10
  36.5 15.2 %collective-permute-start = (f32[1,1,2,256,256]{4,3,2,1,0:T(8,128)S(1)}, f32[1,1,2,256,256]{4,3,2,1,0:T(8,128)S(1)}, u32[]{:S(2)}, u32[]{:S(2)}) collective-permute-start(f32[1,1,2,256,256]{4,3,2,1,0:T(8,128)S(1)} %maximum_add_fusion.4), channel_id=1, source_target_pairs={{96,0},{192,96},{288,192},{384,288},{480,384},{576,480},{672,576},... | collective-permute-start | bytes 1572872 | tf_op jit(solution)/shard_map/while/body/eval_jaxpr/ppermute | solution.py:10
  53.1 16.4 %collective-permute-start = (f32[1,1,2,256,256]{4,3,2,1,0:T(8,128)S(1)}, f32[1,1,2,256,256]{4,3,2,1,0:T(8,128)S(1)}, u32[]{:S(2)}, u32[]{:S(2)}) collective-permute-start(f32[1,1,2,256,256]{4,3,2,1,0:T(8,128)S(1)} %maximum_add_fusion.4), channel_id=1, source_target_pairs={{96,0},{192,96},{288,192},{384,288},{480,384},{576,480},{672,576},... | collective-permute-start | bytes 1572872 | tf_op jit(solution)/shard_map/while/body/eval_jaxpr/ppermute | solution.py:10
  70.8 16.3 %collective-permute-start = (f32[1,1,2,256,256]{4,3,2,1,0:T(8,128)S(1)}, f32[1,1,2,256,256]{4,3,2,1,0:T(8,128)S(1)}, u32[]{:S(2)}, u32[]{:S(2)}) collective-permute-start(f32[1,1,2,256,256]{4,3,2,1,0:T(8,128)S(1)} %maximum_add_fusion.4), channel_id=1, source_target_pairs={{96,0},{192,96},{288,192},{384,288},{480,384},{576,480},{672,576},... | collective-permute-start | bytes 1572872 | tf_op jit(solution)/shard_map/while/body/eval_jaxpr/ppermute | solution.py:10
  88.4 15.4 %collective-permute-start = (f32[1,1,2,256,256]{4,3,2,1,0:T(8,128)S(1)}, f32[1,1,2,256,256]{4,3,2,1,0:T(8,128)S(1)}, u32[]{:S(2)}, u32[]{:S(2)}) collective-permute-start(f32[1,1,2,256,256]{4,3,2,1,0:T(8,128)S(1)} %maximum_add_fusion.4), channel_id=1, source_target_pairs={{96,0},{192,96},{288,192},{384,288},{480,384},{576,480},{672,576},... | collective-permute-start | bytes 1572872 | tf_op jit(solution)/shard_map/while/body/eval_jaxpr/ppermute | solution.py:10
  105.2 14.6 %collective-permute-start = (f32[1,1,2,256,256]{4,3,2,1,0:T(8,128)S(1)}, f32[1,1,2,256,256]{4,3,2,1,0:T(8,128)S(1)}, u32[]{:S(2)}, u32[]{:S(2)}) collective-permute-start(f32[1,1,2,256,256]{4,3,2,1,0:T(8,128)S(1)} %maximum_add_fusion.4), channel_id=1, source_target_pairs={{96,0},{192,96},{288,192},{384,288},{480,384},{576,480},{672,576},... | collective-permute-start | bytes 1572872 | tf_op jit(solution)/shard_map/while/body/eval_jaxpr/ppermute | solution.py:10
  123.8 17.4 %all-to-all-start = ((bf16[16,16,256]{2,1,0:T(8,128)(2,1)}), bf16[16,16,256]{2,1,0:T(8,128)(2,1)S(1)}, u32[]{:S(2)}, u32[]{:S(2)}) async-start(bf16[16,16,256]{2,1,0:T(8,128)(2,1)} %bitcast.27), calls=%async_computation | async-start | bytes 262144 | tf_op jit(solution)/shard_map/all_to_all | solution.py:45
  133.4 0.7 copy-start.5
  141.3 16.5 %copy-start.3 = (f32[2,16,16]{2,1,0:T(8,128)S(1)}, f32[2,16,16]{2,1,0:T(8,128)}, u32[]{:S(2)}) copy-start(f32[2,16,16]{2,1,0:T(8,128)} %param.16) | copy-start | bytes 6148
  141.5 16.7 %collective-permute-start.2 = (bf16[16,16,256]{2,1,0:T(8,128)(2,1)S(1)}, bf16[16,16,256]{2,1,0:T(8,128)(2,1)S(1)}, u32[]{:S(2)}, u32[]{:S(2)}) collective-permute-start(bf16[16,16,256]{2,1,0:T(8,128)(2,1)S(1)} %all-to-all-done), channel_id=1, source_target_pairs={{0,1},{1,0},{2,3},{3,2},{4,5},{5,4},{6,7},{7,6},{8,9},{9,8},{10,11... | collective-permute-start | bytes 393224 | tf_op jit(solution)/shard_map/ppermute | solution.py:50
  147.6 16.4 %collective-permute-start.3 = (bf16[16,16,256]{2,1,0:T(8,128)(2,1)S(1)}, bf16[16,16,256]{2,1,0:T(8,128)(2,1)S(1)}, u32[]{:S(2)}, u32[]{:S(2)}) collective-permute-start(bf16[16,16,256]{2,1,0:T(8,128)(2,1)S(1)} %all-to-all-done), channel_id=1, source_target_pairs={{1,2},{2,1},{3,4},{4,3},{7,8},{8,7},{9,10},{10,9},{13,14},{14,13},... | collective-permute-start | bytes 393224 | tf_op jit(solution)/shard_map/ppermute | solution.py:51
  165.2 11.3 %all-to-all-start.1 = ((bf16[16,16,256]{2,1,0:T(8,128)(2,1)}), bf16[16,16,256]{2,1,0:T(8,128)(2,1)S(1)}, u32[]{:S(2)}, u32[]{:S(2)}) async-start(bf16[16,16,256]{2,1,0:T(8,128)(2,1)} %bitcast.45), calls=%async_computation.1 | async-start | bytes 262144 | tf_op jit(solution)/shard_map/all_to_all | solution.py:61

commit v10 on v6

--- a/solution.py
+++ b/solution.py
@@ -100,11 +100,15 @@
         imag_part = outer[:width, width:] + outer[width:, :width]
         return free_green[0] + jnp.stack([real_part, imag_part], axis=0)[None, None]
 
-    def advance(turn_index, beyond):
-        return passed_along(sweep(beyond), "slab", -1)
-
-    first = passed_along(free_green[0], "slab", -1)
-    beyond = lax.fori_loop(0, lax.axis_size("slab") - 2, advance, first)
+    slabs = lax.axis_size("slab")
+    slab = lax.axis_index("slab")
+    beyond = jnp.zeros(free_green.shape[1:], jnp.float32)
+    sent = free_green[0]
+    for source in range(slabs - 1, 0, -1):
+        if source < slabs - 1:
+            sent = sweep(beyond)
+        arrived = lax.ppermute(sent, "slab", [(source, source - 1)])
+        beyond = jnp.where(slab == source - 1, arrived, beyond)
     green = sweep(beyond)
     self_energy = self_energy_of(green[0, 0], occupation, phonon_weight, phonon_mode)
     return green[None], self_energy.reshape(green.shape)[None]

time: 165 us -> 167 us (1.012)
  the two profiles are of different devices: /device:TPU:25 before, /device:TPU:1 now
where the time goes in v10:
time: 167 us
  waiting for transfers between devices  100 us (60%)
  starting transfers between devices  41.1 us (25%)
  matrix products  12.9 us (8%)
  other arithmetic  7.58 us (5%)
  local copies, waits for them, and re-layouts  3.12 us (2%)
  between operations  1.87 us (1%)
    ppermute x7, waiting for transfers between devices, on_device(): arrived = lax.ppermute(sent, 'slab', [(source, source - 1)])  80.4 us
    ppermute x1, starting transfers between devices, self_energy_of(): facing = lax.ppermute(held, 'energy', across)  10.3 us
    all_to_all x1, starting transfers between devices, self_energy_of(): held = lax.all_to_all(packed.reshape(moms, rows, width), 'kmom', 0, 0)  9.52 us
    ppermute x7, starting transfers between devices, on_device(): arrived = lax.ppermute(sent, 'slab', [(source, source - 1)])  9.49 us
    ppermute x1, starting transfers between devices, self_energy_of(): beside = lax.ppermute(held, 'energy', within)  8.33 us
    all_to_all x1, waiting for transfers between devices, self_energy_of(): held = lax.all_to_all(packed.reshape(moms, rows, width), 'kmom', 0, 0)  7.08 us
    dot_general x7, matrix products, sweep(): mixed = jnp.matmul(left_block, inner, precision=high)  7.02 us
    all_to_all x1, waiting for transfers between devices, self_energy_of(): back = lax.all_to_all(out, 'kmom', 0, 0).reshape(width, width)  6.88 us
  transfers between devices with their start and end apart: 11, of which 4 were waited for; matrix products, arithmetic and copies ran while one was open for 2% of the time, Pallas kernels for 0%

profile of v10, /device:TPU:1, one launch (start us, length us, event | category | flops | bytes accessed | tf_op | source)
XLA Modules:
  0.0 166.8 jit_solution(17651424527934462285)
XLA Ops:
  1.7 1.0 copy-done
  2.6 1.0 convolution_bitcast_fusion
  4.0 1.0 fusion.40
  5.8 1.5 collective-permute-start.1
  7.4 1.0 fusion.42
  9.9 1.5 collective-permute-start.2
  11.5 1.0 fusion.44
  13.2 1.5 collective-permute-start.3
  14.8 1.0 fusion.46
  17.3 1.5 collective-permute-start.4
  18.9 1.0 fusion.48
  21.5 1.5 collective-permute-start.5
  23.0 1.0 fusion.50
  24.8 1.3 collective-permute-start.6
  26.7 80.4 %collective-permute-done.6 = f32[1,1,2,256,256]{4,3,2,1,0:T(8,128)} collective-permute-done((f32[1,1,2,256,256]{4,3,2,1,0:T(8,128)S(1)}, f32[1,1,2,256,256]{4,3,2,1,0:T(8,128)}, u32[]{:S(2)}, u32[]{:S(2)}) %collective-permute-start.6) | collective-permute-done | bytes 524320 | tf_op jit(solution)/shard_map/ppermute | solution.py:110
  107.1 1.1 broadcast_select_fusion.6
  108.3 1.0 fusion.52
  111.1 9.5 %all-to-all-start = ((bf16[16,16,256]{2,1,0:T(8,128)(2,1)}), bf16[16,16,256]{2,1,0:T(8,128)(2,1)S(1)}, u32[]{:S(2)}, u32[]{:S(2)}) async-start(bf16[16,16,256]{2,1,0:T(8,128)(2,1)} %bitcast.40), calls=%async_computation | async-start | bytes 262144 | tf_op jit(solution)/shard_map/all_to_all | solution.py:45
  121.3 7.1 %all-to-all-done = bf16[16,16,256]{2,1,0:T(8,128)(2,1)S(1)} async-done(((bf16[16,16,256]{2,1,0:T(8,128)(2,1)}), bf16[16,16,256]{2,1,0:T(8,128)(2,1)S(1)}, u32[]{:S(2)}, u32[]{:S(2)}) %all-to-all-start) | async-done | bytes 131104 | tf_op jit(solution)/shard_map/all_to_all | solution.py:45
  128.6 8.3 %collective-permute-start.7 = (bf16[16,16,256]{2,1,0:T(8,128)(2,1)S(1)}, bf16[16,16,256]{2,1,0:T(8,128)(2,1)S(1)}, u32[]{:S(2)}, u32[]{:S(2)}) collective-permute-start(bf16[16,16,256]{2,1,0:T(8,128)(2,1)S(1)} %all-to-all-done), channel_id=1, source_target_pairs={{0,1},{1,0},{2,3},{3,2},{4,5},{5,4},{6,7},{7,6},{8,9},{9,8},{10,11... | collective-permute-start | bytes 393224 | tf_op jit(solution)/shard_map/ppermute | solution.py:50
  136.9 10.3 %collective-permute-start.8 = (bf16[16,16,256]{2,1,0:T(8,128)(2,1)S(1)}, bf16[16,16,256]{2,1,0:T(8,128)(2,1)S(1)}, u32[]{:S(2)}, u32[]{:S(2)}) collective-permute-start(bf16[16,16,256]{2,1,0:T(8,128)(2,1)S(1)} %all-to-all-done), channel_id=1, source_target_pairs={{1,2},{2,1},{3,4},{4,3},{7,8},{8,7},{9,10},{10,9},{13,14},{14,13},... | collective-permute-start | bytes 393224 | tf_op jit(solution)/shard_map/ppermute | solution.py:51
  147.6 5.8 %collective-permute-done.8 = bf16[16,16,256]{2,1,0:T(8,128)(2,1)S(1)} collective-permute-done((bf16[16,16,256]{2,1,0:T(8,128)(2,1)S(1)}, bf16[16,16,256]{2,1,0:T(8,128)(2,1)S(1)}, u32[]{:S(2)}, u32[]{:S(2)}) %collective-permute-start.8) | collective-permute-done | bytes 131104 | tf_op jit(solution)/shard_map/ppermute | solution.py:51
  154.6 3.5 %all-to-all-start.1 = ((bf16[16,16,256]{2,1,0:T(8,128)(2,1)}), bf16[16,16,256]{2,1,0:T(8,128)(2,1)S(1)}, u32[]{:S(2)}, u32[]{:S(2)}) async-start(bf16[16,16,256]{2,1,0:T(8,128)(2,1)} %bitcast.58), calls=%async_computation.1 | async-start | bytes 262144 | tf_op jit(solution)/shard_map/all_to_all | solution.py:61
  159.0 6.9 %all-to-all-done.1 = bf16[16,16,256]{2,1,0:T(8,128)(2,1)S(1)} async-done(((bf16[16,16,256]{2,1,0:T(8,128)(2,1)}), bf16[16,16,256]{2,1,0:T(8,128)(2,1)S(1)}, u32[]{:S(2)}, u32[]{:S(2)}) %all-to-all-start.1) | async-done | bytes 131104 | tf_op jit(solution)/shard_map/all_to_all | solution.py:61
  (73 shorter events, 14.3 us)
Async XLA Ops:
  0.6 0.9 copy-start.5
  0.6 1.0 copy-start.3
  0.6 3.3 %collective-permute-start = (f32[1,1,2,256,256]{4,3,2,1,0:T(8,128)}, f32[1,1,2,256,256]{4,3,2,1,0:T(8,128)S(1)}, u32[]{:S(2)}, u32[]{:S(2)}) collective-permute-start(f32[1,1,2,256,256]{4,3,2,1,0:T(8,128)} %bitcast.157), channel_id=1, source_target_pairs={{672,576},{673,577},{674,578},{675,579},{676,580},{677,581},{678,5... | collective-permute-start | bytes 1572872 | tf_op jit(solution)/shard_map/ppermute | solution.py:110
  1.6 1.0 copy-start
  5.8 1.5 collective-permute-start.1
  9.9 1.5 collective-permute-start.2
  13.2 1.5 collective-permute-start.3
  17.3 1.5 collective-permute-start.4
  18.9 1.0 copy-start.1
  20.6 2.3 %copy-start.2 = (f32[1,1,2,256,256]{4,3,2,1,0:T(8,128)S(1)}, f32[1,1,2,256,256]{4,3,2,1,0:T(8,128)}, u32[]{:S(2)}) copy-start(f32[1,1,2,256,256]{4,3,2,1,0:T(8,128)} %copy-done.1) | copy-start | bytes 1572868
  21.5 1.5 collective-permute-start.5
  24.8 82.4 %collective-permute-start.6 = (f32[1,1,2,256,256]{4,3,2,1,0:T(8,128)S(1)}, f32[1,1,2,256,256]{4,3,2,1,0:T(8,128)}, u32[]{:S(2)}, u32[]{:S(2)}) collective-permute-start(f32[1,1,2,256,256]{4,3,2,1,0:T(8,128)S(1)} %maximum_add_fusion.5), channel_id=1, source_target_pairs={{96,0},{97,1},{98,2},{99,3},{100,4},{101,5},{102,6},{103,7},{104,8... | collective-permute-start | bytes 1572872 | tf_op jit(solution)/shard_map/ppermute | solution.py:110
  111.1 17.3 %all-to-all-start = ((bf16[16,16,256]{2,1,0:T(8,128)(2,1)}), bf16[16,16,256]{2,1,0:T(8,128)(2,1)S(1)}, u32[]{:S(2)}, u32[]{:S(2)}) async-start(bf16[16,16,256]{2,1,0:T(8,128)(2,1)} %bitcast.40), calls=%async_computation | async-start | bytes 262144 | tf_op jit(solution)/shard_map/all_to_all | solution.py:45
  120.6 0.7 copy-start.6
  128.4 18.8 %copy-start.4 = (f32[2,16,16]{2,1,0:T(8,128)S(1)}, f32[2,16,16]{2,1,0:T(8,128)}, u32[]{:S(2)}) copy-start(f32[2,16,16]{2,1,0:T(8,128)} %param.10) | copy-start | bytes 6148
  128.6 19.0 %collective-permute-start.7 = (bf16[16,16,256]{2,1,0:T(8,128)(2,1)S(1)}, bf16[16,16,256]{2,1,0:T(8,128)(2,1)S(1)}, u32[]{:S(2)}, u32[]{:S(2)}) collective-permute-start(bf16[16,16,256]{2,1,0:T(8,128)(2,1)S(1)} %all-to-all-done), channel_id=1, source_target_pairs={{0,1},{1,0},{2,3},{3,2},{4,5},{5,4},{6,7},{7,6},{8,9},{9,8},{10,11... | collective-permute-start | bytes 393224 | tf_op jit(solution)/shard_map/ppermute | solution.py:50
  136.9 16.5 %collective-permute-start.8 = (bf16[16,16,256]{2,1,0:T(8,128)(2,1)S(1)}, bf16[16,16,256]{2,1,0:T(8,128)(2,1)S(1)}, u32[]{:S(2)}, u32[]{:S(2)}) collective-permute-start(bf16[16,16,256]{2,1,0:T(8,128)(2,1)S(1)} %all-to-all-done), channel_id=1, source_target_pairs={{1,2},{2,1},{3,4},{4,3},{7,8},{8,7},{9,10},{10,9},{13,14},{14,13},... | collective-permute-start | bytes 393224 | tf_op jit(solution)/shard_map/ppermute | solution.py:51
  154.6 11.3 %all-to-all-start.1 = ((bf16[16,16,256]{2,1,0:T(8,128)(2,1)}), bf16[16,16,256]{2,1,0:T(8,128)(2,1)S(1)}, u32[]{:S(2)}, u32[]{:S(2)}) async-start(bf16[16,16,256]{2,1,0:T(8,128)(2,1)} %bitcast.58), calls=%async_computation.1 | async-start | bytes 262144 | tf_op jit(solution)/shard_map/all_to_all | solution.py:61

commit v11 on v6

--- a/solution.py
+++ b/solution.py
@@ -55,8 +55,8 @@
     weight_still = jnp.where(still, phonon_weight[0], phonon_weight[1])
     weight_moved = jnp.where(still, phonon_weight[1], phonon_weight[0])
     summed = jnp.matmul(
-        weight_still, flat + flat, precision=lax.Precision.HIGHEST
-    ) + jnp.matmul(weight_moved, near, precision=lax.Precision.HIGHEST)
+        weight_still, flat + flat, precision=lax.Precision.HIGH
+    ) + jnp.matmul(weight_moved, near, precision=lax.Precision.HIGH)
     out = summed.astype(jnp.bfloat16).reshape(moms, rows, width)
     back = lax.all_to_all(out, "kmom", 0, 0).reshape(width, width)
     mirrored = back.T

time: 165 us -> 165 us (level)
  no operation moved by 1% of the time
where the time goes in v11:
time: 165 us; the launch traced here: 164 us
  waiting for transfers between devices  94.5 us (57%)
  starting transfers between devices  47.3 us (29%)
  matrix products  11.4 us (7%)
  other arithmetic  4.69 us (3%)
  local copies, waits for them, and re-layouts  4.66 us (3%)
    ppermute x7, waiting for transfers between devices, passed_along(): return lax.ppermute(shard, axis, pairs)  74.6 us
    ppermute x7, starting transfers between devices, passed_along(): return lax.ppermute(shard, axis, pairs)  13.7 us
    ppermute x1, starting transfers between devices, self_energy_of(): beside = lax.ppermute(held, 'energy', within)  10.3 us
    ppermute x1, starting transfers between devices, self_energy_of(): facing = lax.ppermute(held, 'energy', across)  10.3 us
    all_to_all x1, starting transfers between devices, self_energy_of(): held = lax.all_to_all(packed.reshape(moms, rows, width), 'kmom', 0, 0)  9.51 us
    all_to_all x1, waiting for transfers between devices, self_energy_of(): held = lax.all_to_all(packed.reshape(moms, rows, width), 'kmom', 0, 0)  7.08 us
    all_to_all x1, waiting for transfers between devices, self_energy_of(): back = lax.all_to_all(out, 'kmom', 0, 0).reshape(width, width)  6.88 us
    ppermute x1, waiting for transfers between devices, self_energy_of(): facing = lax.ppermute(held, 'energy', across)  5.94 us
  transfers between devices with their start and end apart: 11, of which 10 were waited for; matrix products, arithmetic and copies ran while one was open for 3% of the time, Pallas kernels for 0%

profile of v11, /device:TPU:25, one launch (start us, length us, event | category | flops | bytes accessed | tf_op | source)
XLA Modules:
  0.0 164.5 jit_solution(11883988352492875642)
XLA Ops:
  0.6 2.2 %collective-permute-start.1 = (f32[1,1,2,256,256]{4,3,2,1,0:T(8,128)}, f32[1,1,2,256,256]{4,3,2,1,0:T(8,128)S(1)}, u32[]{:S(2)}, u32[]{:S(2)}) collective-permute-start(f32[1,1,2,256,256]{4,3,2,1,0:T(8,128)} %bitcast.122), channel_id=1, source_target_pairs={{96,0},{192,96},{288,192},{384,288},{480,384},{576,480},{672,576},... | collective-permute-start | bytes 1572872 | tf_op jit(solution)/shard_map/ppermute | solution.py:10
  6.4 1.6 copy.25
  8.6 8.3 %collective-permute-done.1 = f32[1,1,2,256,256]{4,3,2,1,0:T(8,128)S(1)} collective-permute-done((f32[1,1,2,256,256]{4,3,2,1,0:T(8,128)}, f32[1,1,2,256,256]{4,3,2,1,0:T(8,128)S(1)}, u32[]{:S(2)}, u32[]{:S(2)}) %collective-permute-start.1) | collective-permute-done | bytes 524320 | tf_op jit(solution)/shard_map/ppermute | solution.py:10
  16.9 85.9 %while.10 = (s32[]{:T(128)}, f32[1,1,2,256,256]{4,3,2,1,0:T(8,128)S(1)}, f32[1,1,1,2,256,256]{5,4,3,2,1,0:T(8,128)S(1)}, f32[512,512]{1,0:T(8,128)S(1)}, f32[256,512]{1,0:T(8,128)S(1)}, /*index=5*/s32[]{:T(128)}) while((s32[]{:T(128)}, f32[1,1,2,256,256]{4,3,2,1,0:T(8,128)S(1)}, f32[1,1,1,2,256,256]{5,4,3,2,1,0:T(8,128)S(1)}, ...), condition=%wide.region_2.3_spmd, body=%wide.region_1.2_spmd.sunk | while | flops 805699584 | bytes 9437293 | solution.py:107
  18.3 1.9 %collective-permute-start = (f32[1,1,2,256,256]{4,3,2,1,0:T(8,128)S(1)}, f32[1,1,2,256,256]{4,3,2,1,0:T(8,128)S(1)}, u32[]{:S(2)}, u32[]{:S(2)}) collective-permute-start(f32[1,1,2,256,256]{4,3,2,1,0:T(8,128)S(1)} %maximum_add_fusion.4), channel_id=1, source_target_pairs={{96,0},{192,96},{288,192},{384,288},{480,384},{576,480},{672,576},... | collective-permute-start | bytes 1572872 | tf_op jit(solution)/shard_map/while/body/eval_jaxpr/ppermute | solution.py:10
  20.2 13.1 %collective-permute-done = f32[1,1,2,256,256]{4,3,2,1,0:T(8,128)S(1)} collective-permute-done((f32[1,1,2,256,256]{4,3,2,1,0:T(8,128)S(1)}, f32[1,1,2,256,256]{4,3,2,1,0:T(8,128)S(1)}, u32[]{:S(2)}, u32[]{:S(2)}) %collective-permute-start) | collective-permute-done | bytes 524320 | tf_op jit(solution)/shard_map/while/body/eval_jaxpr/ppermute | solution.py:10
  34.7 1.9 %collective-permute-start = (f32[1,1,2,256,256]{4,3,2,1,0:T(8,128)S(1)}, f32[1,1,2,256,256]{4,3,2,1,0:T(8,128)S(1)}, u32[]{:S(2)}, u32[]{:S(2)}) collective-permute-start(f32[1,1,2,256,256]{4,3,2,1,0:T(8,128)S(1)} %maximum_add_fusion.4), channel_id=1, source_target_pairs={{96,0},{192,96},{288,192},{384,288},{480,384},{576,480},{672,576},... | collective-permute-start | bytes 1572872 | tf_op jit(solution)/shard_map/while/body/eval_jaxpr/ppermute | solution.py:10
  36.6 12.3 %collective-permute-done = f32[1,1,2,256,256]{4,3,2,1,0:T(8,128)S(1)} collective-permute-done((f32[1,1,2,256,256]{4,3,2,1,0:T(8,128)S(1)}, f32[1,1,2,256,256]{4,3,2,1,0:T(8,128)S(1)}, u32[]{:S(2)}, u32[]{:S(2)}) %collective-permute-start) | collective-permute-done | bytes 524320 | tf_op jit(solution)/shard_map/while/body/eval_jaxpr/ppermute | solution.py:10
  50.2 1.9 %collective-permute-start = (f32[1,1,2,256,256]{4,3,2,1,0:T(8,128)S(1)}, f32[1,1,2,256,256]{4,3,2,1,0:T(8,128)S(1)}, u32[]{:S(2)}, u32[]{:S(2)}) collective-permute-start(f32[1,1,2,256,256]{4,3,2,1,0:T(8,128)S(1)} %maximum_add_fusion.4), channel_id=1, source_target_pairs={{96,0},{192,96},{288,192},{384,288},{480,384},{576,480},{672,576},... | collective-permute-start | bytes 1572872 | tf_op jit(solution)/shard_map/while/body/eval_jaxpr/ppermute | solution.py:10
  52.1 11.4 %collective-permute-done = f32[1,1,2,256,256]{4,3,2,1,0:T(8,128)S(1)} collective-permute-done((f32[1,1,2,256,256]{4,3,2,1,0:T(8,128)S(1)}, f32[1,1,2,256,256]{4,3,2,1,0:T(8,128)S(1)}, u32[]{:S(2)}, u32[]{:S(2)}) %collective-permute-start) | collective-permute-done | bytes 524320 | tf_op jit(solution)/shard_map/while/body/eval_jaxpr/ppermute | solution.py:10
  64.9 1.9 %collective-permute-start = (f32[1,1,2,256,256]{4,3,2,1,0:T(8,128)S(1)}, f32[1,1,2,256,256]{4,3,2,1,0:T(8,128)S(1)}, u32[]{:S(2)}, u32[]{:S(2)}) collective-permute-start(f32[1,1,2,256,256]{4,3,2,1,0:T(8,128)S(1)} %maximum_add_fusion.4), channel_id=1, source_target_pairs={{96,0},{192,96},{288,192},{384,288},{480,384},{576,480},{672,576},... | collective-permute-start | bytes 1572872 | tf_op jit(solution)/shard_map/while/body/eval_jaxpr/ppermute | solution.py:10
  66.8 10.6 %collective-permute-done = f32[1,1,2,256,256]{4,3,2,1,0:T(8,128)S(1)} collective-permute-done((f32[1,1,2,256,256]{4,3,2,1,0:T(8,128)S(1)}, f32[1,1,2,256,256]{4,3,2,1,0:T(8,128)S(1)}, u32[]{:S(2)}, u32[]{:S(2)}) %collective-permute-start) | collective-permute-done | bytes 524320 | tf_op jit(solution)/shard_map/while/body/eval_jaxpr/ppermute | solution.py:10
  78.7 1.9 %collective-permute-start = (f32[1,1,2,256,256]{4,3,2,1,0:T(8,128)S(1)}, f32[1,1,2,256,256]{4,3,2,1,0:T(8,128)S(1)}, u32[]{:S(2)}, u32[]{:S(2)}) collective-permute-start(f32[1,1,2,256,256]{4,3,2,1,0:T(8,128)S(1)} %maximum_add_fusion.4), channel_id=1, source_target_pairs={{96,0},{192,96},{288,192},{384,288},{480,384},{576,480},{672,576},... | collective-permute-start | bytes 1572872 | tf_op jit(solution)/shard_map/while/body/eval_jaxpr/ppermute | solution.py:10
  80.7 9.7 %collective-permute-done = f32[1,1,2,256,256]{4,3,2,1,0:T(8,128)S(1)} collective-permute-done((f32[1,1,2,256,256]{4,3,2,1,0:T(8,128)S(1)}, f32[1,1,2,256,256]{4,3,2,1,0:T(8,128)S(1)}, u32[]{:S(2)}, u32[]{:S(2)}) %collective-permute-start) | collective-permute-done | bytes 524320 | tf_op jit(solution)/shard_map/while/body/eval_jaxpr/ppermute | solution.py:10
  91.7 1.9 %collective-permute-start = (f32[1,1,2,256,256]{4,3,2,1,0:T(8,128)S(1)}, f32[1,1,2,256,256]{4,3,2,1,0:T(8,128)S(1)}, u32[]{:S(2)}, u32[]{:S(2)}) collective-permute-start(f32[1,1,2,256,256]{4,3,2,1,0:T(8,128)S(1)} %maximum_add_fusion.4), channel_id=1, source_target_pairs={{96,0},{192,96},{288,192},{384,288},{480,384},{576,480},{672,576},... | collective-permute-start | bytes 1572872 | tf_op jit(solution)/shard_map/while/body/eval_jaxpr/ppermute | solution.py:10
  93.7 9.2 %collective-permute-done = f32[1,1,2,256,256]{4,3,2,1,0:T(8,128)S(1)} collective-permute-done((f32[1,1,2,256,256]{4,3,2,1,0:T(8,128)S(1)}, f32[1,1,2,256,256]{4,3,2,1,0:T(8,128)S(1)}, u32[]{:S(2)}, u32[]{:S(2)}) %collective-permute-start) | collective-permute-done | bytes 524320 | tf_op jit(solution)/shard_map/while/body/eval_jaxpr/ppermute | solution.py:10
  102.9 2.2 %fusion.32 = f32[512,256]{1,0:T(8,128)S(1)} fusion(f32[512,512]{0,1:T(8,128)} %maximum_maximum_fusion, f32[512,256]{1,0:T(8,128)S(1)} %bitcast.124), kind=kOutput, calls=%fused_computation.63 | convolution fusion | flops 402653184 | bytes 2097152 | tf_op jit(solution)/shard_map/dot_general | solution.py:97
  106.9 9.5 %all-to-all-start = ((bf16[16,16,256]{2,1,0:T(8,128)(2,1)}), bf16[16,16,256]{2,1,0:T(8,128)(2,1)S(1)}, u32[]{:S(2)}, u32[]{:S(2)}) async-start(bf16[16,16,256]{2,1,0:T(8,128)(2,1)} %bitcast.26), calls=%async_computation | async-start | bytes 262144 | tf_op jit(solution)/shard_map/all_to_all | solution.py:45
  117.1 7.1 %all-to-all-done = bf16[16,16,256]{2,1,0:T(8,128)(2,1)S(1)} async-done(((bf16[16,16,256]{2,1,0:T(8,128)(2,1)}), bf16[16,16,256]{2,1,0:T(8,128)(2,1)S(1)}, u32[]{:S(2)}, u32[]{:S(2)}) %all-to-all-start) | async-done | bytes 131104 | tf_op jit(solution)/shard_map/all_to_all | solution.py:45
  124.4 10.3 %collective-permute-start.2 = (bf16[16,16,256]{2,1,0:T(8,128)(2,1)S(1)}, bf16[16,16,256]{2,1,0:T(8,128)(2,1)S(1)}, u32[]{:S(2)}, u32[]{:S(2)}) collective-permute-start(bf16[16,16,256]{2,1,0:T(8,128)(2,1)S(1)} %all-to-all-done), channel_id=1, source_target_pairs={{0,1},{1,0},{2,3},{3,2},{4,5},{5,4},{6,7},{7,6},{8,9},{9,8},{10,11... | collective-permute-start | bytes 393224 | tf_op jit(solution)/shard_map/ppermute | solution.py:50
  134.7 10.3 %collective-permute-start.3 = (bf16[16,16,256]{2,1,0:T(8,128)(2,1)S(1)}, bf16[16,16,256]{2,1,0:T(8,128)(2,1)S(1)}, u32[]{:S(2)}, u32[]{:S(2)}) collective-permute-start(bf16[16,16,256]{2,1,0:T(8,128)(2,1)S(1)} %all-to-all-done), channel_id=1, source_target_pairs={{1,2},{2,1},{3,4},{4,3},{7,8},{8,7},{9,10},{10,9},{13,14},{14,13},... | collective-permute-start | bytes 393224 | tf_op jit(solution)/shard_map/ppermute | solution.py:51
  145.2 5.9 %collective-permute-done.3 = bf16[16,16,256]{2,1,0:T(8,128)(2,1)S(1)} collective-permute-done((bf16[16,16,256]{2,1,0:T(8,128)(2,1)S(1)}, bf16[16,16,256]{2,1,0:T(8,128)(2,1)S(1)}, u32[]{:S(2)}, u32[]{:S(2)}) %collective-permute-start.3) | collective-permute-done | bytes 131104 | tf_op jit(solution)/shard_map/ppermute | solution.py:51
  152.3 3.5 %all-to-all-start.1 = ((bf16[16,16,256]{2,1,0:T(8,128)(2,1)}), bf16[16,16,256]{2,1,0:T(8,128)(2,1)S(1)}, u32[]{:S(2)}, u32[]{:S(2)}) async-start(bf16[16,16,256]{2,1,0:T(8,128)(2,1)} %bitcast.44), calls=%async_computation.1 | async-start | bytes 262144 | tf_op jit(solution)/shard_map/all_to_all | solution.py:61
  156.7 6.9 %all-to-all-done.1 = bf16[16,16,256]{2,1,0:T(8,128)(2,1)S(1)} async-done(((bf16[16,16,256]{2,1,0:T(8,128)(2,1)}), bf16[16,16,256]{2,1,0:T(8,128)(2,1)S(1)}, u32[]{:S(2)}, u32[]{:S(2)}) %all-to-all-start.1) | async-done | bytes 131104 | tf_op jit(solution)/shard_map/all_to_all | solution.py:61
  (64 shorter events, 17.0 us)
Async XLA Ops:
  0.6 2.3 %copy-start.3 = (s32[1,8,3]{1,0,2:T(1,128)S(1)}, s32[1,8,3]{1,0,2:T(1,128)}, u32[]{:S(2)}) copy-start(s32[1,8,3]{1,0,2:T(1,128)} %param.10) | copy-start | bytes 292
  0.6 2.4 %copy-start.1 = (f32[1,256,256]{2,1,0:T(8,128)S(1)}, f32[1,256,256]{2,1,0:T(8,128)}, u32[]{:S(2)}) copy-start(f32[1,256,256]{2,1,0:T(8,128)} %param.9) | copy-start | bytes 786436
  0.6 16.3 %collective-permute-start.1 = (f32[1,1,2,256,256]{4,3,2,1,0:T(8,128)}, f32[1,1,2,256,256]{4,3,2,1,0:T(8,128)S(1)}, u32[]{:S(2)}, u32[]{:S(2)}) collective-permute-start(f32[1,1,2,256,256]{4,3,2,1,0:T(8,128)} %bitcast.122), channel_id=1, source_target_pairs={{96,0},{192,96},{288,192},{384,288},{480,384},{576,480},{672,576},... | collective-permute-start | bytes 1572872 | tf_op jit(solution)/shard_map/ppermute | solution.py:10
  3.0 1.0 copy-start
  18.3 15.1 %collective-permute-start = (f32[1,1,2,256,256]{4,3,2,1,0:T(8,128)S(1)}, f32[1,1,2,256,256]{4,3,2,1,0:T(8,128)S(1)}, u32[]{:S(2)}, u32[]{:S(2)}) collective-permute-start(f32[1,1,2,256,256]{4,3,2,1,0:T(8,128)S(1)} %maximum_add_fusion.4), channel_id=1, source_target_pairs={{96,0},{192,96},{288,192},{384,288},{480,384},{576,480},{672,576},... | collective-permute-start | bytes 1572872 | tf_op jit(solution)/shard_map/while/body/eval_jaxpr/ppermute | solution.py:10
  34.7 14.2 %collective-permute-start = (f32[1,1,2,256,256]{4,3,2,1,0:T(8,128)S(1)}, f32[1,1,2,256,256]{4,3,2,1,0:T(8,128)S(1)}, u32[]{:S(2)}, u32[]{:S(2)}) collective-permute-start(f32[1,1,2,256,256]{4,3,2,1,0:T(8,128)S(1)} %maximum_add_fusion.4), channel_id=1, source_target_pairs={{96,0},{192,96},{288,192},{384,288},{480,384},{576,480},{672,576},... | collective-permute-start | bytes 1572872 | tf_op jit(solution)/shard_map/while/body/eval_jaxpr/ppermute | solution.py:10
  50.2 13.3 %collective-permute-start = (f32[1,1,2,256,256]{4,3,2,1,0:T(8,128)S(1)}, f32[1,1,2,256,256]{4,3,2,1,0:T(8,128)S(1)}, u32[]{:S(2)}, u32[]{:S(2)}) collective-permute-start(f32[1,1,2,256,256]{4,3,2,1,0:T(8,128)S(1)} %maximum_add_fusion.4), channel_id=1, source_target_pairs={{96,0},{192,96},{288,192},{384,288},{480,384},{576,480},{672,576},... | collective-permute-start | bytes 1572872 | tf_op jit(solution)/shard_map/while/body/eval_jaxpr/ppermute | solution.py:10
  64.9 12.5 %collective-permute-start = (f32[1,1,2,256,256]{4,3,2,1,0:T(8,128)S(1)}, f32[1,1,2,256,256]{4,3,2,1,0:T(8,128)S(1)}, u32[]{:S(2)}, u32[]{:S(2)}) collective-permute-start(f32[1,1,2,256,256]{4,3,2,1,0:T(8,128)S(1)} %maximum_add_fusion.4), channel_id=1, source_target_pairs={{96,0},{192,96},{288,192},{384,288},{480,384},{576,480},{672,576},... | collective-permute-start | bytes 1572872 | tf_op jit(solution)/shard_map/while/body/eval_jaxpr/ppermute | solution.py:10
  78.7 11.6 %collective-permute-start = (f32[1,1,2,256,256]{4,3,2,1,0:T(8,128)S(1)}, f32[1,1,2,256,256]{4,3,2,1,0:T(8,128)S(1)}, u32[]{:S(2)}, u32[]{:S(2)}) collective-permute-start(f32[1,1,2,256,256]{4,3,2,1,0:T(8,128)S(1)} %maximum_add_fusion.4), channel_id=1, source_target_pairs={{96,0},{192,96},{288,192},{384,288},{480,384},{576,480},{672,576},... | collective-permute-start | bytes 1572872 | tf_op jit(solution)/shard_map/while/body/eval_jaxpr/ppermute | solution.py:10
  91.7 11.1 %collective-permute-start = (f32[1,1,2,256,256]{4,3,2,1,0:T(8,128)S(1)}, f32[1,1,2,256,256]{4,3,2,1,0:T(8,128)S(1)}, u32[]{:S(2)}, u32[]{:S(2)}) collective-permute-start(f32[1,1,2,256,256]{4,3,2,1,0:T(8,128)S(1)} %maximum_add_fusion.4), channel_id=1, source_target_pairs={{96,0},{192,96},{288,192},{384,288},{480,384},{576,480},{672,576},... | collective-permute-start | bytes 1572872 | tf_op jit(solution)/shard_map/while/body/eval_jaxpr/ppermute | solution.py:10
  106.9 17.3 %all-to-all-start = ((bf16[16,16,256]{2,1,0:T(8,128)(2,1)}), bf16[16,16,256]{2,1,0:T(8,128)(2,1)S(1)}, u32[]{:S(2)}, u32[]{:S(2)}) async-start(bf16[16,16,256]{2,1,0:T(8,128)(2,1)} %bitcast.26), calls=%async_computation | async-start | bytes 262144 | tf_op jit(solution)/shard_map/all_to_all | solution.py:45
  116.4 0.7 copy-start.4
  124.2 20.8 %copy-start.2 = (f32[2,16,16]{2,1,0:T(8,128)S(1)}, f32[2,16,16]{2,1,0:T(8,128)}, u32[]{:S(2)}) copy-start(f32[2,16,16]{2,1,0:T(8,128)} %param.12) | copy-start | bytes 6148
  124.4 20.8 %collective-permute-start.2 = (bf16[16,16,256]{2,1,0:T(8,128)(2,1)S(1)}, bf16[16,16,256]{2,1,0:T(8,128)(2,1)S(1)}, u32[]{:S(2)}, u32[]{:S(2)}) collective-permute-start(bf16[16,16,256]{2,1,0:T(8,128)(2,1)S(1)} %all-to-all-done), channel_id=1, source_target_pairs={{0,1},{1,0},{2,3},{3,2},{4,5},{5,4},{6,7},{7,6},{8,9},{9,8},{10,11... | collective-permute-start | bytes 393224 | tf_op jit(solution)/shard_map/ppermute | solution.py:50
  134.7 16.5 %collective-permute-start.3 = (bf16[16,16,256]{2,1,0:T(8,128)(2,1)S(1)}, bf16[16,16,256]{2,1,0:T(8,128)(2,1)S(1)}, u32[]{:S(2)}, u32[]{:S(2)}) collective-permute-start(bf16[16,16,256]{2,1,0:T(8,128)(2,1)S(1)} %all-to-all-done), channel_id=1, source_target_pairs={{1,2},{2,1},{3,4},{4,3},{7,8},{8,7},{9,10},{10,9},{13,14},{14,13},... | collective-permute-start | bytes 393224 | tf_op jit(solution)/shard_map/ppermute | solution.py:51
  152.3 11.3 %all-to-all-start.1 = ((bf16[16,16,256]{2,1,0:T(8,128)(2,1)}), bf16[16,16,256]{2,1,0:T(8,128)(2,1)S(1)}, u32[]{:S(2)}, u32[]{:S(2)}) async-start(bf16[16,16,256]{2,1,0:T(8,128)(2,1)} %bitcast.44), calls=%async_computation.1 | async-start | bytes 262144 | tf_op jit(solution)/shard_map/all_to_all | solution.py:61
